TPU v7x, 512 devices: a whole 4x8x8 slice. The times are simulated.
512 devices in a mesh: dp: 16 (over x, z_lo, core), seq: 32 (over z_hi, y).
Axes of the slice: x: 4, y: 8, z: 8 (z_hi: 4, z_lo: 2; z = z_hi * 2 + z_lo), core: 2. Of those that a mesh axis runs over, the one named last changes fastest.
Arguments:
- ssm_input: bfloat16 [16, 8192, 1024], P('dp', 'seq'), may hold values from -6 to 6
- gate_input: bfloat16 [16, 8192, 1024], P('dp', 'seq'), may hold values from -6 to 6
- state_proj: bfloat16 [16, 8192, 512], P('dp', 'seq'), may hold values from -6 to 6
- step_raw: float32 [16, 32, 8192], P('dp', None, 'seq'), may hold values from -5 to 400
- decay_log: float32 [2, 16], replicated, may hold values from -10 to 0
- skip_gain: float32 [16], replicated, may hold values from 0.5 to 2
- norm_gain: float32 [1024], replicated, may hold values from 0.25 to 1.75
- out_weight: bfloat16 [1024, 1024], P('dp'), may hold values from -0.1875 to 0.1875
- latents: bfloat16 [256, 1024], replicated, may hold values from -450 to 450
- lengths: int32 [16], P('dp'), may hold values from 4096 to 8192, as said below
Outputs:
- encoded: bfloat16 [16, 8192, 1024], P('dp', 'seq')
- pooled: bfloat16 [16, 256, 1024], P('dp')
Inputs may be any that keep to these rules, and one draw needn't show every extreme that they name: `lengths`: positions at or after a sequence's length are padding; at least one sequence has none, and one has 4096 real tokens.
All inputs are finite; a program needn't handle non-finite values.
Results may differ from a plain program's by a relative error of at most 0.034.
Values may be sent and summed in bfloat16 or wider, within the bound.
No kernel may reach another device: no remote copies, remote signals or barrier semaphores. Data moves between devices by JAX's collectives and lax.ppermute only.
A program may use at most 128 MiB of HBM per device.

v0:
```python
import math

import jax
import jax.numpy as jnp
from jax import lax
from jax.sharding import PartitionSpec as P

BLOCK = 128


def carried_in(part, axis, combine, identity, reverse):
    count = lax.axis_size(axis)
    place = lax.axis_index(axis)
    ahead = count - 1 - place if reverse else place
    gathered = jax.tree.map(lambda a: lax.all_gather(a, axis), part)
    state = jax.tree.map(lambda a, e: jnp.zeros_like(a) + jnp.asarray(e, a.dtype), part, identity)

    def one(hop, state):
        source = count - 1 - hop if reverse else hop
        return combine(
            state, jax.tree.map(lambda a: lax.dynamic_index_in_dim(a, source, 0, False), gathered)
        )

    return lax.fori_loop(0, ahead, one, state)


def block_terms(x_block, dt_block, b_block, c_block, forget_rate):
    cumulative = jnp.cumsum(-dt_block * forget_rate[:, None], axis=1)
    gram_matrix = jnp.einsum("qn,kn->qk", c_block, b_block, preferred_element_type=jnp.float32)
    symbol_offset = jnp.arange(x_block.shape[0], dtype=jnp.int32)
    causal = symbol_offset[:, None] >= symbol_offset[None, :]
    spread = jnp.where(causal[None], cumulative[:, :, None] - cumulative[:, None, :], -jnp.inf)
    mixing = (gram_matrix[None] * jnp.exp(spread) * dt_block[:, None, :]).astype(jnp.bfloat16)
    intra_out = jnp.einsum("hqk,khp->qhp", mixing, x_block, preferred_element_type=jnp.float32)
    tail_weight = jnp.exp(cumulative[:, -1:] - cumulative) * dt_block
    scaled_x = (x_block * tail_weight.T[:, :, None]).astype(jnp.bfloat16)
    contrib = jnp.einsum("khp,kn->hpn", scaled_x, b_block, preferred_element_type=jnp.float32)
    return (intra_out, cumulative, contrib)


def block_pass(x_seq, dt_seq, b_seq, c_seq, forget_rate):
    head_count, head_size = (x_seq.shape[1], x_seq.shape[2])
    state_size = b_seq.shape[1]
    block_count = x_seq.shape[0] // BLOCK
    x_blocks = x_seq.reshape(block_count, BLOCK, head_count, head_size)
    dt_blocks = dt_seq.reshape(head_count, block_count, BLOCK).transpose(1, 0, 2)
    b_blocks = b_seq.reshape(block_count, BLOCK, state_size)
    c_blocks = c_seq.reshape(block_count, BLOCK, state_size)

    def block_step(carried, inputs):
        decay_sum, running = carried
        x_block, dt_block, b_block, c_block = inputs
        intra_out, cumulative, contrib = block_terms(
            x_block, dt_block, b_block, c_block, forget_rate
        )
        record = (intra_out, cumulative, decay_sum, running)
        running = jnp.exp(cumulative[:, -1])[:, None, None] * running + contrib
        return ((decay_sum + cumulative[:, -1], running), record)

    initial = (
        jnp.zeros((head_count,), jnp.float32),
        jnp.zeros((head_count, head_size, state_size), jnp.float32),
    )
    totals, records = lax.scan(block_step, initial, (x_blocks, dt_blocks, b_blocks, c_blocks))
    return (totals, records)


def apply_state(records, c_seq, incoming):
    intra_outs, cumulatives, decay_sums, runnings = records
    block_count = intra_outs.shape[0]
    c_blocks = c_seq.reshape(block_count, BLOCK, c_seq.shape[1])

    def block_output(inputs):
        intra_out, cumulative, decay_sum, running, c_block = inputs
        held_state = (jnp.exp(decay_sum)[:, None, None] * incoming + running).astype(jnp.bfloat16)
        state_out = jnp.einsum(
            "qn,hpn->qhp", c_block, held_state, preferred_element_type=jnp.float32
        )
        return intra_out + state_out * jnp.exp(cumulative).T[:, :, None]

    outputs = lax.map(block_output, (intra_outs, cumulatives, decay_sums, runnings, c_blocks))
    return outputs.reshape(block_count * BLOCK, outputs.shape[2] * outputs.shape[3])


def chain_combine(earlier, later_pair):
    return (
        earlier[0] + later_pair[0],
        jnp.exp(later_pair[0])[:, None, None] * earlier[1] + later_pair[1],
    )


def body(
    ssm_input,
    gate_input,
    state_proj,
    step_raw,
    decay_log,
    skip_gain,
    norm_gain,
    out_weight,
    latents,
    lengths,
):
    row_count = ssm_input.shape[1]
    inner_width = ssm_input.shape[2]
    head_count = decay_log.shape[1]
    head_size = inner_width // head_count
    state_size = state_proj.shape[2] // 4
    model_width = out_weight.shape[1]
    positions = lax.axis_index("seq") * row_count + jnp.arange(row_count, dtype=jnp.int32)
    is_valid = positions < lengths[0]
    quantized_stride_width = jnp.where(is_valid[None, :], jax.nn.softplus(step_raw[0]), 0.0)
    decay_rates = jnp.exp(decay_log)
    flat_tokens = ssm_input[0]
    tokens = flat_tokens.reshape(row_count, head_count, head_size)
    projections = state_proj[0]
    forward_c = projections[:, state_size : 2 * state_size]
    backward_c = projections[::-1, 3 * state_size :]
    forward_totals, forward_records = block_pass(
        tokens,
        quantized_stride_width[:head_count],
        projections[:, :state_size],
        forward_c,
        decay_rates[0],
    )
    backward_totals, backward_records = block_pass(
        tokens[::-1],
        quantized_stride_width[head_count:, ::-1],
        projections[::-1, 2 * state_size : 3 * state_size],
        backward_c,
        decay_rates[1],
    )
    identity = (
        jnp.zeros((head_count,), jnp.float32),
        jnp.zeros((head_count, head_size, state_size), jnp.float32),
    )
    unused_item, forward_in = carried_in(
        (forward_totals[0], forward_totals[1]), "seq", chain_combine, identity, False
    )
    unused_item, backward_in = carried_in(
        (backward_totals[0], backward_totals[1]), "seq", chain_combine, identity, True
    )
    forward_out = apply_state(forward_records, forward_c, forward_in)
    backward_out = apply_state(backward_records, backward_c, backward_in)[::-1]
    skip_wide = jnp.repeat(skip_gain, head_size)
    mixed_out = forward_out + backward_out + skip_wide[None, :] * flat_tokens.astype(jnp.float32)
    gated_out = mixed_out * jax.nn.silu(gate_input[0].astype(jnp.float32))
    squared = (gated_out * gated_out).reshape(row_count, head_count, head_size)
    mean_square = jnp.mean(squared, axis=2)
    inverse_scale = jnp.repeat(lax.rsqrt(mean_square + 1e-05), head_size, axis=1)
    normed = (gated_out * inverse_scale * norm_gain[None, :]).astype(jnp.bfloat16)
    projected = jnp.dot(
        normed,
        lax.all_gather(out_weight, "dp", axis=0, tiled=True),
        preferred_element_type=jnp.float32,
    )
    encoded = projected.astype(jnp.bfloat16)
    score_scale = 1.0 / math.sqrt(model_width)
    scores = (
        jnp.einsum("rd,sd->rs", latents, encoded, preferred_element_type=jnp.float32) * score_scale
    )
    local_top = jnp.max(jnp.where(is_valid[None, :], scores, -1e30), axis=1)
    top_score = lax.pmax(local_top, "seq")
    prob_values = jnp.where(is_valid[None, :], jnp.exp(scores - top_score[:, None]), 0.0)
    weight_sum = jnp.sum(prob_values, axis=1)
    weighted_sum = jnp.dot(
        prob_values.astype(jnp.bfloat16), encoded, preferred_element_type=jnp.float32
    )
    total_weight, total_sum = (
        lax.psum(weight_sum.astype(jnp.bfloat16), "seq").astype(jnp.float32),
        lax.psum(weighted_sum.astype(jnp.bfloat16), "seq").astype(jnp.float32),
    )
    pooled = (total_sum / total_weight[:, None]).astype(jnp.bfloat16)
    return (encoded[None], pooled[None])


def solution(mesh):
    in_specs = (
        P("dp", "seq", None),
        P("dp", "seq", None),
        P("dp", "seq", None),
        P("dp", None, "seq"),
        P(),
        P(),
        P(),
        P("dp", None),
        P(),
        P("dp"),
    )
    out_specs = (P("dp", "seq", None), P("dp", None, None))
    return jax.shard_map(body, mesh=mesh, in_specs=in_specs, out_specs=out_specs, check_vma=False)
```

profile of v0, /device:TPU:6, one launch (start us, length us, event | category | flops | bytes accessed | tf_op | source)
XLA Modules:
  0.0 933.2 jit_solution(3605383286793981775)
XLA Ops:
  13.9 5.1 while.93
  19.9 1.8 reshape.184
  21.7 1.6 copy.24
  24.6 8.9 while.92
  25.1 1.5 fusion.143
  29.5 1.5 fusion.143
  37.4 90.0 %all-reduce.2 = (f32[512]{0:T(512)S(1)}, f32[512]{0:T(512)S(1)}) all-reduce(f32[512]{0:T(512)S(1)} %dynamic-update-slice.1, f32[512]{0:T(512)S(1)} %dynamic-update-slice), channel_id=4, replica_groups=mesh['dp'=16,'seq'=32] {'seq'}, use_global_device_ids=true, to_apply=%add.1 | all-reduce | flops 1024 | bytes 8192
  127.6 2.0 copy.31
  129.8 113.0 %all-gather.12.cloned.1.call-done = f32[512,64,128]{2,1,0:T(8,128)} async-done(((f32[16,64,128]{2,1,0:T(8,128)}), f32[512,64,128]{2,1,0:T(8,128)}) %all-gather.12.cloned.1.call-update) | async-done | bytes 16777232 | tf_op jit(solution)/shard_map/all_gather | solution.py:15
  242.8 38.6 %while.90 = (s32[]{:T(128)}, f32[16,64,128]{2,1,0:T(8,128)S(1)}, s32[]{:T(128)}, f32[32,16]{1,0:T(8,128)S(1)}, f32[32,16,64,128]{3,2,1,0:T(8,128)}, /*index=5*/s32[]{:T(128)}, s32[]{:T(128)}, s32[]{:T(128)}, s32[]{:T(128)}) while((s32[]{:T(128)}, f32[16,64,128]{2,1,0:T(8,128)S(1)}, s32[]{:T(128)}, f32[32,16]{1,0:T(8,128)S(1)}, ...), condition=%wide.region_11.12_spmd, body=%wide.region_10.11_spmd.sunk | while | flops 262150 | bytes 1573203 | solution.py:24
  281.4 1.4 broadcast.77.clone2
  282.8 28.9 %while.91 = (s32[]{:T(128)}, f32[2,128,16,64]{1,0,3,2:T(2,128)}, f32[2,128,16,64]{1,3,2,0:T(8,128)S(1)}, bf16[2,128,128]{2,1,0:T(8,128)(2,1)S(1)}, f32[2,16]{1,0...) while((s32[]{:T(128)}, f32[2,128,16,64]{1,0,3,2:T(2,128)}, ...), condition=%wide.region_13.14_spmd, body=%wide.region_12.13_spmd.sunk | while | flops 34209792 | bytes 3205361 | solution.py:81
  282.8 1.3 fusion.135
  284.1 13.1 %dynamic_update_slice.59 = f32[2,128,16,64]{1,0,3,2:T(2,128)} dynamic-update-slice(f32[2,128,16,64]{1,0,3,2:T(2,128)} %get-tuple-element.1058, f32[1,128,16,64]{1,0,3,2:T(1,128)S(1)} %bitcast.288, s32[]{:T(128)} %get-tuple-element.1057, s32[]{:T(128)} %constant.138.clone.1..sunk.3, s32[]{:T(128)} %constant.138.clone.1..sunk.3, s32[]{:T(128)} %constant.138.clone.1..sunk.3) | dynamic-update-slice | bytes 1048580 | tf_op jit(solution)/shard_map/while/body/jit(dynamic_update_index_in_dim)/dynamic_update_slice | solution.py:64
  297.2 1.3 fusion.135
  298.5 13.1 %dynamic_update_slice.59 = f32[2,128,16,64]{1,0,3,2:T(2,128)} dynamic-update-slice(f32[2,128,16,64]{1,0,3,2:T(2,128)} %get-tuple-element.1058, f32[1,128,16,64]{1,0,3,2:T(1,128)S(1)} %bitcast.288, s32[]{:T(128)} %get-tuple-element.1057, s32[]{:T(128)} %constant.138.clone.1..sunk.3, s32[]{:T(128)} %constant.138.clone.1..sunk.3, s32[]{:T(128)} %constant.138.clone.1..sunk.3) | dynamic-update-slice | bytes 1048580 | tf_op jit(solution)/shard_map/while/body/jit(dynamic_update_index_in_dim)/dynamic_update_slice | solution.py:64
  311.6 1.4 copy.49
  313.0 1.4 rev.19
  314.4 141.5 %all-gather.10.cloned.1.call-done = f32[512,64,128]{2,1,0:T(8,128)} async-done(((f32[16,64,128]{2,1,0:T(8,128)}), f32[512,64,128]{2,1,0:T(8,128)}) %all-gather.10.cloned.1.call-update) | async-done | bytes 16777232 | tf_op jit(solution)/shard_map/all_gather | solution.py:15
  456.0 1.4 broadcast.77.clone2.1
  457.4 29.1 %while.89 = (s32[]{:T(128)}, f32[2,128,16,64]{1,0,3,2:T(2,128)}, f32[2,128,16,64]{1,3,2,0:T(8,128)}, bf16[2,128,128]{2,1,0:T(8,128)(2,1)S(1)}, f32[2,16]{1,0:T(2...) while((s32[]{:T(128)}, f32[2,128,16,64]{1,0,3,2:T(2,128)}, ...), condition=%wide.region_6.7_spmd, body=%wide.region_5.6_spmd.sunk | while | flops 34209792 | bytes 3205361 | solution.py:81
  457.4 1.5 fusion.131
  458.9 13.1 %dynamic_update_slice.58 = f32[2,128,16,64]{1,0,3,2:T(2,128)} dynamic-update-slice(f32[2,128,16,64]{1,0,3,2:T(2,128)} %get-tuple-element.1112, f32[1,128,16,64]{1,0,3,2:T(1,128)S(1)} %bitcast.289, s32[]{:T(128)} %get-tuple-element.1111, s32[]{:T(128)} %constant.138.clone.1..sunk.1, s32[]{:T(128)} %constant.138.clone.1..sunk.1, s32[]{:T(128)} %constant.138.clone.1..sunk.1) | dynamic-update-slice | bytes 1048580 | tf_op jit(solution)/shard_map/while/body/jit(dynamic_update_index_in_dim)/dynamic_update_slice | solution.py:64
  472.0 1.5 fusion.131
  473.5 13.1 %dynamic_update_slice.58 = f32[2,128,16,64]{1,0,3,2:T(2,128)} dynamic-update-slice(f32[2,128,16,64]{1,0,3,2:T(2,128)} %get-tuple-element.1112, f32[1,128,16,64]{1,0,3,2:T(1,128)S(1)} %bitcast.289, s32[]{:T(128)} %get-tuple-element.1111, s32[]{:T(128)} %constant.138.clone.1..sunk.1, s32[]{:T(128)} %constant.138.clone.1..sunk.1, s32[]{:T(128)} %constant.138.clone.1..sunk.1) | dynamic-update-slice | bytes 1048580 | tf_op jit(solution)/shard_map/while/body/jit(dynamic_update_index_in_dim)/dynamic_update_slice | solution.py:64
  486.5 2.0 bitcast_reduce_fusion
  488.8 9.1 all-gather.8.cloned.1.call-done
  497.9 2.3 convolution_convert_fusion.1
  500.6 115.5 %pmax.7 = f32[256]{0:T(256)S(1)} all-reduce(f32[256]{0:T(256)S(1)} %get-tuple-element.608), channel_id=1, replica_groups=mesh['dp'=16,'seq'=32] {'seq'}, use_global_device_ids=true, to_apply=%region_16.17 | all-reduce | flops 256 | bytes 2048 | tf_op jit(solution)/shard_map/pmax | solution.py:163
  617.4 76.9 %psum.15 = bf16[256]{0:T(256)(128)(2,1)S(1)} all-reduce(bf16[256]{0:T(256)(128)(2,1)S(1)} %fusion.82), channel_id=1, replica_groups=mesh['dp'=16,'seq'=32] {'seq'}, use_global_device_ids=true, to_apply=%region_19.20 | all-reduce | flops 256 | bytes 1024 | tf_op jit(solution)/shard_map/psum | solution.py:170
  694.3 230.3 %all-reduce.5.cloned.1.call-done = bf16[256,1024]{1,0:T(8,128)(2,1)} async-done(((bf16[256,1024]{1,0:T(8,128)(2,1)}), bf16[256,1024]{1,0:T(8,128)(2,1)}) %all-reduce.5.cloned.1.call-update) | async-done | bytes 524304 | tf_op jit(solution)/shard_map/psum | solution.py:171
  924.6 2.1 fusion.81
  (190 shorter events, 61.8 us)
Async XLA Ops:
  7.2 493.0 %copy-start = (bf16[256,1024]{1,0:T(8,128)(2,1)S(1)}, bf16[256,1024]{1,0:T(8,128)(2,1)}, u32[]{:S(2)}) copy-start(bf16[256,1024]{1,0:T(8,128)(2,1)} %param.30) | copy-start | bytes 1572868
  7.2 235.5 %all-gather.12.cloned.1.call-start = ((), (), s32[]{:S(2)}) async-start(), calls=%async_computation.3 | async-start | bytes 17301504 | tf_op jit(solution)/shard_map/all_gather | solution.py:15
  11.4 1.3 copy-start.4
  19.0 0.8 copy-start.1
  19.0 110.6 %copy-start.8 = (f32[16]{0:T(128)S(1)}, f32[16]{0:T(128)}, u32[]{:S(2)}) copy-start(f32[16]{0:T(128)} %param.27) | copy-start | bytes 196
  19.8 436.1 %all-gather.10.cloned.1.call-start = ((), (), s32[]{:S(2)}) async-start(), calls=%async_computation.2 | async-start | bytes 17301504 | tf_op jit(solution)/shard_map/all_gather | solution.py:15
  33.4 0.8 copy-start.2
  33.4 249.3 %copy-start.3 = (f32[2,128,16,64]{1,3,2,0:T(8,128)}, f32[2,128,16,64]{1,3,2,0:T(8,128)S(1)}, u32[]{:S(2)}) copy-start(f32[2,128,16,64]{1,3,2,0:T(8,128)S(1)} %get-tuple-element.1103) | copy-start | bytes 3145732
  34.3 463.6 %all-gather.8.cloned.1.call-start = ((), (), s32[]{:S(2)}) async-start(), calls=%async_computation | async-start | bytes 2228224 | tf_op jit(solution)/shard_map/all_gather | solution.py:154
  35.0 889.6 %all-reduce.5.cloned.1.call-start = ((), (), s32[]{:S(2)}) async-start(), calls=%async_computation.1 | async-start | bytes 1048576 | tf_op jit(solution)/shard_map/psum | solution.py:171
  311.6 174.9 %copy-start.5 = (bf16[1,256,1024]{1,2,0:T(8,128)(2,1)S(1)}, bf16[1,256,1024]{1,2,0:T(8,128)(2,1)}, u32[]{:S(2)}) copy-start(bf16[1,256,1024]{1,2,0:T(8,128)(2,1)} %copy-done.4) | copy-start | bytes 1572868
  311.6 176.9 %copy-start.7 = (f32[1024]{0:T(1024)S(1)}, f32[1024]{0:T(1024)}, u32[]{:S(2)}) copy-start(f32[1024]{0:T(1024)} %param.28) | copy-start | bytes 12292
  500.2 426.5 %copy-start.6 = (bf16[256,1024]{1,0:T(8,128)(2,1)}, bf16[256,1024]{1,0:T(8,128)(2,1)S(1)}, u32[]{:S(2)}) copy-start(bf16[256,1024]{1,0:T(8,128)(2,1)S(1)} %convolution_convert_fusion.1) | copy-start | bytes 1572868
Sparse Core Ops, SparseCore 0:
  19.9 222.7 all-gather.11
  245.9 209.9 all-gather.9
  458.1 39.7 all-gather.7
  617.4 307.1 all-reduce.4
where the time goes:
time: 939 us; the launch traced here: 933 us
  waiting for transfers between devices  495 us (53%)
  blocking collectives  282 us (30%)
  local copies, waits for them, and re-layouts  74.8 us (8%)
  other arithmetic  47.5 us (5%)
  matrix products  16.9 us (2%)
  between operations  15.4 us (2%)
    all_gather x2, waiting for transfers between devices, carried_in(): gathered = jax.tree.map(lambda a: lax.all_gather(a, axis), part)  254 us
    psum x1, waiting for transfers between devices, body(): lax.psum(weighted_sum.astype(jnp.bfloat16), 'seq').astype(jnp.float32)  230 us
    pmax x1, blocking collectives, body(): top_score = lax.pmax(local_top, 'seq')  115 us
    unnamed x1, blocking collectives  90 us
    psum x1, blocking collectives, body(): lax.psum(weight_sum.astype(jnp.bfloat16), 'seq').astype(jnp.float32)  76.9 us
    dynamic_update_slice x12, local copies, waits for them, and re-layouts, block_pass(): lax.scan(block_step, initial, (x_blocks, dt_blocks, b_blocks, c_blocks))  52.4 us
    add x31, other arithmetic, chain_combine(): jnp.exp(later_pair[0])[:, None, None] * earlier[1] + later_pair[1]  37 us
  transfers between devices with their start and end apart: 4, of which 4 were waited for; matrix products, arithmetic and copies ran while one was open for 13% of the time, Pallas kernels for 0%

commit v1 on v0

v1 whole, which is shorter than its diff:
```python
import math

import jax
import jax.numpy as jnp
from jax import lax
from jax.sharding import PartitionSpec as P

BLOCK = 128


def chain_combine(earlier, later):
    return (
        earlier[0] + later[0],
        jnp.exp(later[0])[:, None, None] * earlier[1] + later[1],
    )


def exclusive_scan(part, axis, reverse):
    count = lax.axis_size(axis)
    inclusive = part
    exclusive = jax.tree.map(jnp.zeros_like, part)
    rounds = max(1, (count - 1).bit_length())
    for k in range(rounds):
        shift = 1 << k
        if shift >= count:
            break
        if reverse:
            perm = [(q, q - shift) for q in range(shift, count)]
        else:
            perm = [(q, q + shift) for q in range(count - shift)]
        received = lax.ppermute(inclusive, axis, perm)
        exclusive = chain_combine(received, exclusive)
        if k + 1 < rounds:
            inclusive = chain_combine(received, inclusive)
    return exclusive


def block_pass(x_seq, dt_seq, b_seq, c_seq, forget_rate):
    row_count, head_count, head_size = x_seq.shape
    state_size = b_seq.shape[1]
    block_count = row_count // BLOCK
    x_blocks = x_seq.reshape(block_count, BLOCK, head_count, head_size)
    dt_blocks = dt_seq.reshape(head_count, block_count, BLOCK).transpose(1, 0, 2)
    b_blocks = b_seq.reshape(block_count, BLOCK, state_size)
    c_blocks = c_seq.reshape(block_count, BLOCK, state_size)
    cumulative = jnp.cumsum(-dt_blocks * forget_rate[None, :, None], axis=2)
    gram_matrix = jnp.einsum(
        "cqn,ckn->cqk", c_blocks, b_blocks, preferred_element_type=jnp.float32
    )
    symbol_offset = jnp.arange(BLOCK, dtype=jnp.int32)
    causal = symbol_offset[:, None] >= symbol_offset[None, :]
    spread = jnp.where(
        causal[None, None], cumulative[:, :, :, None] - cumulative[:, :, None, :], -jnp.inf
    )
    mixing = (gram_matrix[:, None] * jnp.exp(spread) * dt_blocks[:, :, None, :]).astype(
        jnp.bfloat16
    )
    intra_out = jnp.einsum(
        "chqk,ckhp->cqhp", mixing, x_blocks, preferred_element_type=jnp.float32
    )
    block_end = cumulative[:, :, -1]
    tail_weight = jnp.exp(block_end[:, :, None] - cumulative) * dt_blocks
    scaled_x = (x_blocks * tail_weight.transpose(0, 2, 1)[:, :, :, None]).astype(jnp.bfloat16)
    contrib = jnp.einsum(
        "ckhp,ckn->chpn", scaled_x, b_blocks, preferred_element_type=jnp.float32
    )
    decay_sum = jnp.zeros((head_count,), jnp.float32)
    running = jnp.zeros((head_count, head_size, state_size), jnp.float32)
    decay_sums = []
    runnings = []
    for c in range(block_count):
        decay_sums.append(decay_sum)
        runnings.append(running)
        running = jnp.exp(block_end[c])[:, None, None] * running + contrib[c]
        decay_sum = decay_sum + block_end[c]
    records = (intra_out, cumulative, jnp.stack(decay_sums), jnp.stack(runnings), c_blocks)
    return ((decay_sum, running), records)


def apply_state(records, incoming):
    intra_out, cumulative, decay_sums, runnings, c_blocks = records
    block_count = intra_out.shape[0]
    held_state = (
        jnp.exp(decay_sums)[:, :, None, None] * incoming[None] + runnings
    ).astype(jnp.bfloat16)
    state_out = jnp.einsum(
        "cqn,chpn->cqhp", c_blocks, held_state, preferred_element_type=jnp.float32
    )
    outputs = intra_out + state_out * jnp.exp(cumulative).transpose(0, 2, 1)[:, :, :, None]
    return outputs.reshape(block_count * BLOCK, outputs.shape[2] * outputs.shape[3])


def pool_combine(lo, hi):
    top = jnp.maximum(lo[0], hi[0])
    lo_scale = jnp.exp(lo[0] - top)
    hi_scale = jnp.exp(hi[0] - top)
    total = lo[1] * lo_scale + hi[1] * hi_scale
    summed = lo[2] * lo_scale[:, None] + hi[2] * hi_scale[:, None]
    return (top, total, summed)


def butterfly_pool(local, axis):
    count = lax.axis_size(axis)
    assert count & (count - 1) == 0
    place = lax.axis_index(axis)
    state = local
    bit = 1
    while bit < count:
        sent = (state[0], state[1], state[2].astype(jnp.bfloat16))
        perm = [(q, q ^ bit) for q in range(count)]
        received = lax.ppermute(sent, axis, perm)
        own = (sent[0], sent[1], sent[2].astype(jnp.float32))
        other = (received[0], received[1], received[2].astype(jnp.float32))
        is_low = (place & bit) == 0
        lo = jax.tree.map(lambda a, b: jnp.where(is_low, a, b), own, other)
        hi = jax.tree.map(lambda a, b: jnp.where(is_low, b, a), own, other)
        state = pool_combine(lo, hi)
        bit *= 2
    return state


def body(
    ssm_input,
    gate_input,
    state_proj,
    step_raw,
    decay_log,
    skip_gain,
    norm_gain,
    out_weight,
    latents,
    lengths,
):
    row_count = ssm_input.shape[1]
    inner_width = ssm_input.shape[2]
    head_count = decay_log.shape[1]
    head_size = inner_width // head_count
    state_size = state_proj.shape[2] // 4
    model_width = out_weight.shape[1]
    positions = lax.axis_index("seq") * row_count + jnp.arange(row_count, dtype=jnp.int32)
    is_valid = positions < lengths[0]
    step_size = jnp.where(is_valid[None, :], jax.nn.softplus(step_raw[0]), 0.0)
    decay_rates = jnp.exp(decay_log)
    flat_tokens = ssm_input[0]
    tokens = flat_tokens.reshape(row_count, head_count, head_size)
    projections = state_proj[0]
    forward_totals, forward_records = block_pass(
        tokens,
        step_size[:head_count],
        projections[:, :state_size],
        projections[:, state_size : 2 * state_size],
        decay_rates[0],
    )
    backward_totals, backward_records = block_pass(
        tokens[::-1],
        step_size[head_count:, ::-1],
        projections[::-1, 2 * state_size : 3 * state_size],
        projections[::-1, 3 * state_size :],
        decay_rates[1],
    )
    unused_item, forward_in = exclusive_scan(forward_totals, "seq", False)
    unused_item, backward_in = exclusive_scan(backward_totals, "seq", True)
    forward_out = apply_state(forward_records, forward_in)
    backward_out = apply_state(backward_records, backward_in)[::-1]
    skip_wide = jnp.repeat(skip_gain, head_size)
    mixed_out = forward_out + backward_out + skip_wide[None, :] * flat_tokens.astype(jnp.float32)
    gated_out = mixed_out * jax.nn.silu(gate_input[0].astype(jnp.float32))
    squared = (gated_out * gated_out).reshape(row_count, head_count, head_size)
    mean_square = jnp.mean(squared, axis=2)
    inverse_scale = jnp.repeat(lax.rsqrt(mean_square + 1e-05), head_size, axis=1)
    normed = (gated_out * inverse_scale * norm_gain[None, :]).astype(jnp.bfloat16)
    projected = jnp.dot(
        normed,
        lax.all_gather(out_weight, "dp", axis=0, tiled=True),
        preferred_element_type=jnp.float32,
    )
    encoded = projected.astype(jnp.bfloat16)
    score_scale = 1.0 / math.sqrt(model_width)
    scores = (
        jnp.einsum("rd,sd->rs", latents, encoded, preferred_element_type=jnp.float32) * score_scale
    )
    local_top = jnp.max(jnp.where(is_valid[None, :], scores, -1e30), axis=1)
    prob_values = jnp.where(is_valid[None, :], jnp.exp(scores - local_top[:, None]), 0.0)
    weight_sum = jnp.sum(prob_values, axis=1)
    weighted_sum = jnp.dot(
        prob_values.astype(jnp.bfloat16), encoded, preferred_element_type=jnp.float32
    )
    unused_item, total_weight, total_sum = butterfly_pool(
        (local_top, weight_sum, weighted_sum), "seq"
    )
    pooled = (total_sum / total_weight[:, None]).astype(jnp.bfloat16)
    return (encoded[None], pooled[None])


def solution(mesh):
    in_specs = (
        P("dp", "seq", None),
        P("dp", "seq", None),
        P("dp", "seq", None),
        P("dp", None, "seq"),
        P(),
        P(),
        P(),
        P("dp", None),
        P(),
        P("dp"),
    )
    out_specs = (P("dp", "seq", None), P("dp", None, None))
    return jax.shard_map(body, mesh=mesh, in_specs=in_specs, out_specs=out_specs, check_vma=False)
```

time: 939 us -> 387 us (0.41)
  the two profiles are of different devices: /device:TPU:6 before, /device:TPU:48 now
where the time goes in v1:
time: 387 us; the launch traced here: 385 us
  waiting for transfers between devices  171 us (44%)
  starting transfers between devices  146 us (38%)
  other arithmetic  23.6 us (6%)
  local copies, waits for them, and re-layouts  18.5 us (5%)
  between operations  15.8 us (4%)
  matrix products  9.61 us (2%)
    ppermute x18, waiting for transfers between devices, exclusive_scan(): received = lax.ppermute(inclusive, axis, perm)  90.2 us
    ppermute x15, waiting for transfers between devices, butterfly_pool(): received = lax.ppermute(sent, axis, perm)  81.1 us
    ppermute x18, starting transfers between devices, exclusive_scan(): received = lax.ppermute(inclusive, axis, perm)  75.5 us
    ppermute x15, starting transfers between devices, butterfly_pool(): received = lax.ppermute(sent, axis, perm)  70.5 us
  transfers between devices with their start and end apart: 34, of which 10 were waited for; matrix products, arithmetic and copies ran while one was open for 10% of the time, Pallas kernels for 0%

profile of v1, /device:TPU:48, one launch (start us, length us, event | category | flops | bytes accessed | tf_op | source)
XLA Modules:
  0.0 384.9 jit_solution(2070218298613978890)
XLA Ops:
  15.8 2.6 collective-permute-start.4
  18.4 5.3 %collective-permute-start = (f32[16]{0:T(128)}, f32[16]{0:T(128)}, u32[]{:S(2)}, u32[]{:S(2)}) collective-permute-start(f32[16]{0:T(128)} %get-tuple-element.5), channel_id=1, source_target_pairs={{0,1},{1,2},{2,3},{3,4},{4,5},{5,6},{6,7},{7,8},{8,9},{9,10},{10,1... | collective-permute-start | bytes 200 | tf_op jit(solution)/shard_map/ppermute | solution.py:31
  30.5 1.9 collective-permute-start.9
  35.9 3.0 convolution_bitcast_fusion.3
  38.9 1.9 convolution_bitcast_fusion.2
  41.6 2.0 multiply_add_fusion.7
  43.7 9.9 %collective-permute-start.5 = (f32[16,64,128]{2,1,0:T(8,128)}, f32[16,64,128]{2,1,0:T(8,128)S(1)}, u32[]{:S(2)}, u32[]{:S(2)}) collective-permute-start(f32[16,64,128]{2,1,0:T(8,128)} %multiply_add_fusion.7), channel_id=1, source_target_pairs={{0,2},{1,3},{2,4},{3,5},{4,6},{5,7},{6,8},{7,9},{8,10},{9,11},{10,... | collective-permute-start | bytes 1572872 | tf_op jit(solution)/shard_map/ppermute | solution.py:31
  53.6 2.0 copy.47
  58.4 4.8 %collective-permute-start.10 = (f32[16]{0:T(128)S(1)}, f32[16]{0:T(128)S(1)}, u32[]{:S(2)}, u32[]{:S(2)}) collective-permute-start(f32[16]{0:T(128)S(1)} %get-tuple-element.42), channel_id=1, source_target_pairs={{2,0},{3,1},{4,2},{5,3},{6,4},{7,5},{8,6},{9,7},{10,8},{11,9},{12,... | collective-permute-start | bytes 200 | tf_op jit(solution)/shard_map/ppermute | solution.py:31
  66.4 8.1 %collective-permute-done.5 = f32[16,64,128]{2,1,0:T(8,128)S(1)} collective-permute-done((f32[16,64,128]{2,1,0:T(8,128)}, f32[16,64,128]{2,1,0:T(8,128)S(1)}, u32[]{:S(2)}, u32[]{:S(2)}) %collective-permute-start.5) | collective-permute-done | bytes 524320 | tf_op jit(solution)/shard_map/ppermute | solution.py:31
  75.7 5.1 %collective-permute-start.6 = (f32[16,64,128]{2,1,0:T(8,128)S(1)}, f32[16,64,128]{2,1,0:T(8,128)S(1)}, u32[]{:S(2)}, u32[]{:S(2)}) collective-permute-start(f32[16,64,128]{2,1,0:T(8,128)S(1)} %multiply_add_fusion.6), channel_id=1, source_target_pairs={{0,4},{1,5},{2,6},{3,7},{4,8},{5,9},{6,10},{7,11},{8,12},{9,13},{1... | collective-permute-start | bytes 1572872 | tf_op jit(solution)/shard_map/ppermute | solution.py:31
  80.7 13.3 %collective-permute-start.2 = (f32[16]{0:T(128)S(1)}, f32[16]{0:T(128)S(1)}, u32[]{:S(2)}, u32[]{:S(2)}) collective-permute-start(f32[16]{0:T(128)S(1)} %get-tuple-element.34), channel_id=1, source_target_pairs={{0,4},{1,5},{2,6},{3,7},{4,8},{5,9},{6,10},{7,11},{8,12},{9,13},{1... | collective-permute-start | bytes 200 | tf_op jit(solution)/shard_map/ppermute | solution.py:31
  96.0 26.5 %collective-permute-done.14 = f32[16,64,128]{2,1,0:T(8,128)S(1)} collective-permute-done((f32[16,64,128]{2,1,0:T(8,128)S(1)}, f32[16,64,128]{2,1,0:T(8,128)S(1)}, u32[]{:S(2)}, u32[]{:S(2)}) %collective-permute-start.14) | collective-permute-done | bytes 524320 | tf_op jit(solution)/shard_map/ppermute | solution.py:31
  126.1 4.4 %collective-permute-start.3 = (f32[16]{0:T(128)S(1)}, f32[16]{0:T(128)S(1)}, u32[]{:S(2)}, u32[]{:S(2)}) collective-permute-start(f32[16]{0:T(128)S(1)} %get-tuple-element.32), channel_id=1, source_target_pairs={{0,8},{1,9},{2,10},{3,11},{4,12},{5,13},{6,14},{7,15},{8,16},{9,17... | collective-permute-start | bytes 200 | tf_op jit(solution)/shard_map/ppermute | solution.py:31
  131.8 17.6 %collective-permute-done.15 = f32[16,64,128]{2,1,0:T(8,128)S(1)} collective-permute-done((f32[16,64,128]{2,1,0:T(8,128)S(1)}, f32[16,64,128]{2,1,0:T(8,128)S(1)}, u32[]{:S(2)}, u32[]{:S(2)}) %collective-permute-start.15) | collective-permute-done | bytes 524320 | tf_op jit(solution)/shard_map/ppermute | solution.py:31
  151.0 13.2 %collective-permute-start.8 = (f32[16,64,128]{2,1,0:T(8,128)S(1)}, f32[16,64,128]{2,1,0:T(8,128)S(1)}, u32[]{:S(2)}, u32[]{:S(2)}) collective-permute-start(f32[16,64,128]{2,1,0:T(8,128)S(1)} %multiply_add_fusion.4), channel_id=1, source_target_pairs={{0,16},{1,17},{2,18},{3,19},{4,20},{5,21},{6,22},{7,23},{8,24},{9,... | collective-permute-start | bytes 1572872 | tf_op jit(solution)/shard_map/ppermute | solution.py:31
  165.6 22.2 %collective-permute-done.16 = f32[16,64,128]{2,1,0:T(8,128)S(1)} collective-permute-done((f32[16,64,128]{2,1,0:T(8,128)S(1)}, f32[16,64,128]{2,1,0:T(8,128)S(1)}, u32[]{:S(2)}, u32[]{:S(2)}) %collective-permute-start.16) | collective-permute-done | bytes 524320 | tf_op jit(solution)/shard_map/ppermute | solution.py:31
  192.0 15.8 %collective-permute-done.17 = f32[16,64,128]{2,1,0:T(8,128)S(1)} collective-permute-done((f32[16,64,128]{2,1,0:T(8,128)S(1)}, f32[16,64,128]{2,1,0:T(8,128)S(1)}, u32[]{:S(2)}, u32[]{:S(2)}) %collective-permute-start.17) | collective-permute-done | bytes 524320 | tf_op jit(solution)/shard_map/ppermute | solution.py:31
  211.3 7.5 %rev.19 = f32[256,1024]{0,1:T(8,128)S(1)} reverse(f32[256,1024]{0,1:T(8,128)} %bitcast.203), dimensions={0} | reverse | bytes 2097152 | tf_op jit(solution)/shard_map/rev | solution.py:164
  220.8 2.3 convolution_convert_fusion.1
  225.9 3.9 %collective-permute-start.28 = (f32[256]{0:T(256)S(1)}, f32[256]{0:T(256)S(1)}, u32[]{:S(2)}, u32[]{:S(2)}) collective-permute-start(f32[256]{0:T(256)S(1)} %fusion.60), channel_id=1, source_target_pairs={{0,1},{1,0},{2,3},{3,2},{4,5},{5,4},{6,7},{7,6},{8,9},{9,8},{10,11... | collective-permute-start | bytes 3080 | tf_op jit(solution)/shard_map/ppermute | solution.py:111
  231.8 7.0 %collective-permute-done.28 = f32[256]{0:T(256)S(1)} collective-permute-done((f32[256]{0:T(256)S(1)}, f32[256]{0:T(256)S(1)}, u32[]{:S(2)}, u32[]{:S(2)}) %collective-permute-start.28) | collective-permute-done | bytes 1056 | tf_op jit(solution)/shard_map/ppermute | solution.py:111
  239.1 9.1 %collective-permute-start.20 = (bf16[256,1024]{1,0:T(8,128)(2,1)S(1)}, bf16[256,1024]{1,0:T(8,128)(2,1)S(1)}, u32[]{:S(2)}, u32[]{:S(2)}) collective-permute-start(bf16[256,1024]{1,0:T(8,128)(2,1)S(1)} %fusion.6), channel_id=1, source_target_pairs={{0,2},{1,3},{2,0},{3,1},{4,6},{5,7},{6,4},{7,5},{8,10},{9,11},{10,... | collective-permute-start | bytes 1572872 | tf_op jit(solution)/shard_map/ppermute | solution.py:111
  250.1 4.8 %collective-permute-start.29 = (f32[256]{0:T(256)S(1)}, f32[256]{0:T(256)S(1)}, u32[]{:S(2)}, u32[]{:S(2)}) collective-permute-start(f32[256]{0:T(256)S(1)} %get-tuple-element.25), channel_id=1, source_target_pairs={{0,2},{1,3},{2,0},{3,1},{4,6},{5,7},{6,4},{7,5},{8,10},{9,11},{10,... | collective-permute-start | bytes 3080 | tf_op jit(solution)/shard_map/ppermute | solution.py:111
  255.0 14.6 %collective-permute-done.21 = f32[256]{0:T(256)S(1)} collective-permute-done((f32[256]{0:T(256)S(1)}, f32[256]{0:T(256)S(1)}, u32[]{:S(2)}, u32[]{:S(2)}) %collective-permute-start.21) | collective-permute-done | bytes 1056 | tf_op jit(solution)/shard_map/ppermute | solution.py:111
  271.8 7.8 %collective-permute-start.23 = (f32[256]{0:T(256)S(1)}, f32[256]{0:T(256)S(1)}, u32[]{:S(2)}, u32[]{:S(2)}) collective-permute-start(f32[256]{0:T(256)S(1)} %get-tuple-element.24), channel_id=1, source_target_pairs={{0,4},{1,5},{2,6},{3,7},{4,0},{5,1},{6,2},{7,3},{8,12},{9,13},{10,... | collective-permute-start | bytes 3080 | tf_op jit(solution)/shard_map/ppermute | solution.py:111
  281.6 14.2 %collective-permute-done.23 = f32[256]{0:T(256)S(1)} collective-permute-done((f32[256]{0:T(256)S(1)}, f32[256]{0:T(256)S(1)}, u32[]{:S(2)}, u32[]{:S(2)}) %collective-permute-start.23) | collective-permute-done | bytes 1056 | tf_op jit(solution)/shard_map/ppermute | solution.py:111
  296.1 16.8 %collective-permute-start.24 = (bf16[256,1024]{1,0:T(8,128)(2,1)S(1)}, bf16[256,1024]{1,0:T(8,128)(2,1)S(1)}, u32[]{:S(2)}, u32[]{:S(2)}) collective-permute-start(bf16[256,1024]{1,0:T(8,128)(2,1)S(1)} %fusion.14), channel_id=1, source_target_pairs={{0,8},{1,9},{2,10},{3,11},{4,12},{5,13},{6,14},{7,15},{8,0},{9,1},... | collective-permute-start | bytes 1572872 | tf_op jit(solution)/shard_map/ppermute | solution.py:111
  314.8 4.8 %collective-permute-start.31 = (f32[256]{0:T(256)S(1)}, f32[256]{0:T(256)S(1)}, u32[]{:S(2)}, u32[]{:S(2)}) collective-permute-start(f32[256]{0:T(256)S(1)} %get-tuple-element.17), channel_id=1, source_target_pairs={{0,8},{1,9},{2,10},{3,11},{4,12},{5,13},{6,14},{7,15},{8,0},{9,1},... | collective-permute-start | bytes 3080 | tf_op jit(solution)/shard_map/ppermute | solution.py:111
  319.6 28.7 %collective-permute-done.25 = f32[256]{0:T(256)S(1)} collective-permute-done((f32[256]{0:T(256)S(1)}, f32[256]{0:T(256)S(1)}, u32[]{:S(2)}, u32[]{:S(2)}) %collective-permute-start.25) | collective-permute-done | bytes 1056 | tf_op jit(solution)/shard_map/ppermute | solution.py:111
  350.5 7.8 %collective-permute-start.27 = (f32[256]{0:T(256)S(1)}, f32[256]{0:T(256)S(1)}, u32[]{:S(2)}, u32[]{:S(2)}) collective-permute-start(f32[256]{0:T(256)S(1)} %get-tuple-element.16), channel_id=1, source_target_pairs={{0,16},{1,17},{2,18},{3,19},{4,20},{5,21},{6,22},{7,23},{8,24},{9,... | collective-permute-start | bytes 3080 | tf_op jit(solution)/shard_map/ppermute | solution.py:111
  360.3 16.6 %collective-permute-done.27 = f32[256]{0:T(256)S(1)} collective-permute-done((f32[256]{0:T(256)S(1)}, f32[256]{0:T(256)S(1)}, u32[]{:S(2)}, u32[]{:S(2)}) %collective-permute-start.27) | collective-permute-done | bytes 1056 | tf_op jit(solution)/shard_map/ppermute | solution.py:111
  (174 shorter events, 63.5 us)
Async XLA Ops:
  7.2 213.6 %all-gather.2.cloned.1.call-start = ((), (), s32[]{:S(2)}) async-start(), calls=%async_computation | async-start | bytes 2228224 | tf_op jit(solution)/shard_map/all_gather | solution.py:174
  15.8 25.8 %collective-permute-start.4 = (f32[16,64,128]{2,1,0:T(8,128)}, f32[16,64,128]{2,1,0:T(8,128)}, u32[]{:S(2)}, u32[]{:S(2)}) collective-permute-start(f32[16,64,128]{2,1,0:T(8,128)} %fusion.47), channel_id=1, source_target_pairs={{0,1},{1,2},{2,3},{3,4},{4,5},{5,6},{6,7},{7,8},{8,9},{9,10},{10,1... | collective-permute-start | bytes 1572872 | tf_op jit(solution)/shard_map/ppermute | solution.py:31
  18.4 22.5 %collective-permute-start = (f32[16]{0:T(128)}, f32[16]{0:T(128)}, u32[]{:S(2)}, u32[]{:S(2)}) collective-permute-start(f32[16]{0:T(128)} %get-tuple-element.5), channel_id=1, source_target_pairs={{0,1},{1,2},{2,3},{3,4},{4,5},{5,6},{6,7},{7,8},{8,9},{9,10},{10,1... | collective-permute-start | bytes 200 | tf_op jit(solution)/shard_map/ppermute | solution.py:31
  28.6 34.6 %collective-permute-start.13 = (f32[16,64,128]{2,1,0:T(8,128)}, f32[16,64,128]{2,1,0:T(8,128)}, u32[]{:S(2)}, u32[]{:S(2)}) collective-permute-start(f32[16,64,128]{2,1,0:T(8,128)} %fusion.46), channel_id=1, source_target_pairs={{1,0},{2,1},{3,2},{4,3},{5,4},{6,5},{7,6},{8,7},{9,8},{10,9},{11,1... | collective-permute-start | bytes 1572872 | tf_op jit(solution)/shard_map/ppermute | solution.py:31
  30.5 27.2 %collective-permute-start.9 = (f32[16]{0:T(128)}, f32[16]{0:T(128)}, u32[]{:S(2)}, u32[]{:S(2)}) collective-permute-start(f32[16]{0:T(128)} %get-tuple-element.9), channel_id=1, source_target_pairs={{1,0},{2,1},{3,2},{4,3},{5,4},{6,5},{7,6},{8,7},{9,8},{10,9},{11,1... | collective-permute-start | bytes 200 | tf_op jit(solution)/shard_map/ppermute | solution.py:31
  43.7 30.8 %collective-permute-start.5 = (f32[16,64,128]{2,1,0:T(8,128)}, f32[16,64,128]{2,1,0:T(8,128)S(1)}, u32[]{:S(2)}, u32[]{:S(2)}) collective-permute-start(f32[16,64,128]{2,1,0:T(8,128)} %multiply_add_fusion.7), channel_id=1, source_target_pairs={{0,2},{1,3},{2,4},{3,5},{4,6},{5,7},{6,8},{7,9},{8,10},{9,11},{10,... | collective-permute-start | bytes 1572872 | tf_op jit(solution)/shard_map/ppermute | solution.py:31
  55.8 24.9 %collective-permute-start.1 = (f32[16]{0:T(128)S(1)}, f32[16]{0:T(128)S(1)}, u32[]{:S(2)}, u32[]{:S(2)}) collective-permute-start(f32[16]{0:T(128)S(1)} %get-tuple-element.36), channel_id=1, source_target_pairs={{0,2},{1,3},{2,4},{3,5},{4,6},{5,7},{6,8},{7,9},{8,10},{9,11},{10,... | collective-permute-start | bytes 200 | tf_op jit(solution)/shard_map/ppermute | solution.py:31
  58.4 35.6 %collective-permute-start.10 = (f32[16]{0:T(128)S(1)}, f32[16]{0:T(128)S(1)}, u32[]{:S(2)}, u32[]{:S(2)}) collective-permute-start(f32[16]{0:T(128)S(1)} %get-tuple-element.42), channel_id=1, source_target_pairs={{2,0},{3,1},{4,2},{5,3},{6,4},{7,5},{8,6},{9,7},{10,8},{11,9},{12,... | collective-permute-start | bytes 200 | tf_op jit(solution)/shard_map/ppermute | solution.py:31
  64.5 58.0 %collective-permute-start.14 = (f32[16,64,128]{2,1,0:T(8,128)S(1)}, f32[16,64,128]{2,1,0:T(8,128)S(1)}, u32[]{:S(2)}, u32[]{:S(2)}) collective-permute-start(f32[16,64,128]{2,1,0:T(8,128)S(1)} %multiply_add_fusion.3), channel_id=1, source_target_pairs={{2,0},{3,1},{4,2},{5,3},{6,4},{7,5},{8,6},{9,7},{10,8},{11,9},{12,... | collective-permute-start | bytes 1572872 | tf_op jit(solution)/shard_map/ppermute | solution.py:31
  75.7 48.9 %collective-permute-start.6 = (f32[16,64,128]{2,1,0:T(8,128)S(1)}, f32[16,64,128]{2,1,0:T(8,128)S(1)}, u32[]{:S(2)}, u32[]{:S(2)}) collective-permute-start(f32[16,64,128]{2,1,0:T(8,128)S(1)} %multiply_add_fusion.6), channel_id=1, source_target_pairs={{0,4},{1,5},{2,6},{3,7},{4,8},{5,9},{6,10},{7,11},{8,12},{9,13},{1... | collective-permute-start | bytes 1572872 | tf_op jit(solution)/shard_map/ppermute | solution.py:31
  80.7 45.3 %collective-permute-start.2 = (f32[16]{0:T(128)S(1)}, f32[16]{0:T(128)S(1)}, u32[]{:S(2)}, u32[]{:S(2)}) collective-permute-start(f32[16]{0:T(128)S(1)} %get-tuple-element.34), channel_id=1, source_target_pairs={{0,4},{1,5},{2,6},{3,7},{4,8},{5,9},{6,10},{7,11},{8,12},{9,13},{1... | collective-permute-start | bytes 200 | tf_op jit(solution)/shard_map/ppermute | solution.py:31
  94.0 36.5 %collective-permute-start.11 = (f32[16]{0:T(128)S(1)}, f32[16]{0:T(128)S(1)}, u32[]{:S(2)}, u32[]{:S(2)}) collective-permute-start(f32[16]{0:T(128)S(1)} %get-tuple-element.40), channel_id=1, source_target_pairs={{4,0},{5,1},{6,2},{7,3},{8,4},{9,5},{10,6},{11,7},{12,8},{13,9},{1... | collective-permute-start | bytes 200 | tf_op jit(solution)/shard_map/ppermute | solution.py:31
  122.6 26.8 %collective-permute-start.15 = (f32[16,64,128]{2,1,0:T(8,128)S(1)}, f32[16,64,128]{2,1,0:T(8,128)S(1)}, u32[]{:S(2)}, u32[]{:S(2)}) collective-permute-start(f32[16,64,128]{2,1,0:T(8,128)S(1)} %multiply_add_fusion.2), channel_id=1, source_target_pairs={{4,0},{5,1},{6,2},{7,3},{8,4},{9,5},{10,6},{11,7},{12,8},{13,9},{1... | collective-permute-start | bytes 1572872 | tf_op jit(solution)/shard_map/ppermute | solution.py:31
  124.7 26.1 %collective-permute-start.7 = (f32[16,64,128]{2,1,0:T(8,128)S(1)}, f32[16,64,128]{2,1,0:T(8,128)S(1)}, u32[]{:S(2)}, u32[]{:S(2)}) collective-permute-start(f32[16,64,128]{2,1,0:T(8,128)S(1)} %multiply_add_fusion.5), channel_id=1, source_target_pairs={{0,8},{1,9},{2,10},{3,11},{4,12},{5,13},{6,14},{7,15},{8,16},{9,17... | collective-permute-start | bytes 1572872 | tf_op jit(solution)/shard_map/ppermute | solution.py:31
  126.1 38.1 %collective-permute-start.3 = (f32[16]{0:T(128)S(1)}, f32[16]{0:T(128)S(1)}, u32[]{:S(2)}, u32[]{:S(2)}) collective-permute-start(f32[16]{0:T(128)S(1)} %get-tuple-element.32), channel_id=1, source_target_pairs={{0,8},{1,9},{2,10},{3,11},{4,12},{5,13},{6,14},{7,15},{8,16},{9,17... | collective-permute-start | bytes 200 | tf_op jit(solution)/shard_map/ppermute | solution.py:31
  130.5 34.4 %collective-permute-start.12 = (f32[16]{0:T(128)S(1)}, f32[16]{0:T(128)S(1)}, u32[]{:S(2)}, u32[]{:S(2)}) collective-permute-start(f32[16]{0:T(128)S(1)} %get-tuple-element.38), channel_id=1, source_target_pairs={{8,0},{9,1},{10,2},{11,3},{12,4},{13,5},{14,6},{15,7},{16,8},{17,9... | collective-permute-start | bytes 200 | tf_op jit(solution)/shard_map/ppermute | solution.py:31
  149.5 38.2 %collective-permute-start.16 = (f32[16,64,128]{2,1,0:T(8,128)S(1)}, f32[16,64,128]{2,1,0:T(8,128)S(1)}, u32[]{:S(2)}, u32[]{:S(2)}) collective-permute-start(f32[16,64,128]{2,1,0:T(8,128)S(1)} %multiply_add_fusion.1), channel_id=1, source_target_pairs={{8,0},{9,1},{10,2},{11,3},{12,4},{13,5},{14,6},{15,7},{16,8},{17,9... | collective-permute-start | bytes 1572872 | tf_op jit(solution)/shard_map/ppermute | solution.py:31
  151.0 38.5 %collective-permute-start.8 = (f32[16,64,128]{2,1,0:T(8,128)S(1)}, f32[16,64,128]{2,1,0:T(8,128)S(1)}, u32[]{:S(2)}, u32[]{:S(2)}) collective-permute-start(f32[16,64,128]{2,1,0:T(8,128)S(1)} %multiply_add_fusion.4), channel_id=1, source_target_pairs={{0,16},{1,17},{2,18},{3,19},{4,20},{5,21},{6,22},{7,23},{8,24},{9,... | collective-permute-start | bytes 1572872 | tf_op jit(solution)/shard_map/ppermute | solution.py:31
  187.9 19.9 %collective-permute-start.17 = (f32[16,64,128]{2,1,0:T(8,128)S(1)}, f32[16,64,128]{2,1,0:T(8,128)S(1)}, u32[]{:S(2)}, u32[]{:S(2)}) collective-permute-start(f32[16,64,128]{2,1,0:T(8,128)S(1)} %multiply_add_fusion), channel_id=1, source_target_pairs={{16,0},{17,1},{18,2},{19,3},{20,4},{21,5},{22,6},{23,7},{24,8},{25... | collective-permute-start | bytes 1572872 | tf_op jit(solution)/shard_map/ppermute | solution.py:31
  223.9 14.9 %collective-permute-start.18 = (bf16[256,1024]{1,0:T(8,128)(2,1)S(1)}, bf16[256,1024]{1,0:T(8,128)(2,1)S(1)}, u32[]{:S(2)}, u32[]{:S(2)}) collective-permute-start(bf16[256,1024]{1,0:T(8,128)(2,1)S(1)} %convolution_convert_fusion), channel_id=1, source_target_pairs={{0,1},{1,0},{2,3},{3,2},{4,5},{5,4},{6,7},{7,6},{8,9},{9,8},{10,11... | collective-permute-start | bytes 1572872 | tf_op jit(solution)/shard_map/ppermute | solution.py:111
  239.1 30.5 %collective-permute-start.20 = (bf16[256,1024]{1,0:T(8,128)(2,1)S(1)}, bf16[256,1024]{1,0:T(8,128)(2,1)S(1)}, u32[]{:S(2)}, u32[]{:S(2)}) collective-permute-start(bf16[256,1024]{1,0:T(8,128)(2,1)S(1)} %fusion.6), channel_id=1, source_target_pairs={{0,2},{1,3},{2,0},{3,1},{4,6},{5,7},{6,4},{7,5},{8,10},{9,11},{10,... | collective-permute-start | bytes 1572872 | tf_op jit(solution)/shard_map/ppermute | solution.py:111
  248.2 21.4 %collective-permute-start.21 = (f32[256]{0:T(256)S(1)}, f32[256]{0:T(256)S(1)}, u32[]{:S(2)}, u32[]{:S(2)}) collective-permute-start(f32[256]{0:T(256)S(1)} %get-tuple-element.28), channel_id=1, source_target_pairs={{0,2},{1,3},{2,0},{3,1},{4,6},{5,7},{6,4},{7,5},{8,10},{9,11},{10,... | collective-permute-start | bytes 3080 | tf_op jit(solution)/shard_map/ppermute | solution.py:111
  250.1 19.5 %collective-permute-start.29 = (f32[256]{0:T(256)S(1)}, f32[256]{0:T(256)S(1)}, u32[]{:S(2)}, u32[]{:S(2)}) collective-permute-start(f32[256]{0:T(256)S(1)} %get-tuple-element.25), channel_id=1, source_target_pairs={{0,2},{1,3},{2,0},{3,1},{4,6},{5,7},{6,4},{7,5},{8,10},{9,11},{10,... | collective-permute-start | bytes 3080 | tf_op jit(solution)/shard_map/ppermute | solution.py:111
  269.9 25.9 %collective-permute-start.22 = (bf16[256,1024]{1,0:T(8,128)(2,1)S(1)}, bf16[256,1024]{1,0:T(8,128)(2,1)S(1)}, u32[]{:S(2)}, u32[]{:S(2)}) collective-permute-start(bf16[256,1024]{1,0:T(8,128)(2,1)S(1)} %fusion.10), channel_id=1, source_target_pairs={{0,4},{1,5},{2,6},{3,7},{4,0},{5,1},{6,2},{7,3},{8,12},{9,13},{10,... | collective-permute-start | bytes 1572872 | tf_op jit(solution)/shard_map/ppermute | solution.py:111
  271.8 23.9 %collective-permute-start.23 = (f32[256]{0:T(256)S(1)}, f32[256]{0:T(256)S(1)}, u32[]{:S(2)}, u32[]{:S(2)}) collective-permute-start(f32[256]{0:T(256)S(1)} %get-tuple-element.24), channel_id=1, source_target_pairs={{0,4},{1,5},{2,6},{3,7},{4,0},{5,1},{6,2},{7,3},{8,12},{9,13},{10,... | collective-permute-start | bytes 3080 | tf_op jit(solution)/shard_map/ppermute | solution.py:111
  279.7 16.1 %collective-permute-start.30 = (f32[256]{0:T(256)S(1)}, f32[256]{0:T(256)S(1)}, u32[]{:S(2)}, u32[]{:S(2)}) collective-permute-start(f32[256]{0:T(256)S(1)} %get-tuple-element.21), channel_id=1, source_target_pairs={{0,4},{1,5},{2,6},{3,7},{4,0},{5,1},{6,2},{7,3},{8,12},{9,13},{10,... | collective-permute-start | bytes 3080 | tf_op jit(solution)/shard_map/ppermute | solution.py:111
  296.1 52.2 %collective-permute-start.24 = (bf16[256,1024]{1,0:T(8,128)(2,1)S(1)}, bf16[256,1024]{1,0:T(8,128)(2,1)S(1)}, u32[]{:S(2)}, u32[]{:S(2)}) collective-permute-start(bf16[256,1024]{1,0:T(8,128)(2,1)S(1)} %fusion.14), channel_id=1, source_target_pairs={{0,8},{1,9},{2,10},{3,11},{4,12},{5,13},{6,14},{7,15},{8,0},{9,1},... | collective-permute-start | bytes 1572872 | tf_op jit(solution)/shard_map/ppermute | solution.py:111
  312.9 35.4 %collective-permute-start.25 = (f32[256]{0:T(256)S(1)}, f32[256]{0:T(256)S(1)}, u32[]{:S(2)}, u32[]{:S(2)}) collective-permute-start(f32[256]{0:T(256)S(1)} %get-tuple-element.20), channel_id=1, source_target_pairs={{0,8},{1,9},{2,10},{3,11},{4,12},{5,13},{6,14},{7,15},{8,0},{9,1},... | collective-permute-start | bytes 3080 | tf_op jit(solution)/shard_map/ppermute | solution.py:111
  314.8 33.5 %collective-permute-start.31 = (f32[256]{0:T(256)S(1)}, f32[256]{0:T(256)S(1)}, u32[]{:S(2)}, u32[]{:S(2)}) collective-permute-start(f32[256]{0:T(256)S(1)} %get-tuple-element.17), channel_id=1, source_target_pairs={{0,8},{1,9},{2,10},{3,11},{4,12},{5,13},{6,14},{7,15},{8,0},{9,1},... | collective-permute-start | bytes 3080 | tf_op jit(solution)/shard_map/ppermute | solution.py:111
  348.6 28.3 %collective-permute-start.26 = (bf16[256,1024]{1,0:T(8,128)(2,1)S(1)}, bf16[256,1024]{1,0:T(8,128)(2,1)S(1)}, u32[]{:S(2)}, u32[]{:S(2)}) collective-permute-start(bf16[256,1024]{1,0:T(8,128)(2,1)S(1)} %fusion.18), channel_id=1, source_target_pairs={{0,16},{1,17},{2,18},{3,19},{4,20},{5,21},{6,22},{7,23},{8,24},{9,... | collective-permute-start | bytes 1572872 | tf_op jit(solution)/shard_map/ppermute | solution.py:111
  350.5 26.4 %collective-permute-start.27 = (f32[256]{0:T(256)S(1)}, f32[256]{0:T(256)S(1)}, u32[]{:S(2)}, u32[]{:S(2)}) collective-permute-start(f32[256]{0:T(256)S(1)} %get-tuple-element.16), channel_id=1, source_target_pairs={{0,16},{1,17},{2,18},{3,19},{4,20},{5,21},{6,22},{7,23},{8,24},{9,... | collective-permute-start | bytes 3080 | tf_op jit(solution)/shard_map/ppermute | solution.py:111
  358.4 18.6 %collective-permute-start.32 = (f32[256]{0:T(256)S(1)}, f32[256]{0:T(256)S(1)}, u32[]{:S(2)}, u32[]{:S(2)}) collective-permute-start(f32[256]{0:T(256)S(1)} %get-tuple-element.13), channel_id=1, source_target_pairs={{0,16},{1,17},{2,18},{3,19},{4,20},{5,21},{6,22},{7,23},{8,24},{9,... | collective-permute-start | bytes 3080 | tf_op jit(solution)/shard_map/ppermute | solution.py:111
  (27 other events, 421.9 us)
Sparse Core Ops, SparseCore 0:
  32.6 44.5 all-gather.1

commit v2 on v1

--- a/solution.py
+++ b/solution.py
@@ -28,7 +28,9 @@
             perm = [(q, q - shift) for q in range(shift, count)]
         else:
             perm = [(q, q + shift) for q in range(count - shift)]
-        received = lax.ppermute(inclusive, axis, perm)
+        sent = (inclusive[0], inclusive[1].astype(jnp.bfloat16))
+        received = lax.ppermute(sent, axis, perm)
+        received = (received[0], received[1].astype(jnp.float32))
         exclusive = chain_combine(received, exclusive)
         if k + 1 < rounds:
             inclusive = chain_combine(received, inclusive)

time: 387 us -> 335 us (0.87)
  the two profiles are of different devices: /device:TPU:48 before, /device:TPU:4 now
where the time goes in v2:
time: 335 us; the launch traced here: 333 us
  starting transfers between devices  165 us (49%)
  waiting for transfers between devices  101 us (30%)
  local copies, waits for them, and re-layouts  21.7 us (6%)
  other arithmetic  20.5 us (6%)
  between operations  15.9 us (5%)
  matrix products  9.17 us (3%)
    ppermute x18, starting transfers between devices, exclusive_scan(): received = lax.ppermute(sent, axis, perm)  97.3 us
    ppermute x15, waiting for transfers between devices, butterfly_pool(): received = lax.ppermute(sent, axis, perm)  68.4 us
    ppermute x15, starting transfers between devices, butterfly_pool(): received = lax.ppermute(sent, axis, perm)  67.4 us
    ppermute x18, waiting for transfers between devices, exclusive_scan(): received = lax.ppermute(sent, axis, perm)  32.9 us
    rev x1, local copies, waits for them, and re-layouts, body(): backward_out = apply_state(backward_records, backward_in)[::-1]  7.5 us
  transfers between devices with their start and end apart: 34, of which 10 were waited for; matrix products, arithmetic and copies ran while one was open for 12% of the time, Pallas kernels for 0%

profile of v2, /device:TPU:4, one launch (start us, length us, event | category | flops | bytes accessed | tf_op | source)
XLA Modules:
  0.0 333.5 jit_solution(2235305705794550425)
XLA Ops:
  15.4 3.5 %collective-permute-start.4 = (bf16[16,64,128]{2,1,0:T(8,128)(2,1)}, bf16[16,64,128]{2,1,0:T(8,128)(2,1)S(1)}, u32[]{:S(2)}, u32[]{:S(2)}) collective-permute-start(bf16[16,64,128]{2,1,0:T(8,128)(2,1)} %get-tuple-element.39), channel_id=1, source_target_pairs={{0,1},{1,2},{2,3},{3,4},{4,5},{5,6},{6,7},{7,8},{8,9},{9,10},{10,1... | collective-permute-start | bytes 786440 | tf_op jit(solution)/shard_map/ppermute | solution.py:32
  18.9 4.0 %collective-permute-start = (f32[16]{0:T(128)}, f32[16]{0:T(128)}, u32[]{:S(2)}, u32[]{:S(2)}) collective-permute-start(f32[16]{0:T(128)} %get-tuple-element.5), channel_id=1, source_target_pairs={{0,1},{1,2},{2,3},{3,4},{4,5},{5,6},{6,7},{7,8},{8,9},{9,10},{10,1... | collective-permute-start | bytes 200 | tf_op jit(solution)/shard_map/ppermute | solution.py:32
  37.0 2.0 copy.47
  40.3 1.9 convolution_bitcast_fusion.3
  44.8 6.6 %collective-permute-start.1 = (f32[16]{0:T(128)S(1)}, f32[16]{0:T(128)S(1)}, u32[]{:S(2)}, u32[]{:S(2)}) collective-permute-start(f32[16]{0:T(128)S(1)} %get-tuple-element.38), channel_id=1, source_target_pairs={{0,2},{1,3},{2,4},{3,5},{4,6},{5,7},{6,8},{7,9},{8,10},{9,11},{10,... | collective-permute-start | bytes 200 | tf_op jit(solution)/shard_map/ppermute | solution.py:32
  53.4 10.6 %collective-permute-start.2 = (f32[16]{0:T(128)S(1)}, f32[16]{0:T(128)S(1)}, u32[]{:S(2)}, u32[]{:S(2)}) collective-permute-start(f32[16]{0:T(128)S(1)} %get-tuple-element.34), channel_id=1, source_target_pairs={{0,4},{1,5},{2,6},{3,7},{4,8},{5,9},{6,10},{7,11},{8,12},{9,13},{1... | collective-permute-start | bytes 200 | tf_op jit(solution)/shard_map/ppermute | solution.py:32
  65.3 12.2 %collective-permute-start.3 = (f32[16]{0:T(128)S(1)}, f32[16]{0:T(128)S(1)}, u32[]{:S(2)}, u32[]{:S(2)}) collective-permute-start(f32[16]{0:T(128)S(1)} %get-tuple-element.32), channel_id=1, source_target_pairs={{0,8},{1,9},{2,10},{3,11},{4,12},{5,13},{6,14},{7,15},{8,16},{9,17... | collective-permute-start | bytes 200 | tf_op jit(solution)/shard_map/ppermute | solution.py:32
  77.7 2.0 collective-permute-start.5
  83.9 15.7 %collective-permute-start.6 = (bf16[16,64,128]{2,1,0:T(8,128)(2,1)S(1)}, bf16[16,64,128]{2,1,0:T(8,128)(2,1)S(1)}, u32[]{:S(2)}, u32[]{:S(2)}) collective-permute-start(bf16[16,64,128]{2,1,0:T(8,128)(2,1)S(1)} %get-tuple-element.35), channel_id=1, source_target_pairs={{0,4},{1,5},{2,6},{3,7},{4,8},{5,9},{6,10},{7,11},{8,12},{9,13},{1... | collective-permute-start | bytes 786440 | tf_op jit(solution)/shard_map/ppermute | solution.py:32
  102.0 13.9 %collective-permute-done.6 = bf16[16,64,128]{2,1,0:T(8,128)(2,1)S(1)} collective-permute-done((bf16[16,64,128]{2,1,0:T(8,128)(2,1)S(1)}, bf16[16,64,128]{2,1,0:T(8,128)(2,1)S(1)}, u32[]{:S(2)}, u32[]{:S(2)}) %collective-permute-start.6) | collective-permute-done | bytes 262176 | tf_op jit(solution)/shard_map/ppermute | solution.py:32
  116.1 15.2 %collective-permute-start.7 = (bf16[16,64,128]{2,1,0:T(8,128)(2,1)S(1)}, bf16[16,64,128]{2,1,0:T(8,128)(2,1)S(1)}, u32[]{:S(2)}, u32[]{:S(2)}) collective-permute-start(bf16[16,64,128]{2,1,0:T(8,128)(2,1)S(1)} %fusion.78), channel_id=1, source_target_pairs={{0,8},{1,9},{2,10},{3,11},{4,12},{5,13},{6,14},{7,15},{8,16},{9,17... | collective-permute-start | bytes 786440 | tf_op jit(solution)/shard_map/ppermute | solution.py:32
  135.4 15.8 %collective-permute-start.8 = (bf16[16,64,128]{2,1,0:T(8,128)(2,1)S(1)}, bf16[16,64,128]{2,1,0:T(8,128)(2,1)S(1)}, u32[]{:S(2)}, u32[]{:S(2)}) collective-permute-start(bf16[16,64,128]{2,1,0:T(8,128)(2,1)S(1)} %fusion.51), channel_id=1, source_target_pairs={{0,16},{1,17},{2,18},{3,19},{4,20},{5,21},{6,22},{7,23},{8,24},{9,... | collective-permute-start | bytes 786440 | tf_op jit(solution)/shard_map/ppermute | solution.py:32
  153.6 3.9 %collective-permute-done.8 = bf16[16,64,128]{2,1,0:T(8,128)(2,1)S(1)} collective-permute-done((bf16[16,64,128]{2,1,0:T(8,128)(2,1)S(1)}, bf16[16,64,128]{2,1,0:T(8,128)(2,1)S(1)}, u32[]{:S(2)}, u32[]{:S(2)}) %collective-permute-start.8) | collective-permute-done | bytes 262176 | tf_op jit(solution)/shard_map/ppermute | solution.py:32
  159.0 13.1 %collective-permute-done.17 = bf16[16,64,128]{2,1,0:T(8,128)(2,1)S(1)} collective-permute-done((bf16[16,64,128]{2,1,0:T(8,128)(2,1)S(1)}, bf16[16,64,128]{2,1,0:T(8,128)(2,1)S(1)}, u32[]{:S(2)}, u32[]{:S(2)}) %collective-permute-start.17) | collective-permute-done | bytes 262176 | tf_op jit(solution)/shard_map/ppermute | solution.py:32
  175.6 7.5 %rev.19 = f32[256,1024]{0,1:T(8,128)S(1)} reverse(f32[256,1024]{0,1:T(8,128)} %bitcast.199), dimensions={0} | reverse | bytes 2097152 | tf_op jit(solution)/shard_map/rev | solution.py:166
  185.0 2.3 convolution_convert_fusion.1
  188.2 1.9 collective-permute-start.18
  190.2 3.9 %collective-permute-start.28 = (f32[256]{0:T(256)S(1)}, f32[256]{0:T(256)S(1)}, u32[]{:S(2)}, u32[]{:S(2)}) collective-permute-start(f32[256]{0:T(256)S(1)} %fusion.80), channel_id=1, source_target_pairs={{0,1},{1,0},{2,3},{3,2},{4,5},{5,4},{6,7},{7,6},{8,9},{9,8},{10,11... | collective-permute-start | bytes 3080 | tf_op jit(solution)/shard_map/ppermute | solution.py:113
  196.1 6.3 %collective-permute-done.28 = f32[256]{0:T(256)S(1)} collective-permute-done((f32[256]{0:T(256)S(1)}, f32[256]{0:T(256)S(1)}, u32[]{:S(2)}, u32[]{:S(2)}) %collective-permute-start.28) | collective-permute-done | bytes 1056 | tf_op jit(solution)/shard_map/ppermute | solution.py:113
  202.7 1.9 collective-permute-start.20
  204.6 4.8 %collective-permute-start.21 = (f32[256]{0:T(256)S(1)}, f32[256]{0:T(256)S(1)}, u32[]{:S(2)}, u32[]{:S(2)}) collective-permute-start(f32[256]{0:T(256)S(1)} %get-tuple-element.28), channel_id=1, source_target_pairs={{0,2},{1,3},{2,0},{3,1},{4,6},{5,7},{6,4},{7,5},{8,10},{9,11},{10,... | collective-permute-start | bytes 3080 | tf_op jit(solution)/shard_map/ppermute | solution.py:113
  211.4 7.9 %collective-permute-done.21 = f32[256]{0:T(256)S(1)} collective-permute-done((f32[256]{0:T(256)S(1)}, f32[256]{0:T(256)S(1)}, u32[]{:S(2)}, u32[]{:S(2)}) %collective-permute-start.21) | collective-permute-done | bytes 1056 | tf_op jit(solution)/shard_map/ppermute | solution.py:113
  219.6 7.2 %collective-permute-start.22 = (bf16[256,1024]{1,0:T(8,128)(2,1)S(1)}, bf16[256,1024]{1,0:T(8,128)(2,1)S(1)}, u32[]{:S(2)}, u32[]{:S(2)}) collective-permute-start(bf16[256,1024]{1,0:T(8,128)(2,1)S(1)} %fusion.10), channel_id=1, source_target_pairs={{0,4},{1,5},{2,6},{3,7},{4,0},{5,1},{6,2},{7,3},{8,12},{9,13},{10,... | collective-permute-start | bytes 1572872 | tf_op jit(solution)/shard_map/ppermute | solution.py:113
  226.8 2.6 collective-permute-start.23
  229.4 7.2 %collective-permute-start.30 = (f32[256]{0:T(256)S(1)}, f32[256]{0:T(256)S(1)}, u32[]{:S(2)}, u32[]{:S(2)}) collective-permute-start(f32[256]{0:T(256)S(1)} %get-tuple-element.21), channel_id=1, source_target_pairs={{0,4},{1,5},{2,6},{3,7},{4,0},{5,1},{6,2},{7,3},{8,12},{9,13},{10,... | collective-permute-start | bytes 3080 | tf_op jit(solution)/shard_map/ppermute | solution.py:113
  236.6 2.2 collective-permute-done.30
  239.1 15.6 %collective-permute-start.24 = (bf16[256,1024]{1,0:T(8,128)(2,1)S(1)}, bf16[256,1024]{1,0:T(8,128)(2,1)S(1)}, u32[]{:S(2)}, u32[]{:S(2)}) collective-permute-start(bf16[256,1024]{1,0:T(8,128)(2,1)S(1)} %fusion.14), channel_id=1, source_target_pairs={{0,8},{1,9},{2,10},{3,11},{4,12},{5,13},{6,14},{7,15},{8,0},{9,1},... | collective-permute-start | bytes 1572872 | tf_op jit(solution)/shard_map/ppermute | solution.py:113
  256.6 4.8 %collective-permute-start.31 = (f32[256]{0:T(256)S(1)}, f32[256]{0:T(256)S(1)}, u32[]{:S(2)}, u32[]{:S(2)}) collective-permute-start(f32[256]{0:T(256)S(1)} %get-tuple-element.17), channel_id=1, source_target_pairs={{0,8},{1,9},{2,10},{3,11},{4,12},{5,13},{6,14},{7,15},{8,0},{9,1},... | collective-permute-start | bytes 3080 | tf_op jit(solution)/shard_map/ppermute | solution.py:113
  261.5 35.6 %collective-permute-done.25 = f32[256]{0:T(256)S(1)} collective-permute-done((f32[256]{0:T(256)S(1)}, f32[256]{0:T(256)S(1)}, u32[]{:S(2)}, u32[]{:S(2)}) %collective-permute-start.25) | collective-permute-done | bytes 1056 | tf_op jit(solution)/shard_map/ppermute | solution.py:113
  297.3 1.9 collective-permute-start.26
  299.3 7.8 %collective-permute-start.27 = (f32[256]{0:T(256)S(1)}, f32[256]{0:T(256)S(1)}, u32[]{:S(2)}, u32[]{:S(2)}) collective-permute-start(f32[256]{0:T(256)S(1)} %get-tuple-element.16), channel_id=1, source_target_pairs={{0,16},{1,17},{2,18},{3,19},{4,20},{5,21},{6,22},{7,23},{8,24},{9,... | collective-permute-start | bytes 3080 | tf_op jit(solution)/shard_map/ppermute | solution.py:113
  309.0 16.4 %collective-permute-done.27 = f32[256]{0:T(256)S(1)} collective-permute-done((f32[256]{0:T(256)S(1)}, f32[256]{0:T(256)S(1)}, u32[]{:S(2)}, u32[]{:S(2)}) %collective-permute-start.27) | collective-permute-done | bytes 1056 | tf_op jit(solution)/shard_map/ppermute | solution.py:113
  (188 shorter events, 59.2 us)
Async XLA Ops:
  7.2 177.8 %all-gather.2.cloned.1.call-start = ((), (), s32[]{:S(2)}) async-start(), calls=%async_computation | async-start | bytes 2228224 | tf_op jit(solution)/shard_map/all_gather | solution.py:176
  15.4 62.2 %collective-permute-start.4 = (bf16[16,64,128]{2,1,0:T(8,128)(2,1)}, bf16[16,64,128]{2,1,0:T(8,128)(2,1)S(1)}, u32[]{:S(2)}, u32[]{:S(2)}) collective-permute-start(bf16[16,64,128]{2,1,0:T(8,128)(2,1)} %get-tuple-element.39), channel_id=1, source_target_pairs={{0,1},{1,2},{2,3},{3,4},{4,5},{5,6},{6,7},{7,8},{8,9},{9,10},{10,1... | collective-permute-start | bytes 786440 | tf_op jit(solution)/shard_map/ppermute | solution.py:32
  18.9 25.2 %collective-permute-start = (f32[16]{0:T(128)}, f32[16]{0:T(128)}, u32[]{:S(2)}, u32[]{:S(2)}) collective-permute-start(f32[16]{0:T(128)} %get-tuple-element.5), channel_id=1, source_target_pairs={{0,1},{1,2},{2,3},{3,4},{4,5},{5,6},{6,7},{7,8},{8,9},{9,10},{10,1... | collective-permute-start | bytes 200 | tf_op jit(solution)/shard_map/ppermute | solution.py:32
  28.0 53.0 %collective-permute-start.13 = (bf16[16,64,128]{2,1,0:T(8,128)(2,1)}, bf16[16,64,128]{2,1,0:T(8,128)(2,1)}, u32[]{:S(2)}, u32[]{:S(2)}) collective-permute-start(bf16[16,64,128]{2,1,0:T(8,128)(2,1)} %get-tuple-element.49), channel_id=1, source_target_pairs={{1,0},{2,1},{3,2},{4,3},{5,4},{6,5},{7,6},{8,7},{9,8},{10,9},{11,1... | collective-permute-start | bytes 786440 | tf_op jit(solution)/shard_map/ppermute | solution.py:32
  29.3 22.1 %collective-permute-start.9 = (f32[16]{0:T(128)}, f32[16]{0:T(128)}, u32[]{:S(2)}, u32[]{:S(2)}) collective-permute-start(f32[16]{0:T(128)} %get-tuple-element.9), channel_id=1, source_target_pairs={{1,0},{2,1},{3,2},{4,3},{5,4},{6,5},{7,6},{8,7},{9,8},{10,9},{11,1... | collective-permute-start | bytes 200 | tf_op jit(solution)/shard_map/ppermute | solution.py:32
  44.8 8.6 %collective-permute-start.1 = (f32[16]{0:T(128)S(1)}, f32[16]{0:T(128)S(1)}, u32[]{:S(2)}, u32[]{:S(2)}) collective-permute-start(f32[16]{0:T(128)S(1)} %get-tuple-element.38), channel_id=1, source_target_pairs={{0,2},{1,3},{2,4},{3,5},{4,6},{5,7},{6,8},{7,9},{8,10},{9,11},{10,... | collective-permute-start | bytes 200 | tf_op jit(solution)/shard_map/ppermute | solution.py:32
  52.1 11.9 %collective-permute-start.10 = (f32[16]{0:T(128)S(1)}, f32[16]{0:T(128)S(1)}, u32[]{:S(2)}, u32[]{:S(2)}) collective-permute-start(f32[16]{0:T(128)S(1)} %get-tuple-element.48), channel_id=1, source_target_pairs={{2,0},{3,1},{4,2},{5,3},{6,4},{7,5},{8,6},{9,7},{10,8},{11,9},{12,... | collective-permute-start | bytes 200 | tf_op jit(solution)/shard_map/ppermute | solution.py:32
  53.4 11.9 %collective-permute-start.2 = (f32[16]{0:T(128)S(1)}, f32[16]{0:T(128)S(1)}, u32[]{:S(2)}, u32[]{:S(2)}) collective-permute-start(f32[16]{0:T(128)S(1)} %get-tuple-element.34), channel_id=1, source_target_pairs={{0,4},{1,5},{2,6},{3,7},{4,8},{5,9},{6,10},{7,11},{8,12},{9,13},{1... | collective-permute-start | bytes 200 | tf_op jit(solution)/shard_map/ppermute | solution.py:32
  64.0 15.7 %collective-permute-start.11 = (f32[16]{0:T(128)S(1)}, f32[16]{0:T(128)S(1)}, u32[]{:S(2)}, u32[]{:S(2)}) collective-permute-start(f32[16]{0:T(128)S(1)} %get-tuple-element.44), channel_id=1, source_target_pairs={{4,0},{5,1},{6,2},{7,3},{8,4},{9,5},{10,6},{11,7},{12,8},{13,9},{1... | collective-permute-start | bytes 200 | tf_op jit(solution)/shard_map/ppermute | solution.py:32
  65.3 66.0 %collective-permute-start.3 = (f32[16]{0:T(128)S(1)}, f32[16]{0:T(128)S(1)}, u32[]{:S(2)}, u32[]{:S(2)}) collective-permute-start(f32[16]{0:T(128)S(1)} %get-tuple-element.32), channel_id=1, source_target_pairs={{0,8},{1,9},{2,10},{3,11},{4,12},{5,13},{6,14},{7,15},{8,16},{9,17... | collective-permute-start | bytes 200 | tf_op jit(solution)/shard_map/ppermute | solution.py:32
  79.8 71.4 %collective-permute-start.12 = (f32[16]{0:T(128)S(1)}, f32[16]{0:T(128)S(1)}, u32[]{:S(2)}, u32[]{:S(2)}) collective-permute-start(f32[16]{0:T(128)S(1)} %get-tuple-element.42), channel_id=1, source_target_pairs={{8,0},{9,1},{10,2},{11,3},{12,4},{13,5},{14,6},{15,7},{16,8},{17,9... | collective-permute-start | bytes 200 | tf_op jit(solution)/shard_map/ppermute | solution.py:32
  82.2 17.3 %collective-permute-start.14 = (bf16[16,64,128]{2,1,0:T(8,128)(2,1)S(1)}, bf16[16,64,128]{2,1,0:T(8,128)(2,1)S(1)}, u32[]{:S(2)}, u32[]{:S(2)}) collective-permute-start(bf16[16,64,128]{2,1,0:T(8,128)(2,1)S(1)} %fusion.77), channel_id=1, source_target_pairs={{2,0},{3,1},{4,2},{5,3},{6,4},{7,5},{8,6},{9,7},{10,8},{11,9},{12,... | collective-permute-start | bytes 786440 | tf_op jit(solution)/shard_map/ppermute | solution.py:32
  83.9 32.1 %collective-permute-start.6 = (bf16[16,64,128]{2,1,0:T(8,128)(2,1)S(1)}, bf16[16,64,128]{2,1,0:T(8,128)(2,1)S(1)}, u32[]{:S(2)}, u32[]{:S(2)}) collective-permute-start(bf16[16,64,128]{2,1,0:T(8,128)(2,1)S(1)} %get-tuple-element.35), channel_id=1, source_target_pairs={{0,4},{1,5},{2,6},{3,7},{4,8},{5,9},{6,10},{7,11},{8,12},{9,13},{1... | collective-permute-start | bytes 786440 | tf_op jit(solution)/shard_map/ppermute | solution.py:32
  100.7 31.3 %collective-permute-start.15 = (bf16[16,64,128]{2,1,0:T(8,128)(2,1)S(1)}, bf16[16,64,128]{2,1,0:T(8,128)(2,1)S(1)}, u32[]{:S(2)}, u32[]{:S(2)}) collective-permute-start(bf16[16,64,128]{2,1,0:T(8,128)(2,1)S(1)} %get-tuple-element.45), channel_id=1, source_target_pairs={{4,0},{5,1},{6,2},{7,3},{8,4},{9,5},{10,6},{11,7},{12,8},{13,9},{1... | collective-permute-start | bytes 786440 | tf_op jit(solution)/shard_map/ppermute | solution.py:32
  116.1 19.1 %collective-permute-start.7 = (bf16[16,64,128]{2,1,0:T(8,128)(2,1)S(1)}, bf16[16,64,128]{2,1,0:T(8,128)(2,1)S(1)}, u32[]{:S(2)}, u32[]{:S(2)}) collective-permute-start(bf16[16,64,128]{2,1,0:T(8,128)(2,1)S(1)} %fusion.78), channel_id=1, source_target_pairs={{0,8},{1,9},{2,10},{3,11},{4,12},{5,13},{6,14},{7,15},{8,16},{9,17... | collective-permute-start | bytes 786440 | tf_op jit(solution)/shard_map/ppermute | solution.py:32
  132.1 19.8 %collective-permute-start.16 = (bf16[16,64,128]{2,1,0:T(8,128)(2,1)S(1)}, bf16[16,64,128]{2,1,0:T(8,128)(2,1)S(1)}, u32[]{:S(2)}, u32[]{:S(2)}) collective-permute-start(bf16[16,64,128]{2,1,0:T(8,128)(2,1)S(1)} %fusion.76), channel_id=1, source_target_pairs={{8,0},{9,1},{10,2},{11,3},{12,4},{13,5},{14,6},{15,7},{16,8},{17,9... | collective-permute-start | bytes 786440 | tf_op jit(solution)/shard_map/ppermute | solution.py:32
  135.4 22.0 %collective-permute-start.8 = (bf16[16,64,128]{2,1,0:T(8,128)(2,1)S(1)}, bf16[16,64,128]{2,1,0:T(8,128)(2,1)S(1)}, u32[]{:S(2)}, u32[]{:S(2)}) collective-permute-start(bf16[16,64,128]{2,1,0:T(8,128)(2,1)S(1)} %fusion.51), channel_id=1, source_target_pairs={{0,16},{1,17},{2,18},{3,19},{4,20},{5,21},{6,22},{7,23},{8,24},{9,... | collective-permute-start | bytes 786440 | tf_op jit(solution)/shard_map/ppermute | solution.py:32
  152.1 20.0 %collective-permute-start.17 = (bf16[16,64,128]{2,1,0:T(8,128)(2,1)S(1)}, bf16[16,64,128]{2,1,0:T(8,128)(2,1)S(1)}, u32[]{:S(2)}, u32[]{:S(2)}) collective-permute-start(bf16[16,64,128]{2,1,0:T(8,128)(2,1)S(1)} %fusion.59), channel_id=1, source_target_pairs={{16,0},{17,1},{18,2},{19,3},{20,4},{21,5},{22,6},{23,7},{24,8},{25... | collective-permute-start | bytes 786440 | tf_op jit(solution)/shard_map/ppermute | solution.py:32
  188.2 14.2 %collective-permute-start.18 = (bf16[256,1024]{1,0:T(8,128)(2,1)S(1)}, bf16[256,1024]{1,0:T(8,128)(2,1)S(1)}, u32[]{:S(2)}, u32[]{:S(2)}) collective-permute-start(bf16[256,1024]{1,0:T(8,128)(2,1)S(1)} %convolution_convert_fusion), channel_id=1, source_target_pairs={{0,1},{1,0},{2,3},{3,2},{4,5},{5,4},{6,7},{7,6},{8,9},{9,8},{10,11... | collective-permute-start | bytes 1572872 | tf_op jit(solution)/shard_map/ppermute | solution.py:113
  190.2 12.2 %collective-permute-start.28 = (f32[256]{0:T(256)S(1)}, f32[256]{0:T(256)S(1)}, u32[]{:S(2)}, u32[]{:S(2)}) collective-permute-start(f32[256]{0:T(256)S(1)} %fusion.80), channel_id=1, source_target_pairs={{0,1},{1,0},{2,3},{3,2},{4,5},{5,4},{6,7},{7,6},{8,9},{9,8},{10,11... | collective-permute-start | bytes 3080 | tf_op jit(solution)/shard_map/ppermute | solution.py:113
  202.7 16.6 %collective-permute-start.20 = (bf16[256,1024]{1,0:T(8,128)(2,1)S(1)}, bf16[256,1024]{1,0:T(8,128)(2,1)S(1)}, u32[]{:S(2)}, u32[]{:S(2)}) collective-permute-start(bf16[256,1024]{1,0:T(8,128)(2,1)S(1)} %fusion.6), channel_id=1, source_target_pairs={{0,2},{1,3},{2,0},{3,1},{4,6},{5,7},{6,4},{7,5},{8,10},{9,11},{10,... | collective-permute-start | bytes 1572872 | tf_op jit(solution)/shard_map/ppermute | solution.py:113
  204.6 14.7 %collective-permute-start.21 = (f32[256]{0:T(256)S(1)}, f32[256]{0:T(256)S(1)}, u32[]{:S(2)}, u32[]{:S(2)}) collective-permute-start(f32[256]{0:T(256)S(1)} %get-tuple-element.28), channel_id=1, source_target_pairs={{0,2},{1,3},{2,0},{3,1},{4,6},{5,7},{6,4},{7,5},{8,10},{9,11},{10,... | collective-permute-start | bytes 3080 | tf_op jit(solution)/shard_map/ppermute | solution.py:113
  209.5 9.9 %collective-permute-start.29 = (f32[256]{0:T(256)S(1)}, f32[256]{0:T(256)S(1)}, u32[]{:S(2)}, u32[]{:S(2)}) collective-permute-start(f32[256]{0:T(256)S(1)} %get-tuple-element.25), channel_id=1, source_target_pairs={{0,2},{1,3},{2,0},{3,1},{4,6},{5,7},{6,4},{7,5},{8,10},{9,11},{10,... | collective-permute-start | bytes 3080 | tf_op jit(solution)/shard_map/ppermute | solution.py:113
  219.6 19.2 %collective-permute-start.22 = (bf16[256,1024]{1,0:T(8,128)(2,1)S(1)}, bf16[256,1024]{1,0:T(8,128)(2,1)S(1)}, u32[]{:S(2)}, u32[]{:S(2)}) collective-permute-start(bf16[256,1024]{1,0:T(8,128)(2,1)S(1)} %fusion.10), channel_id=1, source_target_pairs={{0,4},{1,5},{2,6},{3,7},{4,0},{5,1},{6,2},{7,3},{8,12},{9,13},{10,... | collective-permute-start | bytes 1572872 | tf_op jit(solution)/shard_map/ppermute | solution.py:113
  226.8 9.8 %collective-permute-start.23 = (f32[256]{0:T(256)S(1)}, f32[256]{0:T(256)S(1)}, u32[]{:S(2)}, u32[]{:S(2)}) collective-permute-start(f32[256]{0:T(256)S(1)} %get-tuple-element.24), channel_id=1, source_target_pairs={{0,4},{1,5},{2,6},{3,7},{4,0},{5,1},{6,2},{7,3},{8,12},{9,13},{10,... | collective-permute-start | bytes 3080 | tf_op jit(solution)/shard_map/ppermute | solution.py:113
  229.4 9.4 %collective-permute-start.30 = (f32[256]{0:T(256)S(1)}, f32[256]{0:T(256)S(1)}, u32[]{:S(2)}, u32[]{:S(2)}) collective-permute-start(f32[256]{0:T(256)S(1)} %get-tuple-element.21), channel_id=1, source_target_pairs={{0,4},{1,5},{2,6},{3,7},{4,0},{5,1},{6,2},{7,3},{8,12},{9,13},{10,... | collective-permute-start | bytes 3080 | tf_op jit(solution)/shard_map/ppermute | solution.py:113
  239.1 58.0 %collective-permute-start.24 = (bf16[256,1024]{1,0:T(8,128)(2,1)S(1)}, bf16[256,1024]{1,0:T(8,128)(2,1)S(1)}, u32[]{:S(2)}, u32[]{:S(2)}) collective-permute-start(bf16[256,1024]{1,0:T(8,128)(2,1)S(1)} %fusion.14), channel_id=1, source_target_pairs={{0,8},{1,9},{2,10},{3,11},{4,12},{5,13},{6,14},{7,15},{8,0},{9,1},... | collective-permute-start | bytes 1572872 | tf_op jit(solution)/shard_map/ppermute | solution.py:113
  254.7 42.3 %collective-permute-start.25 = (f32[256]{0:T(256)S(1)}, f32[256]{0:T(256)S(1)}, u32[]{:S(2)}, u32[]{:S(2)}) collective-permute-start(f32[256]{0:T(256)S(1)} %get-tuple-element.20), channel_id=1, source_target_pairs={{0,8},{1,9},{2,10},{3,11},{4,12},{5,13},{6,14},{7,15},{8,0},{9,1},... | collective-permute-start | bytes 3080 | tf_op jit(solution)/shard_map/ppermute | solution.py:113
  256.6 40.4 %collective-permute-start.31 = (f32[256]{0:T(256)S(1)}, f32[256]{0:T(256)S(1)}, u32[]{:S(2)}, u32[]{:S(2)}) collective-permute-start(f32[256]{0:T(256)S(1)} %get-tuple-element.17), channel_id=1, source_target_pairs={{0,8},{1,9},{2,10},{3,11},{4,12},{5,13},{6,14},{7,15},{8,0},{9,1},... | collective-permute-start | bytes 3080 | tf_op jit(solution)/shard_map/ppermute | solution.py:113
  297.3 28.2 %collective-permute-start.26 = (bf16[256,1024]{1,0:T(8,128)(2,1)S(1)}, bf16[256,1024]{1,0:T(8,128)(2,1)S(1)}, u32[]{:S(2)}, u32[]{:S(2)}) collective-permute-start(bf16[256,1024]{1,0:T(8,128)(2,1)S(1)} %fusion.18), channel_id=1, source_target_pairs={{0,16},{1,17},{2,18},{3,19},{4,20},{5,21},{6,22},{7,23},{8,24},{9,... | collective-permute-start | bytes 1572872 | tf_op jit(solution)/shard_map/ppermute | solution.py:113
  299.3 26.2 %collective-permute-start.27 = (f32[256]{0:T(256)S(1)}, f32[256]{0:T(256)S(1)}, u32[]{:S(2)}, u32[]{:S(2)}) collective-permute-start(f32[256]{0:T(256)S(1)} %get-tuple-element.16), channel_id=1, source_target_pairs={{0,16},{1,17},{2,18},{3,19},{4,20},{5,21},{6,22},{7,23},{8,24},{9,... | collective-permute-start | bytes 3080 | tf_op jit(solution)/shard_map/ppermute | solution.py:113
  307.1 18.4 %collective-permute-start.32 = (f32[256]{0:T(256)S(1)}, f32[256]{0:T(256)S(1)}, u32[]{:S(2)}, u32[]{:S(2)}) collective-permute-start(f32[256]{0:T(256)S(1)} %get-tuple-element.13), channel_id=1, source_target_pairs={{0,16},{1,17},{2,18},{3,19},{4,20},{5,21},{6,22},{7,23},{8,24},{9,... | collective-permute-start | bytes 3080 | tf_op jit(solution)/shard_map/ppermute | solution.py:113
  (34 other events, 517.4 us)
Sparse Core Ops, SparseCore 0:
  30.8 46.0 all-gather.1

commit v3 on v2

--- a/solution.py
+++ b/solution.py
@@ -101,16 +101,32 @@
     return (top, total, summed)
 
 
-def butterfly_pool(local, axis):
+def xor_exchange(value, axis, bit):
+    count = lax.axis_size(axis)
+    return lax.ppermute(value, axis, [(q, q ^ bit) for q in range(count)])
+
+
+def reduce_pool(local, axis, scatter_rounds):
     count = lax.axis_size(axis)
     assert count & (count - 1) == 0
     place = lax.axis_index(axis)
     state = local
     bit = 1
+    for unused_round in range(scatter_rounds):
+        if bit >= count:
+            break
+        half = state[0].shape[0] // 2
+        upper = (place & bit) != 0
+        keep = jax.tree.map(lambda a: jnp.where(upper, a[half:], a[:half]), state)
+        send = jax.tree.map(lambda a: jnp.where(upper, a[:half], a[half:]), state)
+        received = xor_exchange((send[0], send[1], send[2].astype(jnp.bfloat16)), axis, bit)
+        other = (received[0], received[1], received[2].astype(jnp.float32))
+        state = pool_combine(keep, other)
+        bit *= 2
+    gather_bits = []
     while bit < count:
         sent = (state[0], state[1], state[2].astype(jnp.bfloat16))
-        perm = [(q, q ^ bit) for q in range(count)]
-        received = lax.ppermute(sent, axis, perm)
+        received = xor_exchange(sent, axis, bit)
         own = (sent[0], sent[1], sent[2].astype(jnp.float32))
         other = (received[0], received[1], received[2].astype(jnp.float32))
         is_low = (place & bit) == 0
@@ -118,7 +134,20 @@
         hi = jax.tree.map(lambda a, b: jnp.where(is_low, b, a), own, other)
         state = pool_combine(lo, hi)
         bit *= 2
-    return state
+    rows = (state[2] / state[1][:, None]).astype(jnp.bfloat16)
+    bit = 1
+    while bit * 2 <= count and len(gather_bits) < scatter_rounds:
+        gather_bits.append(bit)
+        bit *= 2
+    for bit in reversed(gather_bits):
+        received = xor_exchange(rows, axis, bit)
+        upper = (place & bit) != 0
+        rows = jnp.where(
+            upper,
+            jnp.concatenate([received, rows], axis=0),
+            jnp.concatenate([rows, received], axis=0),
+        )
+    return rows
 
 
 def body(
@@ -187,10 +216,7 @@
     weighted_sum = jnp.dot(
         prob_values.astype(jnp.bfloat16), encoded, preferred_element_type=jnp.float32
     )
-    unused_item, total_weight, total_sum = butterfly_pool(
-        (local_top, weight_sum, weighted_sum), "seq"
-    )
-    pooled = (total_sum / total_weight[:, None]).astype(jnp.bfloat16)
+    pooled = reduce_pool((local_top, weight_sum, weighted_sum), "seq", 3)
     return (encoded[None], pooled[None])
 
 

time: 335 us -> 299 us (0.89)
  the two profiles are of different devices: /device:TPU:4 before, /device:TPU:6 now
where the time goes in v3:
time: 299 us; the launch traced here: 297 us
  starting transfers between devices  168 us (56%)
  waiting for transfers between devices  60.5 us (20%)
  local copies, waits for them, and re-layouts  23 us (8%)
  other arithmetic  20.3 us (7%)
  between operations  16 us (5%)
  matrix products  9.17 us (3%)
    ppermute x18, starting transfers between devices, exclusive_scan(): received = lax.ppermute(sent, axis, perm)  97.4 us
    ppermute x18, starting transfers between devices, xor_exchange(): return lax.ppermute(value, axis, [(q, q ^ bit) for q in range(count)])  70.5 us
    ppermute x18, waiting for transfers between devices, exclusive_scan(): received = lax.ppermute(sent, axis, perm)  32.8 us
    ppermute x18, waiting for transfers between devices, xor_exchange(): return lax.ppermute(value, axis, [(q, q ^ bit) for q in range(count)])  27.7 us
    rev x1, local copies, waits for them, and re-layouts, body(): backward_out = apply_state(backward_records, backward_in)[::-1]  7.5 us
  transfers between devices with their start and end apart: 37, of which 10 were waited for; matrix products, arithmetic and copies ran while one was open for 14% of the time, Pallas kernels for 0%

profile of v3, /device:TPU:6, one launch (start us, length us, event | category | flops | bytes accessed | tf_op | source)
XLA Modules:
  0.0 297.0 jit_solution(1254484791659657768)
XLA Ops:
  15.4 3.5 %collective-permute-start.4 = (bf16[16,64,128]{2,1,0:T(8,128)(2,1)}, bf16[16,64,128]{2,1,0:T(8,128)(2,1)S(1)}, u32[]{:S(2)}, u32[]{:S(2)}) collective-permute-start(bf16[16,64,128]{2,1,0:T(8,128)(2,1)} %get-tuple-element.39), channel_id=1, source_target_pairs={{0,1},{1,2},{2,3},{3,4},{4,5},{5,6},{6,7},{7,8},{8,9},{9,10},{10,1... | collective-permute-start | bytes 786440 | tf_op jit(solution)/shard_map/ppermute | solution.py:32
  18.9 4.0 %collective-permute-start = (f32[16]{0:T(128)}, f32[16]{0:T(128)}, u32[]{:S(2)}, u32[]{:S(2)}) collective-permute-start(f32[16]{0:T(128)} %get-tuple-element.5), channel_id=1, source_target_pairs={{0,1},{1,2},{2,3},{3,4},{4,5},{5,6},{6,7},{7,8},{8,9},{9,10},{10,1... | collective-permute-start | bytes 200 | tf_op jit(solution)/shard_map/ppermute | solution.py:32
  36.9 2.0 copy.47
  41.6 1.9 convolution_bitcast_fusion.3
  45.9 6.6 %collective-permute-start.1 = (f32[16]{0:T(128)S(1)}, f32[16]{0:T(128)S(1)}, u32[]{:S(2)}, u32[]{:S(2)}) collective-permute-start(f32[16]{0:T(128)S(1)} %get-tuple-element.38), channel_id=1, source_target_pairs={{0,2},{1,3},{2,4},{3,5},{4,6},{5,7},{6,8},{7,9},{8,10},{9,11},{10,... | collective-permute-start | bytes 200 | tf_op jit(solution)/shard_map/ppermute | solution.py:32
  54.6 10.6 %collective-permute-start.2 = (f32[16]{0:T(128)S(1)}, f32[16]{0:T(128)S(1)}, u32[]{:S(2)}, u32[]{:S(2)}) collective-permute-start(f32[16]{0:T(128)S(1)} %get-tuple-element.34), channel_id=1, source_target_pairs={{0,4},{1,5},{2,6},{3,7},{4,8},{5,9},{6,10},{7,11},{8,12},{9,13},{1... | collective-permute-start | bytes 200 | tf_op jit(solution)/shard_map/ppermute | solution.py:32
  66.6 12.2 %collective-permute-start.3 = (f32[16]{0:T(128)S(1)}, f32[16]{0:T(128)S(1)}, u32[]{:S(2)}, u32[]{:S(2)}) collective-permute-start(f32[16]{0:T(128)S(1)} %get-tuple-element.32), channel_id=1, source_target_pairs={{0,8},{1,9},{2,10},{3,11},{4,12},{5,13},{6,14},{7,15},{8,16},{9,17... | collective-permute-start | bytes 200 | tf_op jit(solution)/shard_map/ppermute | solution.py:32
  78.9 2.0 collective-permute-start.5
  85.1 15.7 %collective-permute-start.6 = (bf16[16,64,128]{2,1,0:T(8,128)(2,1)S(1)}, bf16[16,64,128]{2,1,0:T(8,128)(2,1)S(1)}, u32[]{:S(2)}, u32[]{:S(2)}) collective-permute-start(bf16[16,64,128]{2,1,0:T(8,128)(2,1)S(1)} %get-tuple-element.35), channel_id=1, source_target_pairs={{0,4},{1,5},{2,6},{3,7},{4,8},{5,9},{6,10},{7,11},{8,12},{9,13},{1... | collective-permute-start | bytes 786440 | tf_op jit(solution)/shard_map/ppermute | solution.py:32
  103.2 13.9 %collective-permute-done.6 = bf16[16,64,128]{2,1,0:T(8,128)(2,1)S(1)} collective-permute-done((bf16[16,64,128]{2,1,0:T(8,128)(2,1)S(1)}, bf16[16,64,128]{2,1,0:T(8,128)(2,1)S(1)}, u32[]{:S(2)}, u32[]{:S(2)}) %collective-permute-start.6) | collective-permute-done | bytes 262176 | tf_op jit(solution)/shard_map/ppermute | solution.py:32
  117.3 15.2 %collective-permute-start.7 = (bf16[16,64,128]{2,1,0:T(8,128)(2,1)S(1)}, bf16[16,64,128]{2,1,0:T(8,128)(2,1)S(1)}, u32[]{:S(2)}, u32[]{:S(2)}) collective-permute-start(bf16[16,64,128]{2,1,0:T(8,128)(2,1)S(1)} %fusion.56), channel_id=1, source_target_pairs={{0,8},{1,9},{2,10},{3,11},{4,12},{5,13},{6,14},{7,15},{8,16},{9,17... | collective-permute-start | bytes 786440 | tf_op jit(solution)/shard_map/ppermute | solution.py:32
  136.6 15.8 %collective-permute-start.8 = (bf16[16,64,128]{2,1,0:T(8,128)(2,1)S(1)}, bf16[16,64,128]{2,1,0:T(8,128)(2,1)S(1)}, u32[]{:S(2)}, u32[]{:S(2)}) collective-permute-start(bf16[16,64,128]{2,1,0:T(8,128)(2,1)S(1)} %fusion.30), channel_id=1, source_target_pairs={{0,16},{1,17},{2,18},{3,19},{4,20},{5,21},{6,22},{7,23},{8,24},{9,... | collective-permute-start | bytes 786440 | tf_op jit(solution)/shard_map/ppermute | solution.py:32
  154.8 3.8 %collective-permute-done.8 = bf16[16,64,128]{2,1,0:T(8,128)(2,1)S(1)} collective-permute-done((bf16[16,64,128]{2,1,0:T(8,128)(2,1)S(1)}, bf16[16,64,128]{2,1,0:T(8,128)(2,1)S(1)}, u32[]{:S(2)}, u32[]{:S(2)}) %collective-permute-start.8) | collective-permute-done | bytes 262176 | tf_op jit(solution)/shard_map/ppermute | solution.py:32
  160.2 13.1 %collective-permute-done.17 = bf16[16,64,128]{2,1,0:T(8,128)(2,1)S(1)} collective-permute-done((bf16[16,64,128]{2,1,0:T(8,128)(2,1)S(1)}, bf16[16,64,128]{2,1,0:T(8,128)(2,1)S(1)}, u32[]{:S(2)}, u32[]{:S(2)}) %collective-permute-start.17) | collective-permute-done | bytes 262176 | tf_op jit(solution)/shard_map/ppermute | solution.py:32
  176.8 7.5 %rev.19 = f32[256,1024]{0,1:T(8,128)S(1)} reverse(f32[256,1024]{0,1:T(8,128)} %bitcast.199), dimensions={0} | reverse | bytes 2097152 | tf_op jit(solution)/shard_map/rev | solution.py:195
  186.2 2.3 convolution_convert_fusion
  189.1 1.9 collective-permute-start.28
  191.0 3.9 %collective-permute-start.18 = (f32[128]{0:T(128)S(1)}, f32[128]{0:T(128)S(1)}, u32[]{:S(2)}, u32[]{:S(2)}) collective-permute-start(f32[128]{0:T(128)S(1)} %broadcast_select_fusion.18), channel_id=1, source_target_pairs={{0,1},{1,0},{2,3},{3,2},{4,5},{5,4},{6,7},{7,6},{8,9},{9,8},{10,11... | collective-permute-start | bytes 1544 | tf_op jit(solution)/shard_map/ppermute | solution.py:106
  198.5 4.8 %collective-permute-start.29 = (f32[64]{0:T(128)S(1)}, f32[64]{0:T(128)S(1)}, u32[]{:S(2)}, u32[]{:S(2)}) collective-permute-start(f32[64]{0:T(128)S(1)} %broadcast_select_fusion.12), channel_id=1, source_target_pairs={{0,2},{1,3},{2,0},{3,1},{4,6},{5,7},{6,4},{7,5},{8,10},{9,11},{10,... | collective-permute-start | bytes 776 | tf_op jit(solution)/shard_map/ppermute | solution.py:106
  203.4 3.9 %collective-permute-start.19 = (bf16[128,1024]{1,0:T(8,128)(2,1)S(1)}, bf16[128,1024]{1,0:T(8,128)(2,1)S(1)}, u32[]{:S(2)}, u32[]{:S(2)}) collective-permute-start(bf16[128,1024]{1,0:T(8,128)(2,1)S(1)} %select_convert_fusion), channel_id=1, source_target_pairs={{0,1},{1,0},{2,3},{3,2},{4,5},{5,4},{6,7},{7,6},{8,9},{9,8},{10,11... | collective-permute-start | bytes 786440 | tf_op jit(solution)/shard_map/ppermute | solution.py:106
  207.5 6.5 %collective-permute-start.22 = (f32[32]{0:T(128)S(1)}, f32[32]{0:T(128)S(1)}, u32[]{:S(2)}, u32[]{:S(2)}) collective-permute-start(f32[32]{0:T(128)S(1)} %broadcast_select_fusion.10), channel_id=1, source_target_pairs={{0,4},{1,5},{2,6},{3,7},{4,0},{5,1},{6,2},{7,3},{8,12},{9,13},{10,... | collective-permute-start | bytes 392 | tf_op jit(solution)/shard_map/ppermute | solution.py:106
  214.2 4.4 %collective-permute-start.21 = (bf16[64,1024]{1,0:T(8,128)(2,1)S(1)}, bf16[64,1024]{1,0:T(8,128)(2,1)S(1)}, u32[]{:S(2)}, u32[]{:S(2)}) collective-permute-start(bf16[64,1024]{1,0:T(8,128)(2,1)S(1)} %select_convert_fusion.1), channel_id=1, source_target_pairs={{0,2},{1,3},{2,0},{3,1},{4,6},{5,7},{6,4},{7,5},{8,10},{9,11},{10,... | collective-permute-start | bytes 393224 | tf_op jit(solution)/shard_map/ppermute | solution.py:106
  218.7 4.1 %collective-permute-start.30 = (f32[32]{0:T(128)S(1)}, f32[32]{0:T(128)S(1)}, u32[]{:S(2)}, u32[]{:S(2)}) collective-permute-start(f32[32]{0:T(128)S(1)} %broadcast_select_fusion.8), channel_id=1, source_target_pairs={{0,4},{1,5},{2,6},{3,7},{4,0},{5,1},{6,2},{7,3},{8,12},{9,13},{10,... | collective-permute-start | bytes 392 | tf_op jit(solution)/shard_map/ppermute | solution.py:106
  223.0 5.6 %collective-permute-start.23 = (bf16[32,1024]{1,0:T(8,128)(2,1)S(1)}, bf16[32,1024]{1,0:T(8,128)(2,1)S(1)}, u32[]{:S(2)}, u32[]{:S(2)}) collective-permute-start(bf16[32,1024]{1,0:T(8,128)(2,1)S(1)} %select_convert_fusion.2), channel_id=1, source_target_pairs={{0,4},{1,5},{2,6},{3,7},{4,0},{5,1},{6,2},{7,3},{8,12},{9,13},{10,... | collective-permute-start | bytes 196616 | tf_op jit(solution)/shard_map/ppermute | solution.py:106
  228.7 6.0 %collective-permute-start.25 = (f32[32]{0:T(128)S(1)}, f32[32]{0:T(128)S(1)}, u32[]{:S(2)}, u32[]{:S(2)}) collective-permute-start(f32[32]{0:T(128)S(1)} %get-tuple-element.20), channel_id=1, source_target_pairs={{0,8},{1,9},{2,10},{3,11},{4,12},{5,13},{6,14},{7,15},{8,0},{9,1},... | collective-permute-start | bytes 392 | tf_op jit(solution)/shard_map/ppermute | solution.py:106
  236.7 4.8 %collective-permute-start.24 = (bf16[32,1024]{1,0:T(8,128)(2,1)S(1)}, bf16[32,1024]{1,0:T(8,128)(2,1)S(1)}, u32[]{:S(2)}, u32[]{:S(2)}) collective-permute-start(bf16[32,1024]{1,0:T(8,128)(2,1)S(1)} %add_convert_fusion.4), channel_id=1, source_target_pairs={{0,8},{1,9},{2,10},{3,11},{4,12},{5,13},{6,14},{7,15},{8,0},{9,1},... | collective-permute-start | bytes 196616 | tf_op jit(solution)/shard_map/ppermute | solution.py:106
  243.5 7.8 %collective-permute-start.32 = (f32[32]{0:T(128)S(1)}, f32[32]{0:T(128)S(1)}, u32[]{:S(2)}, u32[]{:S(2)}) collective-permute-start(f32[32]{0:T(128)S(1)} %get-tuple-element.13), channel_id=1, source_target_pairs={{0,16},{1,17},{2,18},{3,19},{4,20},{5,21},{6,22},{7,23},{8,24},{9,... | collective-permute-start | bytes 392 | tf_op jit(solution)/shard_map/ppermute | solution.py:106
  253.4 8.1 %collective-permute-done.26 = bf16[32,1024]{1,0:T(8,128)(2,1)S(1)} collective-permute-done((bf16[32,1024]{1,0:T(8,128)(2,1)S(1)}, bf16[32,1024]{1,0:T(8,128)(2,1)S(1)}, u32[]{:S(2)}, u32[]{:S(2)}) %collective-permute-start.26) | collective-permute-done | bytes 65568 | tf_op jit(solution)/shard_map/ppermute | solution.py:106
  261.6 5.2 %collective-permute-start.33 = (bf16[32,1024]{1,0:T(8,128)(2,1)S(1)}, bf16[32,1024]{1,0:T(8,128)(2,1)S(1)}, u32[]{:S(2)}, u32[]{:S(2)}) collective-permute-start(bf16[32,1024]{1,0:T(8,128)(2,1)S(1)} %fusion.72), channel_id=1, source_target_pairs={{0,4},{1,5},{2,6},{3,7},{4,0},{5,1},{6,2},{7,3},{8,12},{9,13},{10,... | collective-permute-start | bytes 196616 | tf_op jit(solution)/shard_map/ppermute | solution.py:106
  266.8 6.3 %collective-permute-done.33 = bf16[32,1024]{1,0:T(8,128)(2,1)S(1)} collective-permute-done((bf16[32,1024]{1,0:T(8,128)(2,1)S(1)}, bf16[32,1024]{1,0:T(8,128)(2,1)S(1)}, u32[]{:S(2)}, u32[]{:S(2)}) %collective-permute-start.33) | collective-permute-done | bytes 65568 | tf_op jit(solution)/shard_map/ppermute | solution.py:106
  275.0 5.8 %collective-permute-done.34 = bf16[64,1024]{1,0:T(8,128)(2,1)S(1)} collective-permute-done((bf16[64,1024]{1,0:T(8,128)(2,1)S(1)}, bf16[64,1024]{1,0:T(8,128)(2,1)S(1)}, u32[]{:S(2)}, u32[]{:S(2)}) %collective-permute-start.34) | collective-permute-done | bytes 131104 | tf_op jit(solution)/shard_map/ppermute | solution.py:106
  282.8 6.3 %collective-permute-done.35 = bf16[128,1024]{1,0:T(8,128)(2,1)S(1)} collective-permute-done((bf16[128,1024]{1,0:T(8,128)(2,1)S(1)}, bf16[128,1024]{1,0:T(8,128)(2,1)S(1)}, u32[]{:S(2)}, u32[]{:S(2)}) %collective-permute-start.35) | collective-permute-done | bytes 262176 | tf_op jit(solution)/shard_map/ppermute | solution.py:106
  (206 shorter events, 65.2 us)
Async XLA Ops:
  7.2 179.0 %all-gather.2.cloned.1.call-start = ((), (), s32[]{:S(2)}) async-start(), calls=%async_computation | async-start | bytes 2228224 | tf_op jit(solution)/shard_map/all_gather | solution.py:205
  15.4 63.4 %collective-permute-start.4 = (bf16[16,64,128]{2,1,0:T(8,128)(2,1)}, bf16[16,64,128]{2,1,0:T(8,128)(2,1)S(1)}, u32[]{:S(2)}, u32[]{:S(2)}) collective-permute-start(bf16[16,64,128]{2,1,0:T(8,128)(2,1)} %get-tuple-element.39), channel_id=1, source_target_pairs={{0,1},{1,2},{2,3},{3,4},{4,5},{5,6},{6,7},{7,8},{8,9},{9,10},{10,1... | collective-permute-start | bytes 786440 | tf_op jit(solution)/shard_map/ppermute | solution.py:32
  18.9 26.4 %collective-permute-start = (f32[16]{0:T(128)}, f32[16]{0:T(128)}, u32[]{:S(2)}, u32[]{:S(2)}) collective-permute-start(f32[16]{0:T(128)} %get-tuple-element.5), channel_id=1, source_target_pairs={{0,1},{1,2},{2,3},{3,4},{4,5},{5,6},{6,7},{7,8},{8,9},{9,10},{10,1... | collective-permute-start | bytes 200 | tf_op jit(solution)/shard_map/ppermute | solution.py:32
  28.0 54.3 %collective-permute-start.13 = (bf16[16,64,128]{2,1,0:T(8,128)(2,1)}, bf16[16,64,128]{2,1,0:T(8,128)(2,1)}, u32[]{:S(2)}, u32[]{:S(2)}) collective-permute-start(bf16[16,64,128]{2,1,0:T(8,128)(2,1)} %get-tuple-element.49), channel_id=1, source_target_pairs={{1,0},{2,1},{3,2},{4,3},{5,4},{6,5},{7,6},{8,7},{9,8},{10,9},{11,1... | collective-permute-start | bytes 786440 | tf_op jit(solution)/shard_map/ppermute | solution.py:32
  29.3 23.3 %collective-permute-start.9 = (f32[16]{0:T(128)}, f32[16]{0:T(128)}, u32[]{:S(2)}, u32[]{:S(2)}) collective-permute-start(f32[16]{0:T(128)} %get-tuple-element.9), channel_id=1, source_target_pairs={{1,0},{2,1},{3,2},{4,3},{5,4},{6,5},{7,6},{8,7},{9,8},{10,9},{11,1... | collective-permute-start | bytes 200 | tf_op jit(solution)/shard_map/ppermute | solution.py:32
  45.9 8.6 %collective-permute-start.1 = (f32[16]{0:T(128)S(1)}, f32[16]{0:T(128)S(1)}, u32[]{:S(2)}, u32[]{:S(2)}) collective-permute-start(f32[16]{0:T(128)S(1)} %get-tuple-element.38), channel_id=1, source_target_pairs={{0,2},{1,3},{2,4},{3,5},{4,6},{5,7},{6,8},{7,9},{8,10},{9,11},{10,... | collective-permute-start | bytes 200 | tf_op jit(solution)/shard_map/ppermute | solution.py:32
  53.3 12.0 %collective-permute-start.10 = (f32[16]{0:T(128)S(1)}, f32[16]{0:T(128)S(1)}, u32[]{:S(2)}, u32[]{:S(2)}) collective-permute-start(f32[16]{0:T(128)S(1)} %get-tuple-element.48), channel_id=1, source_target_pairs={{2,0},{3,1},{4,2},{5,3},{6,4},{7,5},{8,6},{9,7},{10,8},{11,9},{12,... | collective-permute-start | bytes 200 | tf_op jit(solution)/shard_map/ppermute | solution.py:32
  54.6 12.0 %collective-permute-start.2 = (f32[16]{0:T(128)S(1)}, f32[16]{0:T(128)S(1)}, u32[]{:S(2)}, u32[]{:S(2)}) collective-permute-start(f32[16]{0:T(128)S(1)} %get-tuple-element.34), channel_id=1, source_target_pairs={{0,4},{1,5},{2,6},{3,7},{4,8},{5,9},{6,10},{7,11},{8,12},{9,13},{1... | collective-permute-start | bytes 200 | tf_op jit(solution)/shard_map/ppermute | solution.py:32
  65.2 15.7 %collective-permute-start.11 = (f32[16]{0:T(128)S(1)}, f32[16]{0:T(128)S(1)}, u32[]{:S(2)}, u32[]{:S(2)}) collective-permute-start(f32[16]{0:T(128)S(1)} %get-tuple-element.44), channel_id=1, source_target_pairs={{4,0},{5,1},{6,2},{7,3},{8,4},{9,5},{10,6},{11,7},{12,8},{13,9},{1... | collective-permute-start | bytes 200 | tf_op jit(solution)/shard_map/ppermute | solution.py:32
  66.6 65.9 %collective-permute-start.3 = (f32[16]{0:T(128)S(1)}, f32[16]{0:T(128)S(1)}, u32[]{:S(2)}, u32[]{:S(2)}) collective-permute-start(f32[16]{0:T(128)S(1)} %get-tuple-element.32), channel_id=1, source_target_pairs={{0,8},{1,9},{2,10},{3,11},{4,12},{5,13},{6,14},{7,15},{8,16},{9,17... | collective-permute-start | bytes 200 | tf_op jit(solution)/shard_map/ppermute | solution.py:32
  81.0 71.4 %collective-permute-start.12 = (f32[16]{0:T(128)S(1)}, f32[16]{0:T(128)S(1)}, u32[]{:S(2)}, u32[]{:S(2)}) collective-permute-start(f32[16]{0:T(128)S(1)} %get-tuple-element.42), channel_id=1, source_target_pairs={{8,0},{9,1},{10,2},{11,3},{12,4},{13,5},{14,6},{15,7},{16,8},{17,9... | collective-permute-start | bytes 200 | tf_op jit(solution)/shard_map/ppermute | solution.py:32
  83.4 17.3 %collective-permute-start.14 = (bf16[16,64,128]{2,1,0:T(8,128)(2,1)S(1)}, bf16[16,64,128]{2,1,0:T(8,128)(2,1)S(1)}, u32[]{:S(2)}, u32[]{:S(2)}) collective-permute-start(bf16[16,64,128]{2,1,0:T(8,128)(2,1)S(1)} %fusion.55), channel_id=1, source_target_pairs={{2,0},{3,1},{4,2},{5,3},{6,4},{7,5},{8,6},{9,7},{10,8},{11,9},{12,... | collective-permute-start | bytes 786440 | tf_op jit(solution)/shard_map/ppermute | solution.py:32
  85.1 32.1 %collective-permute-start.6 = (bf16[16,64,128]{2,1,0:T(8,128)(2,1)S(1)}, bf16[16,64,128]{2,1,0:T(8,128)(2,1)S(1)}, u32[]{:S(2)}, u32[]{:S(2)}) collective-permute-start(bf16[16,64,128]{2,1,0:T(8,128)(2,1)S(1)} %get-tuple-element.35), channel_id=1, source_target_pairs={{0,4},{1,5},{2,6},{3,7},{4,8},{5,9},{6,10},{7,11},{8,12},{9,13},{1... | collective-permute-start | bytes 786440 | tf_op jit(solution)/shard_map/ppermute | solution.py:32
  101.9 31.2 %collective-permute-start.15 = (bf16[16,64,128]{2,1,0:T(8,128)(2,1)S(1)}, bf16[16,64,128]{2,1,0:T(8,128)(2,1)S(1)}, u32[]{:S(2)}, u32[]{:S(2)}) collective-permute-start(bf16[16,64,128]{2,1,0:T(8,128)(2,1)S(1)} %get-tuple-element.45), channel_id=1, source_target_pairs={{4,0},{5,1},{6,2},{7,3},{8,4},{9,5},{10,6},{11,7},{12,8},{13,9},{1... | collective-permute-start | bytes 786440 | tf_op jit(solution)/shard_map/ppermute | solution.py:32
  117.3 19.1 %collective-permute-start.7 = (bf16[16,64,128]{2,1,0:T(8,128)(2,1)S(1)}, bf16[16,64,128]{2,1,0:T(8,128)(2,1)S(1)}, u32[]{:S(2)}, u32[]{:S(2)}) collective-permute-start(bf16[16,64,128]{2,1,0:T(8,128)(2,1)S(1)} %fusion.56), channel_id=1, source_target_pairs={{0,8},{1,9},{2,10},{3,11},{4,12},{5,13},{6,14},{7,15},{8,16},{9,17... | collective-permute-start | bytes 786440 | tf_op jit(solution)/shard_map/ppermute | solution.py:32
  133.3 19.9 %collective-permute-start.16 = (bf16[16,64,128]{2,1,0:T(8,128)(2,1)S(1)}, bf16[16,64,128]{2,1,0:T(8,128)(2,1)S(1)}, u32[]{:S(2)}, u32[]{:S(2)}) collective-permute-start(bf16[16,64,128]{2,1,0:T(8,128)(2,1)S(1)} %fusion.54), channel_id=1, source_target_pairs={{8,0},{9,1},{10,2},{11,3},{12,4},{13,5},{14,6},{15,7},{16,8},{17,9... | collective-permute-start | bytes 786440 | tf_op jit(solution)/shard_map/ppermute | solution.py:32
  136.6 22.0 %collective-permute-start.8 = (bf16[16,64,128]{2,1,0:T(8,128)(2,1)S(1)}, bf16[16,64,128]{2,1,0:T(8,128)(2,1)S(1)}, u32[]{:S(2)}, u32[]{:S(2)}) collective-permute-start(bf16[16,64,128]{2,1,0:T(8,128)(2,1)S(1)} %fusion.30), channel_id=1, source_target_pairs={{0,16},{1,17},{2,18},{3,19},{4,20},{5,21},{6,22},{7,23},{8,24},{9,... | collective-permute-start | bytes 786440 | tf_op jit(solution)/shard_map/ppermute | solution.py:32
  153.3 19.9 %collective-permute-start.17 = (bf16[16,64,128]{2,1,0:T(8,128)(2,1)S(1)}, bf16[16,64,128]{2,1,0:T(8,128)(2,1)S(1)}, u32[]{:S(2)}, u32[]{:S(2)}) collective-permute-start(bf16[16,64,128]{2,1,0:T(8,128)(2,1)S(1)} %fusion.38), channel_id=1, source_target_pairs={{16,0},{17,1},{18,2},{19,3},{20,4},{21,5},{22,6},{23,7},{24,8},{25... | collective-permute-start | bytes 786440 | tf_op jit(solution)/shard_map/ppermute | solution.py:32
  196.5 10.8 %collective-permute-start.20 = (f32[64]{0:T(128)S(1)}, f32[64]{0:T(128)S(1)}, u32[]{:S(2)}, u32[]{:S(2)}) collective-permute-start(f32[64]{0:T(128)S(1)} %broadcast_select_fusion.14), channel_id=1, source_target_pairs={{0,2},{1,3},{2,0},{3,1},{4,6},{5,7},{6,4},{7,5},{8,10},{9,11},{10,... | collective-permute-start | bytes 776 | tf_op jit(solution)/shard_map/ppermute | solution.py:106
  198.5 8.8 %collective-permute-start.29 = (f32[64]{0:T(128)S(1)}, f32[64]{0:T(128)S(1)}, u32[]{:S(2)}, u32[]{:S(2)}) collective-permute-start(f32[64]{0:T(128)S(1)} %broadcast_select_fusion.12), channel_id=1, source_target_pairs={{0,2},{1,3},{2,0},{3,1},{4,6},{5,7},{6,4},{7,5},{8,10},{9,11},{10,... | collective-permute-start | bytes 776 | tf_op jit(solution)/shard_map/ppermute | solution.py:106
  203.4 10.6 %collective-permute-start.19 = (bf16[128,1024]{1,0:T(8,128)(2,1)S(1)}, bf16[128,1024]{1,0:T(8,128)(2,1)S(1)}, u32[]{:S(2)}, u32[]{:S(2)}) collective-permute-start(bf16[128,1024]{1,0:T(8,128)(2,1)S(1)} %select_convert_fusion), channel_id=1, source_target_pairs={{0,1},{1,0},{2,3},{3,2},{4,5},{5,4},{6,7},{7,6},{8,9},{9,8},{10,11... | collective-permute-start | bytes 786440 | tf_op jit(solution)/shard_map/ppermute | solution.py:106
  207.5 21.1 %collective-permute-start.22 = (f32[32]{0:T(128)S(1)}, f32[32]{0:T(128)S(1)}, u32[]{:S(2)}, u32[]{:S(2)}) collective-permute-start(f32[32]{0:T(128)S(1)} %broadcast_select_fusion.10), channel_id=1, source_target_pairs={{0,4},{1,5},{2,6},{3,7},{4,0},{5,1},{6,2},{7,3},{8,12},{9,13},{10,... | collective-permute-start | bytes 392 | tf_op jit(solution)/shard_map/ppermute | solution.py:106
  214.2 8.6 %collective-permute-start.21 = (bf16[64,1024]{1,0:T(8,128)(2,1)S(1)}, bf16[64,1024]{1,0:T(8,128)(2,1)S(1)}, u32[]{:S(2)}, u32[]{:S(2)}) collective-permute-start(bf16[64,1024]{1,0:T(8,128)(2,1)S(1)} %select_convert_fusion.1), channel_id=1, source_target_pairs={{0,2},{1,3},{2,0},{3,1},{4,6},{5,7},{6,4},{7,5},{8,10},{9,11},{10,... | collective-permute-start | bytes 393224 | tf_op jit(solution)/shard_map/ppermute | solution.py:106
  218.7 9.9 %collective-permute-start.30 = (f32[32]{0:T(128)S(1)}, f32[32]{0:T(128)S(1)}, u32[]{:S(2)}, u32[]{:S(2)}) collective-permute-start(f32[32]{0:T(128)S(1)} %broadcast_select_fusion.8), channel_id=1, source_target_pairs={{0,4},{1,5},{2,6},{3,7},{4,0},{5,1},{6,2},{7,3},{8,12},{9,13},{10,... | collective-permute-start | bytes 392 | tf_op jit(solution)/shard_map/ppermute | solution.py:106
  223.0 13.6 %collective-permute-start.23 = (bf16[32,1024]{1,0:T(8,128)(2,1)S(1)}, bf16[32,1024]{1,0:T(8,128)(2,1)S(1)}, u32[]{:S(2)}, u32[]{:S(2)}) collective-permute-start(bf16[32,1024]{1,0:T(8,128)(2,1)S(1)} %select_convert_fusion.2), channel_id=1, source_target_pairs={{0,4},{1,5},{2,6},{3,7},{4,0},{5,1},{6,2},{7,3},{8,12},{9,13},{10,... | collective-permute-start | bytes 196616 | tf_op jit(solution)/shard_map/ppermute | solution.py:106
  228.7 12.8 %collective-permute-start.25 = (f32[32]{0:T(128)S(1)}, f32[32]{0:T(128)S(1)}, u32[]{:S(2)}, u32[]{:S(2)}) collective-permute-start(f32[32]{0:T(128)S(1)} %get-tuple-element.20), channel_id=1, source_target_pairs={{0,8},{1,9},{2,10},{3,11},{4,12},{5,13},{6,14},{7,15},{8,0},{9,1},... | collective-permute-start | bytes 392 | tf_op jit(solution)/shard_map/ppermute | solution.py:106
  236.7 14.6 %collective-permute-start.24 = (bf16[32,1024]{1,0:T(8,128)(2,1)S(1)}, bf16[32,1024]{1,0:T(8,128)(2,1)S(1)}, u32[]{:S(2)}, u32[]{:S(2)}) collective-permute-start(bf16[32,1024]{1,0:T(8,128)(2,1)S(1)} %add_convert_fusion.4), channel_id=1, source_target_pairs={{0,8},{1,9},{2,10},{3,11},{4,12},{5,13},{6,14},{7,15},{8,0},{9,1},... | collective-permute-start | bytes 196616 | tf_op jit(solution)/shard_map/ppermute | solution.py:106
  241.5 11.8 %collective-permute-start.27 = (f32[32]{0:T(128)S(1)}, f32[32]{0:T(128)S(1)}, u32[]{:S(2)}, u32[]{:S(2)}) collective-permute-start(f32[32]{0:T(128)S(1)} %get-tuple-element.16), channel_id=1, source_target_pairs={{0,16},{1,17},{2,18},{3,19},{4,20},{5,21},{6,22},{7,23},{8,24},{9,... | collective-permute-start | bytes 392 | tf_op jit(solution)/shard_map/ppermute | solution.py:106
  243.5 9.9 %collective-permute-start.32 = (f32[32]{0:T(128)S(1)}, f32[32]{0:T(128)S(1)}, u32[]{:S(2)}, u32[]{:S(2)}) collective-permute-start(f32[32]{0:T(128)S(1)} %get-tuple-element.13), channel_id=1, source_target_pairs={{0,16},{1,17},{2,18},{3,19},{4,20},{5,21},{6,22},{7,23},{8,24},{9,... | collective-permute-start | bytes 392 | tf_op jit(solution)/shard_map/ppermute | solution.py:106
  251.4 10.1 %collective-permute-start.26 = (bf16[32,1024]{1,0:T(8,128)(2,1)S(1)}, bf16[32,1024]{1,0:T(8,128)(2,1)S(1)}, u32[]{:S(2)}, u32[]{:S(2)}) collective-permute-start(bf16[32,1024]{1,0:T(8,128)(2,1)S(1)} %fusion.62), channel_id=1, source_target_pairs={{0,16},{1,17},{2,18},{3,19},{4,20},{5,21},{6,22},{7,23},{8,24},{9,... | collective-permute-start | bytes 196616 | tf_op jit(solution)/shard_map/ppermute | solution.py:106
  261.6 11.5 %collective-permute-start.33 = (bf16[32,1024]{1,0:T(8,128)(2,1)S(1)}, bf16[32,1024]{1,0:T(8,128)(2,1)S(1)}, u32[]{:S(2)}, u32[]{:S(2)}) collective-permute-start(bf16[32,1024]{1,0:T(8,128)(2,1)S(1)} %fusion.72), channel_id=1, source_target_pairs={{0,4},{1,5},{2,6},{3,7},{4,0},{5,1},{6,2},{7,3},{8,12},{9,13},{10,... | collective-permute-start | bytes 196616 | tf_op jit(solution)/shard_map/ppermute | solution.py:106
  280.9 8.3 %collective-permute-start.35 = (bf16[128,1024]{1,0:T(8,128)(2,1)S(1)}, bf16[128,1024]{1,0:T(8,128)(2,1)S(1)}, u32[]{:S(2)}, u32[]{:S(2)}) collective-permute-start(bf16[128,1024]{1,0:T(8,128)(2,1)S(1)} %maximum_select_fusion.1), channel_id=1, source_target_pairs={{0,1},{1,0},{2,3},{3,2},{4,5},{5,4},{6,7},{7,6},{8,9},{9,8},{10,11... | collective-permute-start | bytes 786440 | tf_op jit(solution)/shard_map/ppermute | solution.py:106
  (37 other events, 545.3 us)
Sparse Core Ops, SparseCore 0:
  30.7 45.9 all-gather.1

commit v4 on v3

--- a/solution.py
+++ b/solution.py
@@ -15,25 +15,29 @@
     )
 
 
-def exclusive_scan(part, axis, reverse):
-    count = lax.axis_size(axis)
-    inclusive = part
-    exclusive = jax.tree.map(jnp.zeros_like, part)
+def exclusive_scans(parts, axis):
+    count = lax.axis_size(axis)
+    inclusive = [part for part, unused_item in parts]
+    exclusive = [jax.tree.map(jnp.zeros_like, part) for part, unused_item in parts]
     rounds = max(1, (count - 1).bit_length())
     for k in range(rounds):
         shift = 1 << k
         if shift >= count:
             break
-        if reverse:
-            perm = [(q, q - shift) for q in range(shift, count)]
-        else:
-            perm = [(q, q + shift) for q in range(count - shift)]
-        sent = (inclusive[0], inclusive[1].astype(jnp.bfloat16))
-        received = lax.ppermute(sent, axis, perm)
-        received = (received[0], received[1].astype(jnp.float32))
-        exclusive = chain_combine(received, exclusive)
-        if k + 1 < rounds:
-            inclusive = chain_combine(received, inclusive)
+        received = []
+        for i, (unused_item, reverse) in enumerate(parts):
+            if reverse:
+                perm = [(q, q - shift) for q in range(shift, count)]
+            else:
+                perm = [(q, q + shift) for q in range(count - shift)]
+            sent = (inclusive[i][0], inclusive[i][1].astype(jnp.bfloat16))
+            received.append(lax.ppermute(sent, axis, perm))
+        received = lax.optimization_barrier(received)
+        for i in range(len(parts)):
+            got = (received[i][0], received[i][1].astype(jnp.float32))
+            exclusive[i] = chain_combine(got, exclusive[i])
+            if k + 1 < rounds:
+                inclusive[i] = chain_combine(got, inclusive[i])
     return exclusive
 
 
@@ -150,6 +154,25 @@
     return rows
 
 
+def all_to_all_pool(local, axis):
+    count = lax.axis_size(axis)
+    local_top, weight_sum, weighted_sum = local
+    row_total, width = weighted_sum.shape
+    rows = row_total // count
+    moved = lax.all_to_all(
+        weighted_sum.astype(jnp.bfloat16), axis, 0, 0, tiled=True
+    ).reshape(count, rows, width)
+    stats = lax.all_to_all(
+        jnp.stack([local_top, weight_sum], axis=0), axis, 1, 1, tiled=True
+    ).reshape(2, count, rows)
+    top = jnp.max(stats[0], axis=0)
+    scale = jnp.exp(stats[0] - top[None, :])
+    total = jnp.sum(stats[1] * scale, axis=0)
+    summed = jnp.sum(moved.astype(jnp.float32) * scale[:, :, None], axis=0)
+    finished = (summed / total[:, None]).astype(jnp.bfloat16)
+    return lax.all_gather(finished, axis, axis=0, tiled=True)
+
+
 def body(
     ssm_input,
     gate_input,
@@ -189,8 +212,9 @@
         projections[::-1, 3 * state_size :],
         decay_rates[1],
     )
-    unused_item, forward_in = exclusive_scan(forward_totals, "seq", False)
-    unused_item, backward_in = exclusive_scan(backward_totals, "seq", True)
+    (unused_item, forward_in), (unused_item, backward_in) = exclusive_scans(
+        [(forward_totals, False), (backward_totals, True)], "seq"
+    )
     forward_out = apply_state(forward_records, forward_in)
     backward_out = apply_state(backward_records, backward_in)[::-1]
     skip_wide = jnp.repeat(skip_gain, head_size)
@@ -216,7 +240,7 @@
     weighted_sum = jnp.dot(
         prob_values.astype(jnp.bfloat16), encoded, preferred_element_type=jnp.float32
     )
-    pooled = reduce_pool((local_top, weight_sum, weighted_sum), "seq", 3)
+    pooled = all_to_all_pool((local_top, weight_sum, weighted_sum), "seq")
     return (encoded[None], pooled[None])
 
 

time: 299 us -> 302 us (1.010)
  blocking collectives: 0 us -> 81.7 us
  starting transfers between devices: 168 us -> 105 us
  waiting for transfers between devices: 60.5 us -> 45.4 us
    all_gather x0 -> x1, blocking collectives: none -> 81.7 us  [all_to_all_pool(): return lax.all_gather(finished, axis, axis=0, tiled=True)]
    ppermute x36 -> x18, starting transfers between devices: 168 us -> 93.4 us  [exclusive_scans(): received.append(lax.ppermute(sent, axis, perm))]
    ppermute x36 -> x18, waiting for transfers between devices: 60.5 us -> 17.7 us  [exclusive_scans(): received.append(lax.ppermute(sent, axis, perm))]
    all_to_all x0 -> x2, waiting for transfers between devices: none -> 27.7 us  [the longest x1 16.6 us: all_to_all_pool(): lax.all_to_all(weighted_sum.astype(jnp.bfloat16), axis, 0, 0, tiled=True)]
    all_to_all x0 -> x2, starting transfers between devices: none -> 12 us  [the longest x1 8.15 us: all_to_all_pool(): lax.all_to_all(jnp.stack([local_top, weight_sum], axis=0), axis, 1, 1, ti...]
  transfers between devices with their start and end apart: 37 -> 21, of which waited for: 10 -> 7; matrix products, arithmetic and copies ran while one was open for 14% -> 13% of each run, Pallas kernels for 0% -> 0%
where the time goes in v4:
time: 302 us; the launch traced here: 301 us
  starting transfers between devices  105 us (35%)
  blocking collectives  81.7 us (27%)
  waiting for transfers between devices  45.4 us (15%)
  local copies, waits for them, and re-layouts  23.1 us (8%)
  other arithmetic  18.9 us (6%)
  between operations  15.6 us (5%)
  matrix products  10.7 us (4%)
    ppermute x18, starting transfers between devices, exclusive_scans(): received.append(lax.ppermute(sent, axis, perm))  93.4 us
    all_gather x1, blocking collectives, all_to_all_pool(): return lax.all_gather(finished, axis, axis=0, tiled=True)  81.7 us
    ppermute x18, waiting for transfers between devices, exclusive_scans(): received.append(lax.ppermute(sent, axis, perm))  17.7 us
    all_to_all x1, waiting for transfers between devices, all_to_all_pool(): lax.all_to_all(weighted_sum.astype(jnp.bfloat16), axis, 0, 0, tiled=True)  16.6 us
    all_to_all x1, waiting for transfers between devices, all_to_all_pool(): lax.all_to_all(jnp.stack([local_top, weight_sum], axis=0), axis, 1, 1, ti...  11.1 us
    all_to_all x1, starting transfers between devices, all_to_all_pool(): lax.all_to_all(jnp.stack([local_top, weight_sum], axis=0), axis, 1, 1, ti...  8.15 us
    rev x1, local copies, waits for them, and re-layouts, body(): backward_out = apply_state(backward_records, backward_in)[::-1]  7.5 us
  transfers between devices with their start and end apart: 21, of which 7 were waited for; matrix products, arithmetic and copies ran while one was open for 13% of the time, Pallas kernels for 0%

profile of v4, /device:TPU:6, one launch (start us, length us, event | category | flops | bytes accessed | tf_op | source)
XLA Modules:
  0.0 300.8 jit_solution(1763640187322875588)
XLA Ops:
  15.9 1.3 collective-permute-start.3
  20.9 5.2 %collective-permute-start.1 = (bf16[16,64,128]{2,1,0:T(8,128)(2,1)}, bf16[16,64,128]{2,1,0:T(8,128)(2,1)}, u32[]{:S(2)}, u32[]{:S(2)}) collective-permute-start(bf16[16,64,128]{2,1,0:T(8,128)(2,1)} %get-tuple-element.68), channel_id=1, source_target_pairs={{0,1},{1,2},{2,3},{3,4},{4,5},{5,6},{6,7},{7,8},{8,9},{9,10},{10,1... | collective-permute-start | bytes 786440 | tf_op jit(solution)/shard_map/ppermute | solution.py:34
  26.1 3.3 %collective-permute-start = (f32[16]{0:T(128)}, f32[16]{0:T(128)}, u32[]{:S(2)}, u32[]{:S(2)}) collective-permute-start(f32[16]{0:T(128)} %get-tuple-element.41), channel_id=1, source_target_pairs={{0,1},{1,2},{2,3},{3,4},{4,5},{5,6},{6,7},{7,8},{8,9},{9,10},{10,1... | collective-permute-start | bytes 200 | tf_op jit(solution)/shard_map/ppermute | solution.py:34
  29.4 1.3 collective-permute-start.2
  30.7 1.6 slice_add_fusion.1
  38.0 2.0 copy.89
  42.0 2.8 convolution_bitcast_fusion.3
  45.8 1.3 collective-permute-start.7
  48.8 6.5 %collective-permute-start.5 = (bf16[16,64,128]{2,1,0:T(8,128)(2,1)S(1)}, bf16[16,64,128]{2,1,0:T(8,128)(2,1)S(1)}, u32[]{:S(2)}, u32[]{:S(2)}) collective-permute-start(bf16[16,64,128]{2,1,0:T(8,128)(2,1)S(1)} %fusion.58), channel_id=1, source_target_pairs={{0,2},{1,3},{2,4},{3,5},{4,6},{5,7},{6,8},{7,9},{8,10},{9,11},{10,... | collective-permute-start | bytes 786440 | tf_op jit(solution)/shard_map/ppermute | solution.py:34
  56.3 1.3 collective-permute-start.6
  57.6 6.8 %collective-permute-start.4 = (f32[16]{0:T(128)S(1)}, f32[16]{0:T(128)S(1)}, u32[]{:S(2)}, u32[]{:S(2)}) collective-permute-start(f32[16]{0:T(128)S(1)} %get-tuple-element.65), channel_id=1, source_target_pairs={{0,2},{1,3},{2,4},{3,5},{4,6},{5,7},{6,8},{7,9},{8,10},{9,11},{10,... | collective-permute-start | bytes 200 | tf_op jit(solution)/shard_map/ppermute | solution.py:34
  65.9 1.3 collective-permute-start.11
  68.3 10.7 %collective-permute-start.9 = (bf16[16,64,128]{2,1,0:T(8,128)(2,1)S(1)}, bf16[16,64,128]{2,1,0:T(8,128)(2,1)S(1)}, u32[]{:S(2)}, u32[]{:S(2)}) collective-permute-start(bf16[16,64,128]{2,1,0:T(8,128)(2,1)S(1)} %get-tuple-element.62), channel_id=1, source_target_pairs={{0,4},{1,5},{2,6},{3,7},{4,8},{5,9},{6,10},{7,11},{8,12},{9,13},{1... | collective-permute-start | bytes 786440 | tf_op jit(solution)/shard_map/ppermute | solution.py:34
  79.0 1.3 collective-permute-start.10
  80.3 12.6 %collective-permute-start.8 = (f32[16]{0:T(128)S(1)}, f32[16]{0:T(128)S(1)}, u32[]{:S(2)}, u32[]{:S(2)}) collective-permute-start(f32[16]{0:T(128)S(1)} %get-tuple-element.57), channel_id=1, source_target_pairs={{0,4},{1,5},{2,6},{3,7},{4,8},{5,9},{6,10},{7,11},{8,12},{9,13},{1... | collective-permute-start | bytes 200 | tf_op jit(solution)/shard_map/ppermute | solution.py:34
  92.9 5.9 %collective-permute-done.10 = f32[16]{0:T(128)S(1)} collective-permute-done((f32[16]{0:T(128)S(1)}, f32[16]{0:T(128)S(1)}, u32[]{:S(2)}, u32[]{:S(2)}) %collective-permute-start.10) | collective-permute-done | bytes 96 | tf_op jit(solution)/shard_map/ppermute | solution.py:34
  99.0 1.3 collective-permute-start.15
  100.4 15.2 %collective-permute-start.13 = (bf16[16,64,128]{2,1,0:T(8,128)(2,1)S(1)}, bf16[16,64,128]{2,1,0:T(8,128)(2,1)S(1)}, u32[]{:S(2)}, u32[]{:S(2)}) collective-permute-start(bf16[16,64,128]{2,1,0:T(8,128)(2,1)S(1)} %fusion.56), channel_id=1, source_target_pairs={{0,8},{1,9},{2,10},{3,11},{4,12},{5,13},{6,14},{7,15},{8,16},{9,17... | collective-permute-start | bytes 786440 | tf_op jit(solution)/shard_map/ppermute | solution.py:34
  115.7 1.3 collective-permute-start.14
  117.0 9.0 %collective-permute-start.12 = (f32[16]{0:T(128)S(1)}, f32[16]{0:T(128)S(1)}, u32[]{:S(2)}, u32[]{:S(2)}) collective-permute-start(f32[16]{0:T(128)S(1)} %get-tuple-element.53), channel_id=1, source_target_pairs={{0,8},{1,9},{2,10},{3,11},{4,12},{5,13},{6,14},{7,15},{8,16},{9,17... | collective-permute-start | bytes 200 | tf_op jit(solution)/shard_map/ppermute | solution.py:34
  127.5 1.4 collective-permute-start.17
  129.2 12.4 %collective-permute-start.16 = (bf16[16,64,128]{2,1,0:T(8,128)(2,1)S(1)}, bf16[16,64,128]{2,1,0:T(8,128)(2,1)S(1)}, u32[]{:S(2)}, u32[]{:S(2)}) collective-permute-start(bf16[16,64,128]{2,1,0:T(8,128)(2,1)S(1)} %fusion.37), channel_id=1, source_target_pairs={{0,16},{1,17},{2,18},{3,19},{4,20},{5,21},{6,22},{7,23},{8,24},{9,... | collective-permute-start | bytes 786440 | tf_op jit(solution)/shard_map/ppermute | solution.py:34
  142.8 2.4 collective-permute-done.17
  145.2 6.8 %collective-permute-done.16 = bf16[16,64,128]{2,1,0:T(8,128)(2,1)S(1)} collective-permute-done((bf16[16,64,128]{2,1,0:T(8,128)(2,1)S(1)}, bf16[16,64,128]{2,1,0:T(8,128)(2,1)S(1)}, u32[]{:S(2)}, u32[]{:S(2)}) %collective-permute-start.16) | collective-permute-done | bytes 262176 | tf_op jit(solution)/shard_map/ppermute | solution.py:34
  157.1 7.5 %rev.19 = f32[256,1024]{0,1:T(8,128)S(1)} reverse(f32[256,1024]{0,1:T(8,128)} %bitcast.204), dimensions={0} | reverse | bytes 2097152 | tf_op jit(solution)/shard_map/rev | solution.py:219
  164.6 1.6 bitcast_reduce_fusion
  166.5 2.3 convolution_convert_fusion.1
  170.2 8.1 %all-to-all-start.1 = ((f32[2,32,8]{2,0,1:T(2,128)}), f32[2,32,8]{2,0,1:T(2,128)S(1)}, u32[]{:S(2)}, u32[]{:S(2)}) async-start(f32[2,32,8]{2,0,1:T(2,128)} %copy.90), calls=%async_computation.1 | async-start | bytes 65536 | tf_op jit(solution)/shard_map/all_to_all | solution.py:165
  179.6 11.1 %all-to-all-done.1 = f32[2,32,8]{2,0,1:T(2,128)S(1)} async-done(((f32[2,32,8]{2,0,1:T(2,128)}), f32[2,32,8]{2,0,1:T(2,128)S(1)}, u32[]{:S(2)}, u32[]{:S(2)}) %all-to-all-start.1) | async-done | bytes 2080 | tf_op jit(solution)/shard_map/all_to_all | solution.py:165
  190.7 3.9 %all-to-all-start = ((bf16[32,8,1024]{2,1,0:T(8,128)(2,1)}), bf16[32,8,1024]{2,1,0:T(8,128)(2,1)S(1)}, u32[]{:S(2)}, u32[]{:S(2)}) async-start(bf16[32,8,1024]{2,1,0:T(8,128)(2,1)} %fusion.4), calls=%async_computation | async-start | bytes 1048576 | tf_op jit(solution)/shard_map/all_to_all | solution.py:162
  194.7 16.6 %all-to-all-done = bf16[32,8,1024]{2,1,0:T(8,128)(2,1)S(1)} async-done(((bf16[32,8,1024]{2,1,0:T(8,128)(2,1)}), bf16[32,8,1024]{2,1,0:T(8,128)(2,1)S(1)}, u32[]{:S(2)}, u32[]{:S(2)}) %all-to-all-start) | async-done | bytes 524320 | tf_op jit(solution)/shard_map/all_to_all | solution.py:162
  211.5 81.7 %all_gather.7 = bf16[256,1024]{1,0:T(8,128)(2,1)S(1)} all-gather(bf16[8,1024]{1,0:T(8,128)(2,1)S(1)} %divide_convert_fusion), channel_id=1, replica_groups=mesh['dp'=16,'seq'=32] {'seq'}, dimensions={0}, use_global_device_ids=true | all-gather | bytes 540672 | tf_op jit(solution)/shard_map/all_gather | solution.py:173
  (167 shorter events, 37.5 us)
Async XLA Ops:
  7.2 161.7 %copy-start = (bf16[256,1024]{1,0:T(8,128)(2,1)S(1)}, bf16[256,1024]{1,0:T(8,128)(2,1)}, u32[]{:S(2)}) copy-start(bf16[256,1024]{1,0:T(8,128)(2,1)} %param.18) | copy-start | bytes 1572868
  7.2 159.3 %all-gather.2.cloned.1.call-start = ((), (), s32[]{:S(2)}) async-start(), calls=%async_computation.2 | async-start | bytes 2228224 | tf_op jit(solution)/shard_map/all_gather | solution.py:229
  15.9 29.0 %collective-permute-start.3 = (bf16[16,64,128]{2,1,0:T(8,128)(2,1)}, bf16[16,64,128]{2,1,0:T(8,128)(2,1)S(1)}, u32[]{:S(2)}, u32[]{:S(2)}) collective-permute-start(bf16[16,64,128]{2,1,0:T(8,128)(2,1)} %get-tuple-element.66), channel_id=1, source_target_pairs={{1,0},{2,1},{3,2},{4,3},{5,4},{6,5},{7,6},{8,7},{9,8},{10,9},{11,1... | collective-permute-start | bytes 786440 | tf_op jit(solution)/shard_map/ppermute | solution.py:34
  19.8 13.7 %copy-start.13 = (f32[2,16,128]{2,1,0:T(8,128)S(1)}, f32[2,16,128]{2,1,0:T(8,128)}, u32[]{:S(2)}) copy-start(f32[2,16,128]{2,1,0:T(8,128)} %copy-done.12) | copy-start | bytes 49156
  19.8 14.3 %copy-start.27 = (f32[16]{0:T(128)S(1)}, f32[16]{0:T(128)}, u32[]{:S(2)}) copy-start(f32[16]{0:T(128)} %copy-done.26) | copy-start | bytes 196
  19.8 14.4 %copy-start.16 = (f32[16,256]{1,0:T(8,128)S(1)}, f32[16,256]{1,0:T(8,128)}, u32[]{:S(2)}) copy-start(f32[16,256]{1,0:T(8,128)} %copy-done.15) | copy-start | bytes 49156
  19.8 15.6 %copy-start.33 = (f32[16]{0:T(128)S(1)}, f32[16]{0:T(128)}, u32[]{:S(2)}) copy-start(f32[16]{0:T(128)} %get-tuple-element.38) | copy-start | bytes 196
  20.9 24.1 %collective-permute-start.1 = (bf16[16,64,128]{2,1,0:T(8,128)(2,1)}, bf16[16,64,128]{2,1,0:T(8,128)(2,1)}, u32[]{:S(2)}, u32[]{:S(2)}) collective-permute-start(bf16[16,64,128]{2,1,0:T(8,128)(2,1)} %get-tuple-element.68), channel_id=1, source_target_pairs={{0,1},{1,2},{2,3},{3,4},{4,5},{5,6},{6,7},{7,8},{8,9},{9,10},{10,1... | collective-permute-start | bytes 786440 | tf_op jit(solution)/shard_map/ppermute | solution.py:34
  26.1 18.8 %collective-permute-start = (f32[16]{0:T(128)}, f32[16]{0:T(128)}, u32[]{:S(2)}, u32[]{:S(2)}) collective-permute-start(f32[16]{0:T(128)} %get-tuple-element.41), channel_id=1, source_target_pairs={{0,1},{1,2},{2,3},{3,4},{4,5},{5,6},{6,7},{7,8},{8,9},{9,10},{10,1... | collective-permute-start | bytes 200 | tf_op jit(solution)/shard_map/ppermute | solution.py:34
  29.4 15.5 %collective-permute-start.2 = (f32[16]{0:T(128)}, f32[16]{0:T(128)}, u32[]{:S(2)}, u32[]{:S(2)}) collective-permute-start(f32[16]{0:T(128)} %get-tuple-element.44), channel_id=1, source_target_pairs={{1,0},{2,1},{3,2},{4,3},{5,4},{6,5},{7,6},{8,7},{9,8},{10,9},{11,1... | collective-permute-start | bytes 200 | tf_op jit(solution)/shard_map/ppermute | solution.py:34
  45.8 19.8 %collective-permute-start.7 = (bf16[16,64,128]{2,1,0:T(8,128)(2,1)S(1)}, bf16[16,64,128]{2,1,0:T(8,128)(2,1)S(1)}, u32[]{:S(2)}, u32[]{:S(2)}) collective-permute-start(bf16[16,64,128]{2,1,0:T(8,128)(2,1)S(1)} %fusion.57), channel_id=1, source_target_pairs={{2,0},{3,1},{4,2},{5,3},{6,4},{7,5},{8,6},{9,7},{10,8},{11,9},{12,... | collective-permute-start | bytes 786440 | tf_op jit(solution)/shard_map/ppermute | solution.py:34
  48.8 16.8 %collective-permute-start.5 = (bf16[16,64,128]{2,1,0:T(8,128)(2,1)S(1)}, bf16[16,64,128]{2,1,0:T(8,128)(2,1)S(1)}, u32[]{:S(2)}, u32[]{:S(2)}) collective-permute-start(bf16[16,64,128]{2,1,0:T(8,128)(2,1)S(1)} %fusion.58), channel_id=1, source_target_pairs={{0,2},{1,3},{2,4},{3,5},{4,6},{5,7},{6,8},{7,9},{8,10},{9,11},{10,... | collective-permute-start | bytes 786440 | tf_op jit(solution)/shard_map/ppermute | solution.py:34
  56.3 8.1 %collective-permute-start.6 = (f32[16]{0:T(128)S(1)}, f32[16]{0:T(128)S(1)}, u32[]{:S(2)}, u32[]{:S(2)}) collective-permute-start(f32[16]{0:T(128)S(1)} %get-tuple-element.61), channel_id=1, source_target_pairs={{2,0},{3,1},{4,2},{5,3},{6,4},{7,5},{8,6},{9,7},{10,8},{11,9},{12,... | collective-permute-start | bytes 200 | tf_op jit(solution)/shard_map/ppermute | solution.py:34
  57.6 8.0 %collective-permute-start.4 = (f32[16]{0:T(128)S(1)}, f32[16]{0:T(128)S(1)}, u32[]{:S(2)}, u32[]{:S(2)}) collective-permute-start(f32[16]{0:T(128)S(1)} %get-tuple-element.65), channel_id=1, source_target_pairs={{0,2},{1,3},{2,4},{3,5},{4,6},{5,7},{6,8},{7,9},{8,10},{9,11},{10,... | collective-permute-start | bytes 200 | tf_op jit(solution)/shard_map/ppermute | solution.py:34
  65.9 33.0 %collective-permute-start.11 = (bf16[16,64,128]{2,1,0:T(8,128)(2,1)S(1)}, bf16[16,64,128]{2,1,0:T(8,128)(2,1)S(1)}, u32[]{:S(2)}, u32[]{:S(2)}) collective-permute-start(bf16[16,64,128]{2,1,0:T(8,128)(2,1)S(1)} %get-tuple-element.58), channel_id=1, source_target_pairs={{4,0},{5,1},{6,2},{7,3},{8,4},{9,5},{10,6},{11,7},{12,8},{13,9},{1... | collective-permute-start | bytes 786440 | tf_op jit(solution)/shard_map/ppermute | solution.py:34
  68.3 30.5 %collective-permute-start.9 = (bf16[16,64,128]{2,1,0:T(8,128)(2,1)S(1)}, bf16[16,64,128]{2,1,0:T(8,128)(2,1)S(1)}, u32[]{:S(2)}, u32[]{:S(2)}) collective-permute-start(bf16[16,64,128]{2,1,0:T(8,128)(2,1)S(1)} %get-tuple-element.62), channel_id=1, source_target_pairs={{0,4},{1,5},{2,6},{3,7},{4,8},{5,9},{6,10},{7,11},{8,12},{9,13},{1... | collective-permute-start | bytes 786440 | tf_op jit(solution)/shard_map/ppermute | solution.py:34
  79.0 19.8 %collective-permute-start.10 = (f32[16]{0:T(128)S(1)}, f32[16]{0:T(128)S(1)}, u32[]{:S(2)}, u32[]{:S(2)}) collective-permute-start(f32[16]{0:T(128)S(1)} %get-tuple-element.55), channel_id=1, source_target_pairs={{4,0},{5,1},{6,2},{7,3},{8,4},{9,5},{10,6},{11,7},{12,8},{13,9},{1... | collective-permute-start | bytes 200 | tf_op jit(solution)/shard_map/ppermute | solution.py:34
  80.3 18.5 %collective-permute-start.8 = (f32[16]{0:T(128)S(1)}, f32[16]{0:T(128)S(1)}, u32[]{:S(2)}, u32[]{:S(2)}) collective-permute-start(f32[16]{0:T(128)S(1)} %get-tuple-element.57), channel_id=1, source_target_pairs={{0,4},{1,5},{2,6},{3,7},{4,8},{5,9},{6,10},{7,11},{8,12},{9,13},{1... | collective-permute-start | bytes 200 | tf_op jit(solution)/shard_map/ppermute | solution.py:34
  99.0 28.3 %collective-permute-start.15 = (bf16[16,64,128]{2,1,0:T(8,128)(2,1)S(1)}, bf16[16,64,128]{2,1,0:T(8,128)(2,1)S(1)}, u32[]{:S(2)}, u32[]{:S(2)}) collective-permute-start(bf16[16,64,128]{2,1,0:T(8,128)(2,1)S(1)} %fusion.55), channel_id=1, source_target_pairs={{8,0},{9,1},{10,2},{11,3},{12,4},{13,5},{14,6},{15,7},{16,8},{17,9... | collective-permute-start | bytes 786440 | tf_op jit(solution)/shard_map/ppermute | solution.py:34
  100.4 26.8 %collective-permute-start.13 = (bf16[16,64,128]{2,1,0:T(8,128)(2,1)S(1)}, bf16[16,64,128]{2,1,0:T(8,128)(2,1)S(1)}, u32[]{:S(2)}, u32[]{:S(2)}) collective-permute-start(bf16[16,64,128]{2,1,0:T(8,128)(2,1)S(1)} %fusion.56), channel_id=1, source_target_pairs={{0,8},{1,9},{2,10},{3,11},{4,12},{5,13},{6,14},{7,15},{8,16},{9,17... | collective-permute-start | bytes 786440 | tf_op jit(solution)/shard_map/ppermute | solution.py:34
  115.7 10.3 %collective-permute-start.14 = (f32[16]{0:T(128)S(1)}, f32[16]{0:T(128)S(1)}, u32[]{:S(2)}, u32[]{:S(2)}) collective-permute-start(f32[16]{0:T(128)S(1)} %get-tuple-element.51), channel_id=1, source_target_pairs={{8,0},{9,1},{10,2},{11,3},{12,4},{13,5},{14,6},{15,7},{16,8},{17,9... | collective-permute-start | bytes 200 | tf_op jit(solution)/shard_map/ppermute | solution.py:34
  117.0 10.3 %collective-permute-start.12 = (f32[16]{0:T(128)S(1)}, f32[16]{0:T(128)S(1)}, u32[]{:S(2)}, u32[]{:S(2)}) collective-permute-start(f32[16]{0:T(128)S(1)} %get-tuple-element.53), channel_id=1, source_target_pairs={{0,8},{1,9},{2,10},{3,11},{4,12},{5,13},{6,14},{7,15},{8,16},{9,17... | collective-permute-start | bytes 200 | tf_op jit(solution)/shard_map/ppermute | solution.py:34
  127.3 26.0 %copy-start.8 = (f32[1,16,64,128]{3,2,1,0:T(8,128)S(1)}, f32[1,16,64,128]{3,2,1,0:T(8,128)}, u32[]{:S(2)}) copy-start(f32[1,16,64,128]{3,2,1,0:T(8,128)} %slice_add_fusion.1) | copy-start | bytes 1572868
  127.3 26.0 %copy-start.9 = (f32[2,128,16,64]{1,3,2,0:T(8,128)S(1)}, f32[2,128,16,64]{1,3,2,0:T(8,128)}, u32[]{:S(2)}) copy-start(f32[2,128,16,64]{1,3,2,0:T(8,128)} %convolution_bitcast_fusion.3) | copy-start | bytes 3145732
  127.3 26.0 %copy-start.10 = (bf16[256,128]{1,0:T(8,128)(2,1)S(1)}, bf16[256,128]{1,0:T(8,128)(2,1)}, u32[]{:S(2)}) copy-start(bf16[256,128]{1,0:T(8,128)(2,1)} %get-tuple-element.70) | copy-start | bytes 196612
  127.3 26.0 %copy-start.21 = (f32[2,128,16]{1,2,0:T(8,128)S(1)}, f32[2,128,16]{1,2,0:T(8,128)}, u32[]{:S(2)}) copy-start(f32[2,128,16]{1,2,0:T(8,128)} %exponential_bitcast_fusion.1) | copy-start | bytes 49156
  127.3 26.0 %copy-start.31 = (f32[2,16]{1,0:T(2,128)S(1)}, f32[2,16]{1,0:T(2,128)}, u32[]{:S(2)}) copy-start(f32[2,16]{1,0:T(2,128)} %pad_exponential_fusion.1) | copy-start | bytes 388
  127.5 17.7 %collective-permute-start.17 = (bf16[16,64,128]{2,1,0:T(8,128)(2,1)S(1)}, bf16[16,64,128]{2,1,0:T(8,128)(2,1)S(1)}, u32[]{:S(2)}, u32[]{:S(2)}) collective-permute-start(bf16[16,64,128]{2,1,0:T(8,128)(2,1)S(1)} %fusion.39), channel_id=1, source_target_pairs={{16,0},{17,1},{18,2},{19,3},{20,4},{21,5},{22,6},{23,7},{24,8},{25... | collective-permute-start | bytes 786440 | tf_op jit(solution)/shard_map/ppermute | solution.py:34
  129.2 22.9 %collective-permute-start.16 = (bf16[16,64,128]{2,1,0:T(8,128)(2,1)S(1)}, bf16[16,64,128]{2,1,0:T(8,128)(2,1)S(1)}, u32[]{:S(2)}, u32[]{:S(2)}) collective-permute-start(bf16[16,64,128]{2,1,0:T(8,128)(2,1)S(1)} %fusion.37), channel_id=1, source_target_pairs={{0,16},{1,17},{2,18},{3,19},{4,20},{5,21},{6,22},{7,23},{8,24},{9,... | collective-permute-start | bytes 786440 | tf_op jit(solution)/shard_map/ppermute | solution.py:34
  168.9 25.7 %copy-start.7 = (bf16[256,1024]{1,0:T(8,128)(2,1)}, bf16[256,1024]{1,0:T(8,128)(2,1)S(1)}, u32[]{:S(2)}) copy-start(bf16[256,1024]{1,0:T(8,128)(2,1)S(1)} %convolution_convert_fusion.1) | copy-start | bytes 1572868
  170.2 20.5 %all-to-all-start.1 = ((f32[2,32,8]{2,0,1:T(2,128)}), f32[2,32,8]{2,0,1:T(2,128)S(1)}, u32[]{:S(2)}, u32[]{:S(2)}) async-start(f32[2,32,8]{2,0,1:T(2,128)} %copy.90), calls=%async_computation.1 | async-start | bytes 65536 | tf_op jit(solution)/shard_map/all_to_all | solution.py:165
  190.7 20.6 %all-to-all-start = ((bf16[32,8,1024]{2,1,0:T(8,128)(2,1)}), bf16[32,8,1024]{2,1,0:T(8,128)(2,1)S(1)}, u32[]{:S(2)}, u32[]{:S(2)}) async-start(bf16[32,8,1024]{2,1,0:T(8,128)(2,1)} %fusion.4), calls=%async_computation | async-start | bytes 1048576 | tf_op jit(solution)/shard_map/all_to_all | solution.py:162
  (23 other events, 122.1 us)
Sparse Core Ops, SparseCore 0:
  30.8 48.0 all-gather.1

commit v5 on v4

--- a/solution.py
+++ b/solution.py
@@ -154,23 +154,41 @@
     return rows
 
 
+def split_wide(values):
+    high = values.astype(jnp.bfloat16)
+    low = (values - high.astype(jnp.float32)).astype(jnp.bfloat16)
+    return high, low
+
+
 def all_to_all_pool(local, axis):
     count = lax.axis_size(axis)
     local_top, weight_sum, weighted_sum = local
     row_total, width = weighted_sum.shape
     rows = row_total // count
-    moved = lax.all_to_all(
-        weighted_sum.astype(jnp.bfloat16), axis, 0, 0, tiled=True
-    ).reshape(count, rows, width)
-    stats = lax.all_to_all(
-        jnp.stack([local_top, weight_sum], axis=0), axis, 1, 1, tiled=True
-    ).reshape(2, count, rows)
-    top = jnp.max(stats[0], axis=0)
-    scale = jnp.exp(stats[0] - top[None, :])
-    total = jnp.sum(stats[1] * scale, axis=0)
-    summed = jnp.sum(moved.astype(jnp.float32) * scale[:, :, None], axis=0)
+    stats = jnp.stack(split_wide(local_top) + split_wide(weight_sum), axis=0)
+    stats = stats.reshape(4, count, rows).transpose(1, 0, 2).reshape(count, 4 * rows)
+    pad = (-4 * rows) % 128
+    packed = jnp.concatenate(
+        [
+            weighted_sum.astype(jnp.bfloat16).reshape(count, rows * width),
+            jnp.pad(stats, ((0, 0), (0, pad))),
+        ],
+        axis=1,
+    )
+    moved = lax.all_to_all(packed, axis, 0, 0, tiled=True)
+    parts = moved[:, : rows * width].reshape(count, rows, width).astype(jnp.float32)
+    got = moved[:, rows * width : rows * width + 4 * rows].astype(jnp.float32)
+    got = got.reshape(count, 4, rows)
+    tops = got[:, 0] + got[:, 1]
+    totals = got[:, 2] + got[:, 3]
+    top = jnp.max(tops, axis=0)
+    scale = jnp.exp(tops - top[None, :])
+    total = jnp.sum(totals * scale, axis=0)
+    summed = jnp.sum(parts * scale[:, :, None], axis=0)
     finished = (summed / total[:, None]).astype(jnp.bfloat16)
-    return lax.all_gather(finished, axis, axis=0, tiled=True)
+    spread_rows = jnp.broadcast_to(finished[None], (count, rows, width))
+    gathered = lax.all_to_all(spread_rows, axis, 0, 0, tiled=True)
+    return gathered.reshape(row_total, width)
 
 
 def body(

time: 302 us -> 242 us (0.80)
  the two profiles are of different devices: /device:TPU:6 before, /device:TPU:8 now
where the time goes in v5:
time: 242 us; the launch traced here: 240 us
  starting transfers between devices  89 us (37%)
  blocking collectives  59.9 us (25%)
  local copies, waits for them, and re-layouts  30.2 us (12%)
  other arithmetic  21.3 us (9%)
  between operations  15.7 us (6%)
  waiting for transfers between devices  14.1 us (6%)
  matrix products  9.91 us (4%)
    ppermute x18, starting transfers between devices, exclusive_scans(): received.append(lax.ppermute(sent, axis, perm))  89 us
    all_to_all x1, blocking collectives, all_to_all_pool(): moved = lax.all_to_all(packed, axis, 0, 0, tiled=True)  36.3 us
    all_to_all x1, blocking collectives, all_to_all_pool(): gathered = lax.all_to_all(spread_rows, axis, 0, 0, tiled=True)  23.6 us
    ppermute x18, waiting for transfers between devices, exclusive_scans(): received.append(lax.ppermute(sent, axis, perm))  14.1 us
    unnamed x76, local copies, waits for them, and re-layouts  8.48 us
    rev x1, local copies, waits for them, and re-layouts, body(): backward_out = apply_state(backward_records, backward_in)[::-1]  7.5 us
    convert_element_type x10, other arithmetic, exclusive_scans(): sent = (inclusive[i][0], inclusive[i][1].astype(jnp.bfloat16))  5.41 us
  transfers between devices with their start and end apart: 19, of which 5 were waited for; matrix products, arithmetic and copies ran while one was open for 16% of the time, Pallas kernels for 0%

profile of v5, /device:TPU:8, one launch (start us, length us, event | category | flops | bytes accessed | tf_op | source)
XLA Modules:
  0.0 240.1 jit_solution(4743079961206483043)
XLA Ops:
  16.4 7.7 %collective-permute-start.3 = (bf16[16,64,128]{2,1,0:T(8,128)(2,1)}, bf16[16,64,128]{2,1,0:T(8,128)(2,1)S(1)}, u32[]{:S(2)}, u32[]{:S(2)}) collective-permute-start(bf16[16,64,128]{2,1,0:T(8,128)(2,1)} %get-tuple-element.70), channel_id=1, source_target_pairs={{1,0},{2,1},{3,2},{4,3},{5,4},{6,5},{7,6},{8,7},{9,8},{10,9},{11,1... | collective-permute-start | bytes 786440 | tf_op jit(solution)/shard_map/ppermute | solution.py:34
  27.8 1.9 collective-permute-start.1
  29.8 1.9 collective-permute-start
  31.7 4.5 %collective-permute-start.2 = (f32[16]{0:T(128)}, f32[16]{0:T(128)}, u32[]{:S(2)}, u32[]{:S(2)}) collective-permute-start(f32[16]{0:T(128)} %get-tuple-element.44), channel_id=1, source_target_pairs={{1,0},{2,1},{3,2},{4,3},{5,4},{6,5},{7,6},{8,7},{9,8},{10,9},{11,1... | collective-permute-start | bytes 200 | tf_op jit(solution)/shard_map/ppermute | solution.py:34
  36.2 1.5 slice_add_fusion.1
  43.5 2.0 copy.100
  47.4 2.8 %convolution_bitcast_fusion.3 = f32[2,128,16,64]{1,3,2,0:T(8,128)} fusion(f32[2,16,128]{2,1,0:T(8,128)} %bitcast.239, f32[2,16,128]{2,1,0:T(8,128)} %copy-done.12, f32[2,128,128]{2,1,0:T(8,128)S(1)} %fusion.103, pred[128,128]{1,0:T(8,128)(4,1)} %iota_compare_fusion.1, bf16[2,128,16,64]{1,0,3,2:T(2,128)(2,1)S(1)} %copy-done.6), kind=kOutput, calls=%fused_computation.11 | convolution fusion | flops 69730304 | bytes 1753088 | tf_op jit(solution)/shard_map/chqk,ckhp->cqhp/dot_general | solution.py:64
  51.3 1.3 collective-permute-start.7
  54.3 5.5 %collective-permute-start.5 = (bf16[16,64,128]{2,1,0:T(8,128)(2,1)S(1)}, bf16[16,64,128]{2,1,0:T(8,128)(2,1)S(1)}, u32[]{:S(2)}, u32[]{:S(2)}) collective-permute-start(bf16[16,64,128]{2,1,0:T(8,128)(2,1)S(1)} %fusion.61), channel_id=1, source_target_pairs={{0,2},{1,3},{2,4},{3,5},{4,6},{5,7},{6,8},{7,9},{8,10},{9,11},{10,... | collective-permute-start | bytes 786440 | tf_op jit(solution)/shard_map/ppermute | solution.py:34
  60.8 1.3 collective-permute-start.6
  62.1 5.4 %collective-permute-start.4 = (f32[16]{0:T(128)S(1)}, f32[16]{0:T(128)S(1)}, u32[]{:S(2)}, u32[]{:S(2)}) collective-permute-start(f32[16]{0:T(128)S(1)} %get-tuple-element.69), channel_id=1, source_target_pairs={{0,2},{1,3},{2,4},{3,5},{4,6},{5,7},{6,8},{7,9},{8,10},{9,11},{10,... | collective-permute-start | bytes 200 | tf_op jit(solution)/shard_map/ppermute | solution.py:34
  67.5 1.3 collective-permute-done.4
  69.0 1.3 collective-permute-start.11
  71.5 8.5 %collective-permute-start.9 = (bf16[16,64,128]{2,1,0:T(8,128)(2,1)S(1)}, bf16[16,64,128]{2,1,0:T(8,128)(2,1)S(1)}, u32[]{:S(2)}, u32[]{:S(2)}) collective-permute-start(bf16[16,64,128]{2,1,0:T(8,128)(2,1)S(1)} %get-tuple-element.66), channel_id=1, source_target_pairs={{0,4},{1,5},{2,6},{3,7},{4,8},{5,9},{6,10},{7,11},{8,12},{9,13},{1... | collective-permute-start | bytes 786440 | tf_op jit(solution)/shard_map/ppermute | solution.py:34
  80.0 1.3 collective-permute-start.10
  81.3 12.6 %collective-permute-start.8 = (f32[16]{0:T(128)S(1)}, f32[16]{0:T(128)S(1)}, u32[]{:S(2)}, u32[]{:S(2)}) collective-permute-start(f32[16]{0:T(128)S(1)} %get-tuple-element.61), channel_id=1, source_target_pairs={{0,4},{1,5},{2,6},{3,7},{4,8},{5,9},{6,10},{7,11},{8,12},{9,13},{1... | collective-permute-start | bytes 200 | tf_op jit(solution)/shard_map/ppermute | solution.py:34
  93.9 6.4 %collective-permute-done.10 = f32[16]{0:T(128)S(1)} collective-permute-done((f32[16]{0:T(128)S(1)}, f32[16]{0:T(128)S(1)}, u32[]{:S(2)}, u32[]{:S(2)}) %collective-permute-start.10) | collective-permute-done | bytes 96 | tf_op jit(solution)/shard_map/ppermute | solution.py:34
  100.4 1.3 collective-permute-start.15
  101.9 10.8 %collective-permute-start.13 = (bf16[16,64,128]{2,1,0:T(8,128)(2,1)S(1)}, bf16[16,64,128]{2,1,0:T(8,128)(2,1)S(1)}, u32[]{:S(2)}, u32[]{:S(2)}) collective-permute-start(bf16[16,64,128]{2,1,0:T(8,128)(2,1)S(1)} %fusion.59), channel_id=1, source_target_pairs={{0,8},{1,9},{2,10},{3,11},{4,12},{5,13},{6,14},{7,15},{8,16},{9,17... | collective-permute-start | bytes 786440 | tf_op jit(solution)/shard_map/ppermute | solution.py:34
  112.7 1.3 collective-permute-start.14
  114.0 10.9 %collective-permute-start.12 = (f32[16]{0:T(128)S(1)}, f32[16]{0:T(128)S(1)}, u32[]{:S(2)}, u32[]{:S(2)}) collective-permute-start(f32[16]{0:T(128)S(1)} %get-tuple-element.57), channel_id=1, source_target_pairs={{0,8},{1,9},{2,10},{3,11},{4,12},{5,13},{6,14},{7,15},{8,16},{9,17... | collective-permute-start | bytes 200 | tf_op jit(solution)/shard_map/ppermute | solution.py:34
  125.0 1.3 collective-permute-done.12
  126.5 1.4 collective-permute-start.17
  128.2 10.0 %collective-permute-start.16 = (bf16[16,64,128]{2,1,0:T(8,128)(2,1)S(1)}, bf16[16,64,128]{2,1,0:T(8,128)(2,1)S(1)}, u32[]{:S(2)}, u32[]{:S(2)}) collective-permute-start(bf16[16,64,128]{2,1,0:T(8,128)(2,1)S(1)} %fusion.40), channel_id=1, source_target_pairs={{0,16},{1,17},{2,18},{3,19},{4,20},{5,21},{6,22},{7,23},{8,24},{9,... | collective-permute-start | bytes 786440 | tf_op jit(solution)/shard_map/ppermute | solution.py:34
  140.3 4.3 %collective-permute-done.16 = bf16[16,64,128]{2,1,0:T(8,128)(2,1)S(1)} collective-permute-done((bf16[16,64,128]{2,1,0:T(8,128)(2,1)S(1)}, bf16[16,64,128]{2,1,0:T(8,128)(2,1)S(1)}, u32[]{:S(2)}, u32[]{:S(2)}) %collective-permute-start.16) | collective-permute-done | bytes 262176 | tf_op jit(solution)/shard_map/ppermute | solution.py:34
  149.7 7.5 %rev.19 = f32[256,1024]{0,1:T(8,128)S(1)} reverse(f32[256,1024]{0,1:T(8,128)} %bitcast.227), dimensions={0} | reverse | bytes 2097152 | tf_op jit(solution)/shard_map/rev | solution.py:237
  157.2 1.6 bitcast_reduce_fusion
  159.1 2.3 convolution_convert_fusion.1
  165.5 36.3 %all_to_all.17 = bf16[32,2,4160]{2,1,0:T(2,128)(2,1)S(1)} all-to-all(bf16[32,2,4160]{2,1,0:T(2,128)(2,1)S(1)} %reshape.310), channel_id=1, replica_groups=mesh['dp'=16,'seq'=32] {'seq'}, dimensions={0} | all-to-all | bytes 1064960 | tf_op jit(solution)/shard_map/all_to_all | solution.py:178
  201.8 1.9 reshape.311
  203.6 3.6 %copy.107 = bf16[32,1,8320]{0,2,1:T(8,128)(2,1)S(1)} copy(bf16[32,1,8320]{2,1,0:T(2,128)(2,1)} %reshape.311) | data formatting | bytes 1064960 | tf_op jit(solution)/shard_map/all_to_all | solution.py:178
  208.9 23.6 %all_to_all.18 = bf16[32,8,1024]{2,1,0:T(8,128)(2,1)S(1)} all-to-all(bf16[32,8,1024]{2,1,0:T(8,128)(2,1)S(1)} %broadcast_in_dim.59), channel_id=1, replica_groups=mesh['dp'=16,'seq'=32] {'seq'}, dimensions={0} | all-to-all | bytes 1048576 | tf_op jit(solution)/shard_map/all_to_all | solution.py:190
  (177 shorter events, 39.1 us)
Async XLA Ops:
  7.2 154.3 %copy-start = (bf16[256,1024]{1,0:T(8,128)(2,1)S(1)}, bf16[256,1024]{1,0:T(8,128)(2,1)}, u32[]{:S(2)}) copy-start(bf16[256,1024]{1,0:T(8,128)(2,1)} %param.18) | copy-start | bytes 1572868
  7.2 151.9 %all-gather.2.cloned.1.call-start = ((), (), s32[]{:S(2)}) async-start(), calls=%async_computation.2 | async-start | bytes 2228224 | tf_op jit(solution)/shard_map/all_gather | solution.py:247
  9.3 16.5 %copy-start.17 = (f32[2,2,8,128]{3,2,1,0:T(8,128)}, f32[2,2,8,128]{3,2,1,0:T(8,128)S(1)}, u32[]{:S(2)}) copy-start(f32[2,2,8,128]{3,2,1,0:T(8,128)S(1)} %get-tuple-element.78) | copy-start | bytes 49156
  14.4 12.0 %copy-start.11 = (bf16[256,128]{1,0:T(8,128)(2,1)}, bf16[256,128]{1,0:T(8,128)(2,1)S(1)}, u32[]{:S(2)}) copy-start(bf16[256,128]{1,0:T(8,128)(2,1)S(1)} %get-tuple-element.77) | copy-start | bytes 196612
  16.4 34.0 %collective-permute-start.3 = (bf16[16,64,128]{2,1,0:T(8,128)(2,1)}, bf16[16,64,128]{2,1,0:T(8,128)(2,1)S(1)}, u32[]{:S(2)}, u32[]{:S(2)}) collective-permute-start(bf16[16,64,128]{2,1,0:T(8,128)(2,1)} %get-tuple-element.70), channel_id=1, source_target_pairs={{1,0},{2,1},{3,2},{4,3},{5,4},{6,5},{7,6},{8,7},{9,8},{10,9},{11,1... | collective-permute-start | bytes 786440 | tf_op jit(solution)/shard_map/ppermute | solution.py:34
  26.7 11.1 %copy-start.18 = (f32[2,2,8,128]{3,2,1,0:T(8,128)S(1)}, f32[2,2,8,128]{3,2,1,0:T(8,128)}, u32[]{:S(2)}) copy-start(f32[2,2,8,128]{3,2,1,0:T(8,128)} %copy-done.17) | copy-start | bytes 49156
  26.7 12.3 %copy-start.13 = (f32[2,16,128]{2,1,0:T(8,128)S(1)}, f32[2,16,128]{2,1,0:T(8,128)}, u32[]{:S(2)}) copy-start(f32[2,16,128]{2,1,0:T(8,128)} %copy-done.12) | copy-start | bytes 49156
  26.7 12.9 %copy-start.27 = (f32[16]{0:T(128)S(1)}, f32[16]{0:T(128)}, u32[]{:S(2)}) copy-start(f32[16]{0:T(128)} %copy-done.26) | copy-start | bytes 196
  26.7 13.0 %copy-start.16 = (f32[16,256]{1,0:T(8,128)S(1)}, f32[16,256]{1,0:T(8,128)}, u32[]{:S(2)}) copy-start(f32[16,256]{1,0:T(8,128)} %copy-done.15) | copy-start | bytes 49156
  26.7 14.2 %copy-start.33 = (f32[16]{0:T(128)S(1)}, f32[16]{0:T(128)}, u32[]{:S(2)}) copy-start(f32[16]{0:T(128)} %get-tuple-element.38) | copy-start | bytes 196
  27.8 22.6 %collective-permute-start.1 = (bf16[16,64,128]{2,1,0:T(8,128)(2,1)}, bf16[16,64,128]{2,1,0:T(8,128)(2,1)}, u32[]{:S(2)}, u32[]{:S(2)}) collective-permute-start(bf16[16,64,128]{2,1,0:T(8,128)(2,1)} %get-tuple-element.72), channel_id=1, source_target_pairs={{0,1},{1,2},{2,3},{3,4},{4,5},{5,6},{6,7},{7,8},{8,9},{9,10},{10,1... | collective-permute-start | bytes 786440 | tf_op jit(solution)/shard_map/ppermute | solution.py:34
  29.8 20.6 %collective-permute-start = (f32[16]{0:T(128)}, f32[16]{0:T(128)}, u32[]{:S(2)}, u32[]{:S(2)}) collective-permute-start(f32[16]{0:T(128)} %get-tuple-element.41), channel_id=1, source_target_pairs={{0,1},{1,2},{2,3},{3,4},{4,5},{5,6},{6,7},{7,8},{8,9},{9,10},{10,1... | collective-permute-start | bytes 200 | tf_op jit(solution)/shard_map/ppermute | solution.py:34
  31.7 18.7 %collective-permute-start.2 = (f32[16]{0:T(128)}, f32[16]{0:T(128)}, u32[]{:S(2)}, u32[]{:S(2)}) collective-permute-start(f32[16]{0:T(128)} %get-tuple-element.44), channel_id=1, source_target_pairs={{1,0},{2,1},{3,2},{4,3},{5,4},{6,5},{7,6},{8,7},{9,8},{10,9},{11,1... | collective-permute-start | bytes 200 | tf_op jit(solution)/shard_map/ppermute | solution.py:34
  51.3 17.5 %collective-permute-start.7 = (bf16[16,64,128]{2,1,0:T(8,128)(2,1)S(1)}, bf16[16,64,128]{2,1,0:T(8,128)(2,1)S(1)}, u32[]{:S(2)}, u32[]{:S(2)}) collective-permute-start(bf16[16,64,128]{2,1,0:T(8,128)(2,1)S(1)} %fusion.60), channel_id=1, source_target_pairs={{2,0},{3,1},{4,2},{5,3},{6,4},{7,5},{8,6},{9,7},{10,8},{11,9},{12,... | collective-permute-start | bytes 786440 | tf_op jit(solution)/shard_map/ppermute | solution.py:34
  54.3 14.5 %collective-permute-start.5 = (bf16[16,64,128]{2,1,0:T(8,128)(2,1)S(1)}, bf16[16,64,128]{2,1,0:T(8,128)(2,1)S(1)}, u32[]{:S(2)}, u32[]{:S(2)}) collective-permute-start(bf16[16,64,128]{2,1,0:T(8,128)(2,1)S(1)} %fusion.61), channel_id=1, source_target_pairs={{0,2},{1,3},{2,4},{3,5},{4,6},{5,7},{6,8},{7,9},{8,10},{9,11},{10,... | collective-permute-start | bytes 786440 | tf_op jit(solution)/shard_map/ppermute | solution.py:34
  60.8 6.8 %collective-permute-start.6 = (f32[16]{0:T(128)S(1)}, f32[16]{0:T(128)S(1)}, u32[]{:S(2)}, u32[]{:S(2)}) collective-permute-start(f32[16]{0:T(128)S(1)} %get-tuple-element.65), channel_id=1, source_target_pairs={{2,0},{3,1},{4,2},{5,3},{6,4},{7,5},{8,6},{9,7},{10,8},{11,9},{12,... | collective-permute-start | bytes 200 | tf_op jit(solution)/shard_map/ppermute | solution.py:34
  62.1 6.7 %collective-permute-start.4 = (f32[16]{0:T(128)S(1)}, f32[16]{0:T(128)S(1)}, u32[]{:S(2)}, u32[]{:S(2)}) collective-permute-start(f32[16]{0:T(128)S(1)} %get-tuple-element.69), channel_id=1, source_target_pairs={{0,2},{1,3},{2,4},{3,5},{4,6},{5,7},{6,8},{7,9},{8,10},{9,11},{10,... | collective-permute-start | bytes 200 | tf_op jit(solution)/shard_map/ppermute | solution.py:34
  69.0 31.3 %collective-permute-start.11 = (bf16[16,64,128]{2,1,0:T(8,128)(2,1)S(1)}, bf16[16,64,128]{2,1,0:T(8,128)(2,1)S(1)}, u32[]{:S(2)}, u32[]{:S(2)}) collective-permute-start(bf16[16,64,128]{2,1,0:T(8,128)(2,1)S(1)} %get-tuple-element.62), channel_id=1, source_target_pairs={{4,0},{5,1},{6,2},{7,3},{8,4},{9,5},{10,6},{11,7},{12,8},{13,9},{1... | collective-permute-start | bytes 786440 | tf_op jit(solution)/shard_map/ppermute | solution.py:34
  71.5 28.8 %collective-permute-start.9 = (bf16[16,64,128]{2,1,0:T(8,128)(2,1)S(1)}, bf16[16,64,128]{2,1,0:T(8,128)(2,1)S(1)}, u32[]{:S(2)}, u32[]{:S(2)}) collective-permute-start(bf16[16,64,128]{2,1,0:T(8,128)(2,1)S(1)} %get-tuple-element.66), channel_id=1, source_target_pairs={{0,4},{1,5},{2,6},{3,7},{4,8},{5,9},{6,10},{7,11},{8,12},{9,13},{1... | collective-permute-start | bytes 786440 | tf_op jit(solution)/shard_map/ppermute | solution.py:34
  80.0 20.3 %collective-permute-start.10 = (f32[16]{0:T(128)S(1)}, f32[16]{0:T(128)S(1)}, u32[]{:S(2)}, u32[]{:S(2)}) collective-permute-start(f32[16]{0:T(128)S(1)} %get-tuple-element.59), channel_id=1, source_target_pairs={{4,0},{5,1},{6,2},{7,3},{8,4},{9,5},{10,6},{11,7},{12,8},{13,9},{1... | collective-permute-start | bytes 200 | tf_op jit(solution)/shard_map/ppermute | solution.py:34
  81.3 19.0 %collective-permute-start.8 = (f32[16]{0:T(128)S(1)}, f32[16]{0:T(128)S(1)}, u32[]{:S(2)}, u32[]{:S(2)}) collective-permute-start(f32[16]{0:T(128)S(1)} %get-tuple-element.61), channel_id=1, source_target_pairs={{0,4},{1,5},{2,6},{3,7},{4,8},{5,9},{6,10},{7,11},{8,12},{9,13},{1... | collective-permute-start | bytes 200 | tf_op jit(solution)/shard_map/ppermute | solution.py:34
  100.4 25.9 %collective-permute-start.15 = (bf16[16,64,128]{2,1,0:T(8,128)(2,1)S(1)}, bf16[16,64,128]{2,1,0:T(8,128)(2,1)S(1)}, u32[]{:S(2)}, u32[]{:S(2)}) collective-permute-start(bf16[16,64,128]{2,1,0:T(8,128)(2,1)S(1)} %fusion.58), channel_id=1, source_target_pairs={{8,0},{9,1},{10,2},{11,3},{12,4},{13,5},{14,6},{15,7},{16,8},{17,9... | collective-permute-start | bytes 786440 | tf_op jit(solution)/shard_map/ppermute | solution.py:34
  101.9 24.4 %collective-permute-start.13 = (bf16[16,64,128]{2,1,0:T(8,128)(2,1)S(1)}, bf16[16,64,128]{2,1,0:T(8,128)(2,1)S(1)}, u32[]{:S(2)}, u32[]{:S(2)}) collective-permute-start(bf16[16,64,128]{2,1,0:T(8,128)(2,1)S(1)} %fusion.59), channel_id=1, source_target_pairs={{0,8},{1,9},{2,10},{3,11},{4,12},{5,13},{6,14},{7,15},{8,16},{9,17... | collective-permute-start | bytes 786440 | tf_op jit(solution)/shard_map/ppermute | solution.py:34
  112.7 12.3 %collective-permute-start.14 = (f32[16]{0:T(128)S(1)}, f32[16]{0:T(128)S(1)}, u32[]{:S(2)}, u32[]{:S(2)}) collective-permute-start(f32[16]{0:T(128)S(1)} %get-tuple-element.55), channel_id=1, source_target_pairs={{8,0},{9,1},{10,2},{11,3},{12,4},{13,5},{14,6},{15,7},{16,8},{17,9... | collective-permute-start | bytes 200 | tf_op jit(solution)/shard_map/ppermute | solution.py:34
  114.0 12.2 %collective-permute-start.12 = (f32[16]{0:T(128)S(1)}, f32[16]{0:T(128)S(1)}, u32[]{:S(2)}, u32[]{:S(2)}) collective-permute-start(f32[16]{0:T(128)S(1)} %get-tuple-element.57), channel_id=1, source_target_pairs={{0,8},{1,9},{2,10},{3,11},{4,12},{5,13},{6,14},{7,15},{8,16},{9,17... | collective-permute-start | bytes 200 | tf_op jit(solution)/shard_map/ppermute | solution.py:34
  126.3 19.6 %copy-start.8 = (f32[1,16,64,128]{3,2,1,0:T(8,128)S(1)}, f32[1,16,64,128]{3,2,1,0:T(8,128)}, u32[]{:S(2)}) copy-start(f32[1,16,64,128]{3,2,1,0:T(8,128)} %slice_add_fusion.1) | copy-start | bytes 1572868
  126.3 19.6 %copy-start.9 = (f32[2,128,16,64]{1,3,2,0:T(8,128)S(1)}, f32[2,128,16,64]{1,3,2,0:T(8,128)}, u32[]{:S(2)}) copy-start(f32[2,128,16,64]{1,3,2,0:T(8,128)} %convolution_bitcast_fusion.3) | copy-start | bytes 3145732
  126.3 19.6 %copy-start.10 = (bf16[256,128]{1,0:T(8,128)(2,1)S(1)}, bf16[256,128]{1,0:T(8,128)(2,1)}, u32[]{:S(2)}) copy-start(bf16[256,128]{1,0:T(8,128)(2,1)} %get-tuple-element.74) | copy-start | bytes 196612
  126.3 19.6 %copy-start.21 = (f32[2,128,16]{1,2,0:T(8,128)S(1)}, f32[2,128,16]{1,2,0:T(8,128)}, u32[]{:S(2)}) copy-start(f32[2,128,16]{1,2,0:T(8,128)} %exponential_bitcast_fusion.1) | copy-start | bytes 49156
  126.3 19.6 %copy-start.31 = (f32[2,16]{1,0:T(2,128)S(1)}, f32[2,16]{1,0:T(2,128)}, u32[]{:S(2)}) copy-start(f32[2,16]{1,0:T(2,128)} %pad_exponential_fusion.1) | copy-start | bytes 388
  126.5 13.8 %collective-permute-start.17 = (bf16[16,64,128]{2,1,0:T(8,128)(2,1)S(1)}, bf16[16,64,128]{2,1,0:T(8,128)(2,1)S(1)}, u32[]{:S(2)}, u32[]{:S(2)}) collective-permute-start(bf16[16,64,128]{2,1,0:T(8,128)(2,1)S(1)} %fusion.42), channel_id=1, source_target_pairs={{16,0},{17,1},{18,2},{19,3},{20,4},{21,5},{22,6},{23,7},{24,8},{25... | collective-permute-start | bytes 786440 | tf_op jit(solution)/shard_map/ppermute | solution.py:34
  128.2 16.4 %collective-permute-start.16 = (bf16[16,64,128]{2,1,0:T(8,128)(2,1)S(1)}, bf16[16,64,128]{2,1,0:T(8,128)(2,1)S(1)}, u32[]{:S(2)}, u32[]{:S(2)}) collective-permute-start(bf16[16,64,128]{2,1,0:T(8,128)(2,1)S(1)} %fusion.40), channel_id=1, source_target_pairs={{0,16},{1,17},{2,18},{3,19},{4,20},{5,21},{6,22},{7,23},{8,24},{9,... | collective-permute-start | bytes 786440 | tf_op jit(solution)/shard_map/ppermute | solution.py:34
  (21 other events, 87.9 us)
Sparse Core Ops, SparseCore 0:
  36.3 41.9 all-gather.1

commit v6 on v5

--- a/solution.py
+++ b/solution.py
@@ -155,9 +155,9 @@
 
 
 def split_wide(values):
-    high = values.astype(jnp.bfloat16)
-    low = (values - high.astype(jnp.float32)).astype(jnp.bfloat16)
-    return high, low
+    rounded = lax.reduce_precision(values, exponent_bits=8, mantissa_bits=7)
+    low = (values - rounded).astype(jnp.bfloat16)
+    return rounded.astype(jnp.bfloat16), low
 
 
 def all_to_all_pool(local, axis):

time: 242 us -> 242 us (level)
  no operation moved by 1% of the time
where the time goes in v6:
time: 242 us; the launch traced here: 240 us
  starting transfers between devices  89 us (37%)
  blocking collectives  59.9 us (25%)
  local copies, waits for them, and re-layouts  30.2 us (12%)
  other arithmetic  21.3 us (9%)
  between operations  15.7 us (6%)
  waiting for transfers between devices  14.1 us (6%)
  matrix products  9.91 us (4%)
    ppermute x18, starting transfers between devices, exclusive_scans(): received.append(lax.ppermute(sent, axis, perm))  89 us
    all_to_all x1, blocking collectives, all_to_all_pool(): moved = lax.all_to_all(packed, axis, 0, 0, tiled=True)  36.3 us
    all_to_all x1, blocking collectives, all_to_all_pool(): gathered = lax.all_to_all(spread_rows, axis, 0, 0, tiled=True)  23.6 us
    ppermute x18, waiting for transfers between devices, exclusive_scans(): received.append(lax.ppermute(sent, axis, perm))  14.1 us
    unnamed x76, local copies, waits for them, and re-layouts  8.48 us
    rev x1, local copies, waits for them, and re-layouts, body(): backward_out = apply_state(backward_records, backward_in)[::-1]  7.5 us
    convert_element_type x10, other arithmetic, exclusive_scans(): sent = (inclusive[i][0], inclusive[i][1].astype(jnp.bfloat16))  5.41 us
  transfers between devices with their start and end apart: 19, of which 5 were waited for; matrix products, arithmetic and copies ran while one was open for 16% of the time, Pallas kernels for 0%

profile of v6, /device:TPU:8, one launch (start us, length us, event | category | flops | bytes accessed | tf_op | source)
XLA Modules:
  0.0 240.1 jit_solution(10865013715205224408)
XLA Ops:
  16.4 7.7 %collective-permute-start.3 = (bf16[16,64,128]{2,1,0:T(8,128)(2,1)}, bf16[16,64,128]{2,1,0:T(8,128)(2,1)S(1)}, u32[]{:S(2)}, u32[]{:S(2)}) collective-permute-start(bf16[16,64,128]{2,1,0:T(8,128)(2,1)} %get-tuple-element.66), channel_id=1, source_target_pairs={{1,0},{2,1},{3,2},{4,3},{5,4},{6,5},{7,6},{8,7},{9,8},{10,9},{11,1... | collective-permute-start | bytes 786440 | tf_op jit(solution)/shard_map/ppermute | solution.py:34
  27.8 1.9 collective-permute-start.1
  29.8 1.9 collective-permute-start
  31.7 4.5 %collective-permute-start.2 = (f32[16]{0:T(128)}, f32[16]{0:T(128)}, u32[]{:S(2)}, u32[]{:S(2)}) collective-permute-start(f32[16]{0:T(128)} %get-tuple-element.44), channel_id=1, source_target_pairs={{1,0},{2,1},{3,2},{4,3},{5,4},{6,5},{7,6},{8,7},{9,8},{10,9},{11,1... | collective-permute-start | bytes 200 | tf_op jit(solution)/shard_map/ppermute | solution.py:34
  36.2 1.5 slice_add_fusion.1
  43.5 2.0 copy.100
  47.4 2.8 %convolution_bitcast_fusion.3 = f32[2,128,16,64]{1,3,2,0:T(8,128)} fusion(f32[2,16,128]{2,1,0:T(8,128)} %bitcast.239, f32[2,16,128]{2,1,0:T(8,128)} %copy-done.12, f32[2,128,128]{2,1,0:T(8,128)S(1)} %fusion.105, pred[128,128]{1,0:T(8,128)(4,1)} %iota_compare_fusion.1, bf16[2,128,16,64]{1,0,3,2:T(2,128)(2,1)S(1)} %copy-done.6), kind=kOutput, calls=%fused_computation.11 | convolution fusion | flops 69730304 | bytes 1753088 | tf_op jit(solution)/shard_map/chqk,ckhp->cqhp/dot_general | solution.py:64
  51.3 1.3 collective-permute-start.7
  54.3 5.5 %collective-permute-start.5 = (bf16[16,64,128]{2,1,0:T(8,128)(2,1)S(1)}, bf16[16,64,128]{2,1,0:T(8,128)(2,1)S(1)}, u32[]{:S(2)}, u32[]{:S(2)}) collective-permute-start(bf16[16,64,128]{2,1,0:T(8,128)(2,1)S(1)} %fusion.61), channel_id=1, source_target_pairs={{0,2},{1,3},{2,4},{3,5},{4,6},{5,7},{6,8},{7,9},{8,10},{9,11},{10,... | collective-permute-start | bytes 786440 | tf_op jit(solution)/shard_map/ppermute | solution.py:34
  60.8 1.3 collective-permute-start.6
  62.1 5.4 %collective-permute-start.4 = (f32[16]{0:T(128)S(1)}, f32[16]{0:T(128)S(1)}, u32[]{:S(2)}, u32[]{:S(2)}) collective-permute-start(f32[16]{0:T(128)S(1)} %get-tuple-element.65), channel_id=1, source_target_pairs={{0,2},{1,3},{2,4},{3,5},{4,6},{5,7},{6,8},{7,9},{8,10},{9,11},{10,... | collective-permute-start | bytes 200 | tf_op jit(solution)/shard_map/ppermute | solution.py:34
  67.5 1.3 collective-permute-done.4
  69.0 1.3 collective-permute-start.11
  71.5 8.5 %collective-permute-start.9 = (bf16[16,64,128]{2,1,0:T(8,128)(2,1)S(1)}, bf16[16,64,128]{2,1,0:T(8,128)(2,1)S(1)}, u32[]{:S(2)}, u32[]{:S(2)}) collective-permute-start(bf16[16,64,128]{2,1,0:T(8,128)(2,1)S(1)} %get-tuple-element.62), channel_id=1, source_target_pairs={{0,4},{1,5},{2,6},{3,7},{4,8},{5,9},{6,10},{7,11},{8,12},{9,13},{1... | collective-permute-start | bytes 786440 | tf_op jit(solution)/shard_map/ppermute | solution.py:34
  80.0 1.3 collective-permute-start.10
  81.3 12.6 %collective-permute-start.8 = (f32[16]{0:T(128)S(1)}, f32[16]{0:T(128)S(1)}, u32[]{:S(2)}, u32[]{:S(2)}) collective-permute-start(f32[16]{0:T(128)S(1)} %get-tuple-element.57), channel_id=1, source_target_pairs={{0,4},{1,5},{2,6},{3,7},{4,8},{5,9},{6,10},{7,11},{8,12},{9,13},{1... | collective-permute-start | bytes 200 | tf_op jit(solution)/shard_map/ppermute | solution.py:34
  93.9 6.4 %collective-permute-done.10 = f32[16]{0:T(128)S(1)} collective-permute-done((f32[16]{0:T(128)S(1)}, f32[16]{0:T(128)S(1)}, u32[]{:S(2)}, u32[]{:S(2)}) %collective-permute-start.10) | collective-permute-done | bytes 96 | tf_op jit(solution)/shard_map/ppermute | solution.py:34
  100.4 1.3 collective-permute-start.15
  101.9 10.8 %collective-permute-start.13 = (bf16[16,64,128]{2,1,0:T(8,128)(2,1)S(1)}, bf16[16,64,128]{2,1,0:T(8,128)(2,1)S(1)}, u32[]{:S(2)}, u32[]{:S(2)}) collective-permute-start(bf16[16,64,128]{2,1,0:T(8,128)(2,1)S(1)} %fusion.59), channel_id=1, source_target_pairs={{0,8},{1,9},{2,10},{3,11},{4,12},{5,13},{6,14},{7,15},{8,16},{9,17... | collective-permute-start | bytes 786440 | tf_op jit(solution)/shard_map/ppermute | solution.py:34
  112.7 1.3 collective-permute-start.14
  114.0 10.9 %collective-permute-start.12 = (f32[16]{0:T(128)S(1)}, f32[16]{0:T(128)S(1)}, u32[]{:S(2)}, u32[]{:S(2)}) collective-permute-start(f32[16]{0:T(128)S(1)} %get-tuple-element.53), channel_id=1, source_target_pairs={{0,8},{1,9},{2,10},{3,11},{4,12},{5,13},{6,14},{7,15},{8,16},{9,17... | collective-permute-start | bytes 200 | tf_op jit(solution)/shard_map/ppermute | solution.py:34
  125.0 1.3 collective-permute-done.12
  126.5 1.4 collective-permute-start.17
  128.2 10.0 %collective-permute-start.16 = (bf16[16,64,128]{2,1,0:T(8,128)(2,1)S(1)}, bf16[16,64,128]{2,1,0:T(8,128)(2,1)S(1)}, u32[]{:S(2)}, u32[]{:S(2)}) collective-permute-start(bf16[16,64,128]{2,1,0:T(8,128)(2,1)S(1)} %fusion.40), channel_id=1, source_target_pairs={{0,16},{1,17},{2,18},{3,19},{4,20},{5,21},{6,22},{7,23},{8,24},{9,... | collective-permute-start | bytes 786440 | tf_op jit(solution)/shard_map/ppermute | solution.py:34
  140.3 4.3 %collective-permute-done.16 = bf16[16,64,128]{2,1,0:T(8,128)(2,1)S(1)} collective-permute-done((bf16[16,64,128]{2,1,0:T(8,128)(2,1)S(1)}, bf16[16,64,128]{2,1,0:T(8,128)(2,1)S(1)}, u32[]{:S(2)}, u32[]{:S(2)}) %collective-permute-start.16) | collective-permute-done | bytes 262176 | tf_op jit(solution)/shard_map/ppermute | solution.py:34
  149.7 7.5 %rev.19 = f32[256,1024]{0,1:T(8,128)S(1)} reverse(f32[256,1024]{0,1:T(8,128)} %bitcast.227), dimensions={0} | reverse | bytes 2097152 | tf_op jit(solution)/shard_map/rev | solution.py:237
  157.2 1.6 bitcast_reduce_fusion
  159.1 2.3 convolution_convert_fusion.1
  165.5 36.3 %all_to_all.17 = bf16[32,2,4160]{2,1,0:T(2,128)(2,1)S(1)} all-to-all(bf16[32,2,4160]{2,1,0:T(2,128)(2,1)S(1)} %reshape.310), channel_id=1, replica_groups=mesh['dp'=16,'seq'=32] {'seq'}, dimensions={0} | all-to-all | bytes 1064960 | tf_op jit(solution)/shard_map/all_to_all | solution.py:178
  201.8 1.9 reshape.311
  203.6 3.6 %copy.107 = bf16[32,1,8320]{0,2,1:T(8,128)(2,1)S(1)} copy(bf16[32,1,8320]{2,1,0:T(2,128)(2,1)} %reshape.311) | data formatting | bytes 1064960 | tf_op jit(solution)/shard_map/all_to_all | solution.py:178
  208.9 23.6 %all_to_all.18 = bf16[32,8,1024]{2,1,0:T(8,128)(2,1)S(1)} all-to-all(bf16[32,8,1024]{2,1,0:T(8,128)(2,1)S(1)} %broadcast_in_dim.59), channel_id=1, replica_groups=mesh['dp'=16,'seq'=32] {'seq'}, dimensions={0} | all-to-all | bytes 1048576 | tf_op jit(solution)/shard_map/all_to_all | solution.py:190
  (177 shorter events, 39.1 us)
Async XLA Ops:
  7.2 154.3 %copy-start = (bf16[256,1024]{1,0:T(8,128)(2,1)S(1)}, bf16[256,1024]{1,0:T(8,128)(2,1)}, u32[]{:S(2)}) copy-start(bf16[256,1024]{1,0:T(8,128)(2,1)} %param.18) | copy-start | bytes 1572868
  7.2 151.9 %all-gather.2.cloned.1.call-start = ((), (), s32[]{:S(2)}) async-start(), calls=%async_computation.2 | async-start | bytes 2228224 | tf_op jit(solution)/shard_map/all_gather | solution.py:247
  9.3 16.5 %copy-start.17 = (f32[2,2,8,128]{3,2,1,0:T(8,128)}, f32[2,2,8,128]{3,2,1,0:T(8,128)S(1)}, u32[]{:S(2)}) copy-start(f32[2,2,8,128]{3,2,1,0:T(8,128)S(1)} %get-tuple-element.74) | copy-start | bytes 49156
  14.4 12.0 %copy-start.11 = (bf16[256,128]{1,0:T(8,128)(2,1)}, bf16[256,128]{1,0:T(8,128)(2,1)S(1)}, u32[]{:S(2)}) copy-start(bf16[256,128]{1,0:T(8,128)(2,1)S(1)} %get-tuple-element.73) | copy-start | bytes 196612
  16.4 34.0 %collective-permute-start.3 = (bf16[16,64,128]{2,1,0:T(8,128)(2,1)}, bf16[16,64,128]{2,1,0:T(8,128)(2,1)S(1)}, u32[]{:S(2)}, u32[]{:S(2)}) collective-permute-start(bf16[16,64,128]{2,1,0:T(8,128)(2,1)} %get-tuple-element.66), channel_id=1, source_target_pairs={{1,0},{2,1},{3,2},{4,3},{5,4},{6,5},{7,6},{8,7},{9,8},{10,9},{11,1... | collective-permute-start | bytes 786440 | tf_op jit(solution)/shard_map/ppermute | solution.py:34
  26.7 11.1 %copy-start.18 = (f32[2,2,8,128]{3,2,1,0:T(8,128)S(1)}, f32[2,2,8,128]{3,2,1,0:T(8,128)}, u32[]{:S(2)}) copy-start(f32[2,2,8,128]{3,2,1,0:T(8,128)} %copy-done.17) | copy-start | bytes 49156
  26.7 12.3 %copy-start.13 = (f32[2,16,128]{2,1,0:T(8,128)S(1)}, f32[2,16,128]{2,1,0:T(8,128)}, u32[]{:S(2)}) copy-start(f32[2,16,128]{2,1,0:T(8,128)} %copy-done.12) | copy-start | bytes 49156
  26.7 12.9 %copy-start.27 = (f32[16]{0:T(128)S(1)}, f32[16]{0:T(128)}, u32[]{:S(2)}) copy-start(f32[16]{0:T(128)} %copy-done.26) | copy-start | bytes 196
  26.7 13.0 %copy-start.16 = (f32[16,256]{1,0:T(8,128)S(1)}, f32[16,256]{1,0:T(8,128)}, u32[]{:S(2)}) copy-start(f32[16,256]{1,0:T(8,128)} %copy-done.15) | copy-start | bytes 49156
  26.7 14.2 %copy-start.33 = (f32[16]{0:T(128)S(1)}, f32[16]{0:T(128)}, u32[]{:S(2)}) copy-start(f32[16]{0:T(128)} %get-tuple-element.38) | copy-start | bytes 196
  27.8 22.6 %collective-permute-start.1 = (bf16[16,64,128]{2,1,0:T(8,128)(2,1)}, bf16[16,64,128]{2,1,0:T(8,128)(2,1)}, u32[]{:S(2)}, u32[]{:S(2)}) collective-permute-start(bf16[16,64,128]{2,1,0:T(8,128)(2,1)} %get-tuple-element.68), channel_id=1, source_target_pairs={{0,1},{1,2},{2,3},{3,4},{4,5},{5,6},{6,7},{7,8},{8,9},{9,10},{10,1... | collective-permute-start | bytes 786440 | tf_op jit(solution)/shard_map/ppermute | solution.py:34
  29.8 20.6 %collective-permute-start = (f32[16]{0:T(128)}, f32[16]{0:T(128)}, u32[]{:S(2)}, u32[]{:S(2)}) collective-permute-start(f32[16]{0:T(128)} %get-tuple-element.41), channel_id=1, source_target_pairs={{0,1},{1,2},{2,3},{3,4},{4,5},{5,6},{6,7},{7,8},{8,9},{9,10},{10,1... | collective-permute-start | bytes 200 | tf_op jit(solution)/shard_map/ppermute | solution.py:34
  31.7 18.7 %collective-permute-start.2 = (f32[16]{0:T(128)}, f32[16]{0:T(128)}, u32[]{:S(2)}, u32[]{:S(2)}) collective-permute-start(f32[16]{0:T(128)} %get-tuple-element.44), channel_id=1, source_target_pairs={{1,0},{2,1},{3,2},{4,3},{5,4},{6,5},{7,6},{8,7},{9,8},{10,9},{11,1... | collective-permute-start | bytes 200 | tf_op jit(solution)/shard_map/ppermute | solution.py:34
  51.3 17.5 %collective-permute-start.7 = (bf16[16,64,128]{2,1,0:T(8,128)(2,1)S(1)}, bf16[16,64,128]{2,1,0:T(8,128)(2,1)S(1)}, u32[]{:S(2)}, u32[]{:S(2)}) collective-permute-start(bf16[16,64,128]{2,1,0:T(8,128)(2,1)S(1)} %fusion.60), channel_id=1, source_target_pairs={{2,0},{3,1},{4,2},{5,3},{6,4},{7,5},{8,6},{9,7},{10,8},{11,9},{12,... | collective-permute-start | bytes 786440 | tf_op jit(solution)/shard_map/ppermute | solution.py:34
  54.3 14.5 %collective-permute-start.5 = (bf16[16,64,128]{2,1,0:T(8,128)(2,1)S(1)}, bf16[16,64,128]{2,1,0:T(8,128)(2,1)S(1)}, u32[]{:S(2)}, u32[]{:S(2)}) collective-permute-start(bf16[16,64,128]{2,1,0:T(8,128)(2,1)S(1)} %fusion.61), channel_id=1, source_target_pairs={{0,2},{1,3},{2,4},{3,5},{4,6},{5,7},{6,8},{7,9},{8,10},{9,11},{10,... | collective-permute-start | bytes 786440 | tf_op jit(solution)/shard_map/ppermute | solution.py:34
  60.8 6.8 %collective-permute-start.6 = (f32[16]{0:T(128)S(1)}, f32[16]{0:T(128)S(1)}, u32[]{:S(2)}, u32[]{:S(2)}) collective-permute-start(f32[16]{0:T(128)S(1)} %get-tuple-element.61), channel_id=1, source_target_pairs={{2,0},{3,1},{4,2},{5,3},{6,4},{7,5},{8,6},{9,7},{10,8},{11,9},{12,... | collective-permute-start | bytes 200 | tf_op jit(solution)/shard_map/ppermute | solution.py:34
  62.1 6.7 %collective-permute-start.4 = (f32[16]{0:T(128)S(1)}, f32[16]{0:T(128)S(1)}, u32[]{:S(2)}, u32[]{:S(2)}) collective-permute-start(f32[16]{0:T(128)S(1)} %get-tuple-element.65), channel_id=1, source_target_pairs={{0,2},{1,3},{2,4},{3,5},{4,6},{5,7},{6,8},{7,9},{8,10},{9,11},{10,... | collective-permute-start | bytes 200 | tf_op jit(solution)/shard_map/ppermute | solution.py:34
  69.0 31.3 %collective-permute-start.11 = (bf16[16,64,128]{2,1,0:T(8,128)(2,1)S(1)}, bf16[16,64,128]{2,1,0:T(8,128)(2,1)S(1)}, u32[]{:S(2)}, u32[]{:S(2)}) collective-permute-start(bf16[16,64,128]{2,1,0:T(8,128)(2,1)S(1)} %get-tuple-element.58), channel_id=1, source_target_pairs={{4,0},{5,1},{6,2},{7,3},{8,4},{9,5},{10,6},{11,7},{12,8},{13,9},{1... | collective-permute-start | bytes 786440 | tf_op jit(solution)/shard_map/ppermute | solution.py:34
  71.5 28.8 %collective-permute-start.9 = (bf16[16,64,128]{2,1,0:T(8,128)(2,1)S(1)}, bf16[16,64,128]{2,1,0:T(8,128)(2,1)S(1)}, u32[]{:S(2)}, u32[]{:S(2)}) collective-permute-start(bf16[16,64,128]{2,1,0:T(8,128)(2,1)S(1)} %get-tuple-element.62), channel_id=1, source_target_pairs={{0,4},{1,5},{2,6},{3,7},{4,8},{5,9},{6,10},{7,11},{8,12},{9,13},{1... | collective-permute-start | bytes 786440 | tf_op jit(solution)/shard_map/ppermute | solution.py:34
  80.0 20.3 %collective-permute-start.10 = (f32[16]{0:T(128)S(1)}, f32[16]{0:T(128)S(1)}, u32[]{:S(2)}, u32[]{:S(2)}) collective-permute-start(f32[16]{0:T(128)S(1)} %get-tuple-element.55), channel_id=1, source_target_pairs={{4,0},{5,1},{6,2},{7,3},{8,4},{9,5},{10,6},{11,7},{12,8},{13,9},{1... | collective-permute-start | bytes 200 | tf_op jit(solution)/shard_map/ppermute | solution.py:34
  81.3 19.0 %collective-permute-start.8 = (f32[16]{0:T(128)S(1)}, f32[16]{0:T(128)S(1)}, u32[]{:S(2)}, u32[]{:S(2)}) collective-permute-start(f32[16]{0:T(128)S(1)} %get-tuple-element.57), channel_id=1, source_target_pairs={{0,4},{1,5},{2,6},{3,7},{4,8},{5,9},{6,10},{7,11},{8,12},{9,13},{1... | collective-permute-start | bytes 200 | tf_op jit(solution)/shard_map/ppermute | solution.py:34
  100.4 25.9 %collective-permute-start.15 = (bf16[16,64,128]{2,1,0:T(8,128)(2,1)S(1)}, bf16[16,64,128]{2,1,0:T(8,128)(2,1)S(1)}, u32[]{:S(2)}, u32[]{:S(2)}) collective-permute-start(bf16[16,64,128]{2,1,0:T(8,128)(2,1)S(1)} %fusion.58), channel_id=1, source_target_pairs={{8,0},{9,1},{10,2},{11,3},{12,4},{13,5},{14,6},{15,7},{16,8},{17,9... | collective-permute-start | bytes 786440 | tf_op jit(solution)/shard_map/ppermute | solution.py:34
  101.9 24.4 %collective-permute-start.13 = (bf16[16,64,128]{2,1,0:T(8,128)(2,1)S(1)}, bf16[16,64,128]{2,1,0:T(8,128)(2,1)S(1)}, u32[]{:S(2)}, u32[]{:S(2)}) collective-permute-start(bf16[16,64,128]{2,1,0:T(8,128)(2,1)S(1)} %fusion.59), channel_id=1, source_target_pairs={{0,8},{1,9},{2,10},{3,11},{4,12},{5,13},{6,14},{7,15},{8,16},{9,17... | collective-permute-start | bytes 786440 | tf_op jit(solution)/shard_map/ppermute | solution.py:34
  112.7 12.3 %collective-permute-start.14 = (f32[16]{0:T(128)S(1)}, f32[16]{0:T(128)S(1)}, u32[]{:S(2)}, u32[]{:S(2)}) collective-permute-start(f32[16]{0:T(128)S(1)} %get-tuple-element.51), channel_id=1, source_target_pairs={{8,0},{9,1},{10,2},{11,3},{12,4},{13,5},{14,6},{15,7},{16,8},{17,9... | collective-permute-start | bytes 200 | tf_op jit(solution)/shard_map/ppermute | solution.py:34
  114.0 12.2 %collective-permute-start.12 = (f32[16]{0:T(128)S(1)}, f32[16]{0:T(128)S(1)}, u32[]{:S(2)}, u32[]{:S(2)}) collective-permute-start(f32[16]{0:T(128)S(1)} %get-tuple-element.53), channel_id=1, source_target_pairs={{0,8},{1,9},{2,10},{3,11},{4,12},{5,13},{6,14},{7,15},{8,16},{9,17... | collective-permute-start | bytes 200 | tf_op jit(solution)/shard_map/ppermute | solution.py:34
  126.3 19.6 %copy-start.8 = (f32[1,16,64,128]{3,2,1,0:T(8,128)S(1)}, f32[1,16,64,128]{3,2,1,0:T(8,128)}, u32[]{:S(2)}) copy-start(f32[1,16,64,128]{3,2,1,0:T(8,128)} %slice_add_fusion.1) | copy-start | bytes 1572868
  126.3 19.6 %copy-start.9 = (f32[2,128,16,64]{1,3,2,0:T(8,128)S(1)}, f32[2,128,16,64]{1,3,2,0:T(8,128)}, u32[]{:S(2)}) copy-start(f32[2,128,16,64]{1,3,2,0:T(8,128)} %convolution_bitcast_fusion.3) | copy-start | bytes 3145732
  126.3 19.6 %copy-start.10 = (bf16[256,128]{1,0:T(8,128)(2,1)S(1)}, bf16[256,128]{1,0:T(8,128)(2,1)}, u32[]{:S(2)}) copy-start(bf16[256,128]{1,0:T(8,128)(2,1)} %get-tuple-element.70) | copy-start | bytes 196612
  126.3 19.6 %copy-start.21 = (f32[2,128,16]{1,2,0:T(8,128)S(1)}, f32[2,128,16]{1,2,0:T(8,128)}, u32[]{:S(2)}) copy-start(f32[2,128,16]{1,2,0:T(8,128)} %exponential_bitcast_fusion.1) | copy-start | bytes 49156
  126.3 19.6 %copy-start.31 = (f32[2,16]{1,0:T(2,128)S(1)}, f32[2,16]{1,0:T(2,128)}, u32[]{:S(2)}) copy-start(f32[2,16]{1,0:T(2,128)} %pad_exponential_fusion.1) | copy-start | bytes 388
  126.5 13.8 %collective-permute-start.17 = (bf16[16,64,128]{2,1,0:T(8,128)(2,1)S(1)}, bf16[16,64,128]{2,1,0:T(8,128)(2,1)S(1)}, u32[]{:S(2)}, u32[]{:S(2)}) collective-permute-start(bf16[16,64,128]{2,1,0:T(8,128)(2,1)S(1)} %fusion.42), channel_id=1, source_target_pairs={{16,0},{17,1},{18,2},{19,3},{20,4},{21,5},{22,6},{23,7},{24,8},{25... | collective-permute-start | bytes 786440 | tf_op jit(solution)/shard_map/ppermute | solution.py:34
  128.2 16.4 %collective-permute-start.16 = (bf16[16,64,128]{2,1,0:T(8,128)(2,1)S(1)}, bf16[16,64,128]{2,1,0:T(8,128)(2,1)S(1)}, u32[]{:S(2)}, u32[]{:S(2)}) collective-permute-start(bf16[16,64,128]{2,1,0:T(8,128)(2,1)S(1)} %fusion.40), channel_id=1, source_target_pairs={{0,16},{1,17},{2,18},{3,19},{4,20},{5,21},{6,22},{7,23},{8,24},{9,... | collective-permute-start | bytes 786440 | tf_op jit(solution)/shard_map/ppermute | solution.py:34
  (21 other events, 87.9 us)
Sparse Core Ops, SparseCore 0:
  36.3 41.9 all-gather.1

commit v7 on v6

--- a/solution.py
+++ b/solution.py
@@ -39,6 +39,79 @@
             if k + 1 < rounds:
                 inclusive[i] = chain_combine(got, inclusive[i])
     return exclusive
+
+
+def split_wide(values):
+    rounded = lax.reduce_precision(values, exponent_bits=8, mantissa_bits=7)
+    low = (values - rounded).astype(jnp.bfloat16)
+    return rounded.astype(jnp.bfloat16), low
+
+
+def transposed_scans(forward_totals, backward_totals, axis):
+    count = lax.axis_size(axis)
+    head_count, head_size, state_size = forward_totals[1].shape
+    assert count % head_count == 0
+    per_head = count // head_count
+    chunk = head_size * state_size // per_head
+    head_of = jnp.arange(count, dtype=jnp.int32) // per_head
+
+    def pack(totals):
+        flat = totals[1].astype(jnp.bfloat16).reshape(count, chunk)
+        high, low = split_wide(totals[0][head_of])
+        tail = jnp.zeros((count, 128), jnp.bfloat16).at[:, 0].set(high).at[:, 1].set(low)
+        return jnp.concatenate([flat, tail], axis=1)
+
+    width = chunk + 128
+    got = lax.all_to_all(
+        jnp.concatenate([pack(forward_totals), pack(backward_totals)], axis=1),
+        axis,
+        0,
+        0,
+        tiled=True,
+    )
+
+    def unpack(block):
+        decay = block[:, chunk].astype(jnp.float32) + block[:, chunk + 1].astype(jnp.float32)
+        return decay, block[:, :chunk].astype(jnp.float32)
+
+    forward_decay, forward_parts = unpack(got[:, :width])
+    backward_decay, backward_parts = unpack(got[:, width:])
+    place = jnp.arange(count, dtype=jnp.int32)
+    dest = place[:, None, None]
+    source = place[None, :, None]
+    between = place[None, None, :]
+    forward_span = jnp.sum(
+        jnp.where((source < between) & (between < dest), forward_decay[None, None, :], 0.0),
+        axis=2,
+    )
+    forward_weight = jnp.where(place[None, :] < place[:, None], jnp.exp(forward_span), 0.0)
+    backward_span = jnp.sum(
+        jnp.where((dest < between) & (between < source), backward_decay[None, None, :], 0.0),
+        axis=2,
+    )
+    backward_weight = jnp.where(place[None, :] > place[:, None], jnp.exp(backward_span), 0.0)
+    forward_in = jnp.dot(
+        forward_weight, forward_parts, precision=lax.Precision.HIGHEST,
+        preferred_element_type=jnp.float32,
+    )
+    backward_in = jnp.dot(
+        backward_weight, backward_parts, precision=lax.Precision.HIGHEST,
+        preferred_element_type=jnp.float32,
+    )
+    returned = lax.all_to_all(
+        jnp.concatenate(
+            [forward_in.astype(jnp.bfloat16), backward_in.astype(jnp.bfloat16)], axis=1
+        ),
+        axis,
+        0,
+        0,
+        tiled=True,
+    )
+    shape = (head_count, head_size, state_size)
+    return (
+        returned[:, :chunk].astype(jnp.float32).reshape(shape),
+        returned[:, chunk:].astype(jnp.float32).reshape(shape),
+    )
 
 
 def block_pass(x_seq, dt_seq, b_seq, c_seq, forget_rate):
@@ -154,12 +227,6 @@
     return rows
 
 
-def split_wide(values):
-    rounded = lax.reduce_precision(values, exponent_bits=8, mantissa_bits=7)
-    low = (values - rounded).astype(jnp.bfloat16)
-    return rounded.astype(jnp.bfloat16), low
-
-
 def all_to_all_pool(local, axis):
     count = lax.axis_size(axis)
     local_top, weight_sum, weighted_sum = local
@@ -230,9 +297,7 @@
         projections[::-1, 3 * state_size :],
         decay_rates[1],
     )
-    (unused_item, forward_in), (unused_item, backward_in) = exclusive_scans(
-        [(forward_totals, False), (backward_totals, True)], "seq"
-    )
+    forward_in, backward_in = transposed_scans(forward_totals, backward_totals, "seq")
     forward_out = apply_state(forward_records, forward_in)
     backward_out = apply_state(backward_records, backward_in)[::-1]
     skip_wide = jnp.repeat(skip_gain, head_size)

time: 242 us -> 192 us (0.79)
  the two profiles are of different devices: /device:TPU:8 before, /device:TPU:6 now
where the time goes in v7:
time: 192 us; the launch traced here: 189 us
  blocking collectives  49 us (26%)
  local copies, waits for them, and re-layouts  42.1 us (22%)
  waiting for transfers between devices  28.9 us (15%)
  starting transfers between devices  21.7 us (11%)
  other arithmetic  19.7 us (10%)
  between operations  15.5 us (8%)
  matrix products  11.8 us (6%)
    all_to_all x1, blocking collectives, all_to_all_pool(): moved = lax.all_to_all(packed, axis, 0, 0, tiled=True)  25.1 us
    all_to_all x1, blocking collectives, all_to_all_pool(): gathered = lax.all_to_all(spread_rows, axis, 0, 0, tiled=True)  23.8 us
    all_to_all x1, starting transfers between devices, transposed_scans(): lax.all_to_all(jnp.concatenate([pack(forward_totals), pack(backward_total...  16 us
    all_to_all x1, waiting for transfers between devices, transposed_scans(): lax.all_to_all(jnp.concatenate([pack(forward_totals), pack(backward_total...  15.7 us
    all_to_all x1, waiting for transfers between devices, transposed_scans(): lax.all_to_all(jnp.concatenate([forward_in.astype(jnp.bfloat16), backward...  12.5 us
    unnamed x60, local copies, waits for them, and re-layouts  11.7 us
    rev x1, local copies, waits for them, and re-layouts, body(): backward_out = apply_state(backward_records, backward_in)[::-1]  7.5 us
    all_to_all x1, starting transfers between devices, transposed_scans(): lax.all_to_all(jnp.concatenate([forward_in.astype(jnp.bfloat16), backward...  5.74 us
  transfers between devices with their start and end apart: 3, of which 2 were waited for; matrix products, arithmetic and copies ran while one was open for 16% of the time, Pallas kernels for 0%

profile of v7, /device:TPU:6, one launch (start us, length us, event | category | flops | bytes accessed | tf_op | source)
XLA Modules:
  0.0 188.8 jit_solution(14140317284710261840)
XLA Ops:
  14.1 1.2 copy.161
  17.0 0.9 broadcast_add_fusion.1
  19.0 0.9 mul.251
  23.3 1.1 fusion.83
  24.4 2.0 %squeeze.19 = f32[32,4096]{1,0:T(8,128)} reshape(f32[1,16,64,128]{3,2,1,0:T(8,128)} %get-tuple-element.69) | data formatting | bytes 1048576 | tf_op jit(solution)/shard_map/squeeze | solution.py:153
  28.4 0.9 mul.260
  30.9 1.3 fusion.60
  32.2 1.3 fusion.59
  33.8 1.4 add_convert_fusion.5
  36.1 1.0 reduce.48
  37.2 0.9 reshape.568
  38.1 16.0 %all-to-all-start = ((bf16[32,2,4224]{2,1,0:T(2,128)(2,1)}), bf16[32,2,4224]{2,1,0:T(2,128)(2,1)S(1)}, u32[]{:S(2)}, u32[]{:S(2)}) async-start(bf16[32,2,4224]{2,1,0:T(2,128)(2,1)} %reshape.568), calls=%async_computation | async-start | bytes 1081344 | tf_op jit(solution)/shard_map/all_to_all | solution.py:65
  57.8 15.7 %all-to-all-done = bf16[32,2,4224]{2,1,0:T(2,128)(2,1)S(1)} async-done(((bf16[32,2,4224]{2,1,0:T(2,128)(2,1)}), bf16[32,2,4224]{2,1,0:T(2,128)(2,1)S(1)}, u32[]{:S(2)}, u32[]{:S(2)}) %all-to-all-start) | async-done | bytes 540704 | tf_op jit(solution)/shard_map/all_to_all | solution.py:65
  75.4 1.1 reduce.49
  76.5 1.2 reshape.570
  77.7 5.7 %all-to-all-start.1 = ((bf16[32,2,4096]{2,1,0:T(2,128)(2,1)}), bf16[32,2,4096]{2,1,0:T(2,128)(2,1)S(1)}, u32[]{:S(2)}, u32[]{:S(2)}) async-start(bf16[32,2,4096]{2,1,0:T(2,128)(2,1)} %reshape.570), calls=%async_computation.1 | async-start | bytes 1048576 | tf_op jit(solution)/shard_map/all_to_all | solution.py:101
  84.1 1.0 copy.181
  85.6 1.9 %convolution_bitcast_fusion.3 = f32[2,128,16,64]{1,3,2,0:T(8,128)} fusion(f32[2,16,128]{2,1,0:T(8,128)S(1)} %bitcast.241, f32[2,16,128]{2,1,0:T(8,128)S(1)} %reduce_window_sum.17, f32[2,128,128]{2,1,0:T(8,128)S(1)} %fusion.85, pred[128,128]{1,0:T(8,128)(4,1)S(1)} %copy-done.14, bf16[2,128,16,64]{1,0,3,2:T(2,128)(2,1)S(1)} %reshape_reshape_squeeze.3), kind=kOutput, calls=%fused_computation.15 | convolution fusion | flops 69730304 | bytes 1753088 | tf_op jit(solution)/shard_map/chqk,ckhp->cqhp/dot_general | solution.py:137
  87.6 1.9 %convolution_bitcast_fusion.2 = f32[2,128,16,64]{1,3,2,0:T(8,128)} fusion(f32[2,16,128]{2,1,0:T(8,128)S(1)} %copy-done.15, f32[2,16,128]{2,1,0:T(8,128)S(1)} %reduce_window_sum.18, f32[2,128,128]{2,1,0:T(8,128)S(1)} %fusion.86, pred[128,128]{1,0:T(8,128)(4,1)S(1)} %copy-done.14, bf16[256,16,64]{0,2,1:T(8,128)(2,1)S(1)} %copy-done.2), kind=kOutput, calls=%fused_computation.14 | convolution fusion | flops 69730304 | bytes 1753088 | tf_op jit(solution)/shard_map/chqk,ckhp->cqhp/dot_general | solution.py:137
  89.5 12.5 %all-to-all-done.1 = bf16[32,2,4096]{2,1,0:T(2,128)(2,1)S(1)} async-done(((bf16[32,2,4096]{2,1,0:T(2,128)(2,1)}), bf16[32,2,4096]{2,1,0:T(2,128)(2,1)S(1)}, u32[]{:S(2)}, u32[]{:S(2)}) %all-to-all-start.1) | async-done | bytes 524320 | tf_op jit(solution)/shard_map/all_to_all | solution.py:101
  103.6 1.6 fusion.2
  106.1 1.7 fusion.4
  108.7 1.1 copy.224
  109.7 7.5 %rev.19 = f32[256,1024]{0,1:T(8,128)S(1)} reverse(f32[256,1024]{0,1:T(8,128)} %bitcast.225), dimensions={0} | reverse | bytes 2097152 | tf_op jit(solution)/shard_map/rev | solution.py:302
  117.3 1.6 bitcast_reduce_fusion
  119.2 2.3 %convolution_convert_fusion.3 = bf16[256,1024]{1,0:T(8,128)(2,1)S(1)} fusion(bf16[256,1024]{0,1:T(8,128)(2,1)S(1)} %fusion.12, bf16[1024,1024]{1,0:T(8,128)(2,1)} %all-gather.2.cloned.1.call-done), kind=kOutput, calls=%fused_computation.19 | convolution fusion | flops 537133056 | bytes 3145728 | tf_op jit(solution)/shard_map/dot_general | solution.py:310
  123.6 1.0 reduce.50
  125.0 25.1 %all_to_all.41 = bf16[32,2,4160]{2,1,0:T(2,128)(2,1)S(1)} all-to-all(bf16[32,2,4160]{2,1,0:T(2,128)(2,1)S(1)} %reshape.572), channel_id=1, replica_groups=mesh['dp'=16,'seq'=32] {'seq'}, dimensions={0} | all-to-all | bytes 1064960 | tf_op jit(solution)/shard_map/all_to_all | solution.py:245
  150.1 1.8 reshape.573
  152.0 3.6 %copy.188 = bf16[32,1,8320]{0,2,1:T(8,128)(2,1)S(1)} copy(bf16[32,1,8320]{2,1,0:T(2,128)(2,1)} %reshape.573) | data formatting | bytes 1064960 | tf_op jit(solution)/shard_map/all_to_all | solution.py:245
  156.0 1.2 fusion
  157.3 23.8 %all_to_all.42 = bf16[32,8,1024]{2,1,0:T(8,128)(2,1)S(1)} all-to-all(bf16[32,8,1024]{2,1,0:T(8,128)(2,1)S(1)} %broadcast_in_dim.140), channel_id=1, replica_groups=mesh['dp'=16,'seq'=32] {'seq'}, dimensions={0} | all-to-all | bytes 1048576 | tf_op jit(solution)/shard_map/all_to_all | solution.py:257
  (149 shorter events, 30.8 us)
Async XLA Ops:
  7.2 114.3 %copy-start = (bf16[256,1024]{1,0:T(8,128)(2,1)S(1)}, bf16[256,1024]{1,0:T(8,128)(2,1)}, u32[]{:S(2)}) copy-start(bf16[256,1024]{1,0:T(8,128)(2,1)} %param.26) | copy-start | bytes 1572868
  7.2 8.3 %copy-start.11 = (bf16[1,256,512]{2,1,0:T(8,128)(2,1)S(1)}, bf16[1,256,512]{2,1,0:T(8,128)(2,1)}, u32[]{:S(2)}) copy-start(bf16[1,256,512]{2,1,0:T(8,128)(2,1)} %param.20) | copy-start | bytes 786436
  7.9 0.6 copy-start.16
  21.5 2.9 %copy-start.1 = (bf16[256,16,64]{0,2,1:T(8,128)(2,1)}, bf16[256,16,64]{0,2,1:T(8,128)(2,1)S(1)}, u32[]{:S(2)}) copy-start(bf16[256,16,64]{0,2,1:T(8,128)(2,1)S(1)} %rev.16) | copy-start | bytes 1572868
  27.3 6.5 %copy-start.4 = (f32[32,4096]{1,0:T(8,128)S(1)}, f32[32,4096]{1,0:T(8,128)}, u32[]{:S(2)}) copy-start(f32[32,4096]{1,0:T(8,128)} %squeeze.18) | copy-start | bytes 1572868
  29.3 5.9 %copy-start.5 = (f32[32,4096]{1,0:T(8,128)S(1)}, f32[32,4096]{1,0:T(8,128)}, u32[]{:S(2)}) copy-start(f32[32,4096]{1,0:T(8,128)} %squeeze.19) | copy-start | bytes 1572868
  33.7 1.5 copy-start.6
  33.8 1.5 copy-start.7
  33.8 1.7 copy-start.8
  38.1 35.4 %all-to-all-start = ((bf16[32,2,4224]{2,1,0:T(2,128)(2,1)}), bf16[32,2,4224]{2,1,0:T(2,128)(2,1)S(1)}, u32[]{:S(2)}, u32[]{:S(2)}) async-start(bf16[32,2,4224]{2,1,0:T(2,128)(2,1)} %reshape.568), calls=%async_computation | async-start | bytes 1081344 | tf_op jit(solution)/shard_map/all_to_all | solution.py:65
  54.1 65.1 %all-gather.2.cloned.1.call-start = ((), (), s32[]{:S(2)}) async-start(), calls=%async_computation.4 | async-start | bytes 2228224 | tf_op jit(solution)/shard_map/all_gather | solution.py:312
  75.3 8.1 %copy-start.22 = (f32[16]{0:T(128)S(1)}, f32[16]{0:T(128)}, u32[]{:S(2)}) copy-start(f32[16]{0:T(128)} %get-tuple-element.56) | copy-start | bytes 196
  75.3 8.8 %copy-start.10 = (bf16[1,256,1024]{2,1,0:T(8,128)(2,1)S(1)}, bf16[1,256,1024]{2,1,0:T(8,128)(2,1)}, u32[]{:S(2)}) copy-start(bf16[1,256,1024]{2,1,0:T(8,128)(2,1)} %param.19) | copy-start | bytes 1572868
  75.4 9.7 %copy-start.21 = (f32[16]{0:T(128)S(1)}, f32[16]{0:T(128)}, u32[]{:S(2)}) copy-start(f32[16]{0:T(128)} %param.23) | copy-start | bytes 196
  76.5 9.2 %copy-start.14 = (pred[128,128]{1,0:T(8,128)(4,1)S(1)}, pred[128,128]{1,0:T(8,128)(4,1)}, u32[]{:S(2)}) copy-start(pred[128,128]{1,0:T(8,128)(4,1)} %iota_compare_fusion.1) | copy-start | bytes 49156
  77.7 24.4 %all-to-all-start.1 = ((bf16[32,2,4096]{2,1,0:T(2,128)(2,1)}), bf16[32,2,4096]{2,1,0:T(2,128)(2,1)S(1)}, u32[]{:S(2)}, u32[]{:S(2)}) async-start(bf16[32,2,4096]{2,1,0:T(2,128)(2,1)} %reshape.570), calls=%async_computation.1 | async-start | bytes 1048576 | tf_op jit(solution)/shard_map/all_to_all | solution.py:101
  85.6 2.0 %copy-start.2 = (bf16[256,16,64]{0,2,1:T(8,128)(2,1)S(1)}, bf16[256,16,64]{0,2,1:T(8,128)(2,1)}, u32[]{:S(2)}) copy-start(bf16[256,16,64]{0,2,1:T(8,128)(2,1)} %copy-done.1) | copy-start | bytes 1572868
  85.6 2.0 %copy-start.15 = (f32[2,16,128]{2,1,0:T(8,128)S(1)}, f32[2,16,128]{2,1,0:T(8,128)}, u32[]{:S(2)}) copy-start(f32[2,16,128]{2,1,0:T(8,128)} %bitcast_bitcast_fusion.1) | copy-start | bytes 49156
  102.6 1.0 copy-start.9
  102.6 1.0 copy-start.13
  102.6 1.0 copy-start.19
  105.2 0.9 copy-start.12
  105.2 0.9 copy-start.20
  117.2 1.6 copy-start.18
  118.9 2.6 %copy-start.17 = (pred[256]{0:T(512)(128)(4,1)S(1)}, pred[256]{0:T(512)(128)(4,1)}, u32[]{:S(2)}) copy-start(pred[256]{0:T(512)(128)(4,1)} %copy-done.16) | copy-start | bytes 772
  121.5 0.8 copy-start.3
Sparse Core Ops, SparseCore 0:
  57.0 46.4 all-gather.1

commit v8 on v7

--- a/solution.py
+++ b/solution.py
@@ -114,7 +114,7 @@
     )
 
 
-def block_pass(x_seq, dt_seq, b_seq, c_seq, forget_rate):
+def block_pass(x_seq, dt_seq, b_seq, c_seq, forget_rate, reverse):
     row_count, head_count, head_size = x_seq.shape
     state_size = b_seq.shape[1]
     block_count = row_count // BLOCK
@@ -122,12 +122,15 @@
     dt_blocks = dt_seq.reshape(head_count, block_count, BLOCK).transpose(1, 0, 2)
     b_blocks = b_seq.reshape(block_count, BLOCK, state_size)
     c_blocks = c_seq.reshape(block_count, BLOCK, state_size)
-    cumulative = jnp.cumsum(-dt_blocks * forget_rate[None, :, None], axis=2)
+    cumulative = lax.cumsum(-dt_blocks * forget_rate[None, :, None], axis=2, reverse=reverse)
     gram_matrix = jnp.einsum(
         "cqn,ckn->cqk", c_blocks, b_blocks, preferred_element_type=jnp.float32
     )
     symbol_offset = jnp.arange(BLOCK, dtype=jnp.int32)
-    causal = symbol_offset[:, None] >= symbol_offset[None, :]
+    if reverse:
+        causal = symbol_offset[:, None] <= symbol_offset[None, :]
+    else:
+        causal = symbol_offset[:, None] >= symbol_offset[None, :]
     spread = jnp.where(
         causal[None, None], cumulative[:, :, :, None] - cumulative[:, :, None, :], -jnp.inf
     )
@@ -137,7 +140,7 @@
     intra_out = jnp.einsum(
         "chqk,ckhp->cqhp", mixing, x_blocks, preferred_element_type=jnp.float32
     )
-    block_end = cumulative[:, :, -1]
+    block_end = cumulative[:, :, 0] if reverse else cumulative[:, :, -1]
     tail_weight = jnp.exp(block_end[:, :, None] - cumulative) * dt_blocks
     scaled_x = (x_blocks * tail_weight.transpose(0, 2, 1)[:, :, :, None]).astype(jnp.bfloat16)
     contrib = jnp.einsum(
@@ -145,11 +148,12 @@
     )
     decay_sum = jnp.zeros((head_count,), jnp.float32)
     running = jnp.zeros((head_count, head_size, state_size), jnp.float32)
-    decay_sums = []
-    runnings = []
-    for c in range(block_count):
-        decay_sums.append(decay_sum)
-        runnings.append(running)
+    decay_sums = [None] * block_count
+    runnings = [None] * block_count
+    order = range(block_count - 1, -1, -1) if reverse else range(block_count)
+    for c in order:
+        decay_sums[c] = decay_sum
+        runnings[c] = running
         running = jnp.exp(block_end[c])[:, None, None] * running + contrib[c]
         decay_sum = decay_sum + block_end[c]
     records = (intra_out, cumulative, jnp.stack(decay_sums), jnp.stack(runnings), c_blocks)
@@ -289,17 +293,19 @@
         projections[:, :state_size],
         projections[:, state_size : 2 * state_size],
         decay_rates[0],
+        False,
     )
     backward_totals, backward_records = block_pass(
-        tokens[::-1],
-        step_size[head_count:, ::-1],
-        projections[::-1, 2 * state_size : 3 * state_size],
-        projections[::-1, 3 * state_size :],
+        tokens,
+        step_size[head_count:],
+        projections[:, 2 * state_size : 3 * state_size],
+        projections[:, 3 * state_size :],
         decay_rates[1],
+        True,
     )
     forward_in, backward_in = transposed_scans(forward_totals, backward_totals, "seq")
     forward_out = apply_state(forward_records, forward_in)
-    backward_out = apply_state(backward_records, backward_in)[::-1]
+    backward_out = apply_state(backward_records, backward_in)
     skip_wide = jnp.repeat(skip_gain, head_size)
     mixed_out = forward_out + backward_out + skip_wide[None, :] * flat_tokens.astype(jnp.float32)
     gated_out = mixed_out * jax.nn.silu(gate_input[0].astype(jnp.float32))

time: 192 us -> 182 us (0.948)
  local copies, waits for them, and re-layouts: 42.1 us -> 33.9 us
    rev x5 -> x0, local copies, waits for them, and re-layouts: 9.08 us -> none  [the longest x1 7.5 us: body(): backward_out = apply_state(backward_records, backward_in)[::-1]]
    unnamed x60 -> x49, local copies, waits for them, and re-layouts: 11.7 us -> 15.1 us
    another operation x6 -> x5, other arithmetic: 5.08 us -> 5.68 us  [the longest x2 3.06 us: block_pass(): lax.cumsum(-dt_blocks * forget_rate[None, :, None], axis=2, reverse=reverse)]
  transfers between devices with their start and end apart: 3 -> 3, of which waited for: 2 -> 2; matrix products, arithmetic and copies ran while one was open for 16% -> 14% of each run, Pallas kernels for 0% -> 0%
where the time goes in v8:
time: 182 us; the launch traced here: 180 us
  blocking collectives  48.6 us (27%)
  local copies, waits for them, and re-layouts  33.9 us (19%)
  waiting for transfers between devices  30.2 us (17%)
  starting transfers between devices  22.1 us (12%)
  other arithmetic  18.2 us (10%)
  between operations  15.4 us (8%)
  matrix products  11.4 us (6%)
    all_to_all x1, blocking collectives, all_to_all_pool(): moved = lax.all_to_all(packed, axis, 0, 0, tiled=True)  24.6 us
    all_to_all x1, blocking collectives, all_to_all_pool(): gathered = lax.all_to_all(spread_rows, axis, 0, 0, tiled=True)  24 us
    all_to_all x1, waiting for transfers between devices, transposed_scans(): lax.all_to_all(jnp.concatenate([pack(forward_totals), pack(backward_total...  16.8 us
    all_to_all x1, starting transfers between devices, transposed_scans(): lax.all_to_all(jnp.concatenate([pack(forward_totals), pack(backward_total...  16.1 us
    unnamed x49, local copies, waits for them, and re-layouts  15.1 us
    all_to_all x1, waiting for transfers between devices, transposed_scans(): lax.all_to_all(jnp.concatenate([forward_in.astype(jnp.bfloat16), backward...  12.7 us
    all_to_all x1, starting transfers between devices, transposed_scans(): lax.all_to_all(jnp.concatenate([forward_in.astype(jnp.bfloat16), backward...  6 us
    mul x8, local copies, waits for them, and re-layouts, block_pass(): running = jnp.exp(block_end[c])[:, None, None] * running + contrib[c]  3.99 us
  transfers between devices with their start and end apart: 3, of which 2 were waited for; matrix products, arithmetic and copies ran while one was open for 14% of the time, Pallas kernels for 0%

profile of v8, /device:TPU:6, one launch (start us, length us, event | category | flops | bytes accessed | tf_op | source)
XLA Modules:
  0.0 179.8 jit_solution(8267473472697553993)
XLA Ops:
  11.0 2.5 %reduce_window_sum.21 = f32[2,16,128]{2,1,0:T(8,128)S(1)} reduce-window(f32[2,16,128]{2,1,0:T(8,128)S(1)} %negate_multiply_fusion, f32[]{:T(128)} %constant.131.clone.1), window={size=1x1x128 pad=0_0x0_0x0_127}, to_apply=%region_3.4 | reduce-window | flops 520192 | bytes 32772 | tf_op jit(solution)/shard_map/block_pass/reduce_window_sum | solution.py:125
  15.1 1.2 copy.146
  16.9 0.9 broadcast_add_fusion.1
  18.1 0.9 mul.267
  19.1 0.9 mul.263
  20.3 1.1 fusion.92
  21.4 2.0 %squeeze.19 = f32[32,4096]{1,0:T(8,128)} reshape(f32[1,16,64,128]{3,2,1,0:T(8,128)} %get-tuple-element.67) | data formatting | bytes 1048576 | tf_op jit(solution)/shard_map/squeeze | solution.py:157
  23.4 0.9 squeeze.20
  24.4 0.9 mul.280
  27.8 1.3 fusion.69
  29.4 1.4 add_convert_fusion.5
  31.8 1.0 reduce.49
  32.8 1.0 reshape.589
  33.7 16.1 %all-to-all-start = ((bf16[32,2,4224]{2,1,0:T(2,128)(2,1)}), bf16[32,2,4224]{2,1,0:T(2,128)(2,1)}, u32[]{:S(2)}, u32[]{:S(2)}) async-start(bf16[32,2,4224]{2,1,0:T(2,128)(2,1)} %reshape.589), calls=%async_computation | async-start | bytes 1081344 | tf_op jit(solution)/shard_map/all_to_all | solution.py:65
  52.4 16.8 %all-to-all-done = bf16[32,2,4224]{2,1,0:T(2,128)(2,1)} async-done(((bf16[32,2,4224]{2,1,0:T(2,128)(2,1)}), bf16[32,2,4224]{2,1,0:T(2,128)(2,1)}, u32[]{:S(2)}, u32[]{:S(2)}) %all-to-all-start) | async-done | bytes 540704 | tf_op jit(solution)/shard_map/all_to_all | solution.py:65
  69.2 3.7 %reshape.590 = bf16[32,1,8448]{2,1,0:T(2,128)(2,1)S(1)} reshape(bf16[32,2,4224]{2,1,0:T(2,128)(2,1)} %all-to-all-done) | data formatting | bytes 1081344
  74.3 1.0 reduce.50
  75.3 1.2 reshape.591
  76.5 6.0 %all-to-all-start.1 = ((bf16[32,2,4096]{2,1,0:T(2,128)(2,1)}), bf16[32,2,4096]{2,1,0:T(2,128)(2,1)}, u32[]{:S(2)}, u32[]{:S(2)}) async-start(bf16[32,2,4096]{2,1,0:T(2,128)(2,1)} %reshape.591), calls=%async_computation.1 | async-start | bytes 1048576 | tf_op jit(solution)/shard_map/all_to_all | solution.py:101
  82.7 1.5 reshape.554
  84.8 1.9 %convolution_bitcast_fusion.2 = f32[2,128,16,64]{1,3,2,0:T(8,128)} fusion(f32[2,16,128]{2,1,0:T(8,128)S(1)} %copy-done.13, f32[2,16,128]{2,1,0:T(8,128)S(1)} %reduce_window_sum.21, f32[2,128,128]{2,1,0:T(8,128)S(1)} %fusion.95, pred[128,128]{1,0:T(8,128)(4,1)S(1)} %copy-done.11, bf16[2,128,16,64]{1,0,3,2:T(2,128)(2,1)S(1)} %reshape_reshape_squeeze.4), kind=kOutput, calls=%fused_computation.18 | convolution fusion | flops 69730304 | bytes 1753088 | tf_op jit(solution)/shard_map/chqk,ckhp->cqhp/dot_general | solution.py:140
  86.7 1.9 %convolution_bitcast_fusion.3 = f32[2,128,16,64]{1,3,2,0:T(8,128)} fusion(f32[2,16,128]{2,1,0:T(8,128)S(1)} %copy-done.12, f32[2,16,128]{2,1,0:T(8,128)S(1)} %reduce_window_sum.20, f32[2,128,128]{2,1,0:T(8,128)S(1)} %fusion.94, pred[128,128]{1,0:T(8,128)(4,1)S(1)} %copy-done.10, bf16[2,128,16,64]{1,0,3,2:T(2,128)(2,1)S(1)} %reshape_reshape_squeeze.4), kind=kOutput, calls=%fused_computation.19 | convolution fusion | flops 69730304 | bytes 1753088 | tf_op jit(solution)/shard_map/chqk,ckhp->cqhp/dot_general | solution.py:140
  88.6 12.7 %all-to-all-done.1 = bf16[32,2,4096]{2,1,0:T(2,128)(2,1)} async-done(((bf16[32,2,4096]{2,1,0:T(2,128)(2,1)}), bf16[32,2,4096]{2,1,0:T(2,128)(2,1)}, u32[]{:S(2)}, u32[]{:S(2)}) %all-to-all-start.1) | async-done | bytes 524320 | tf_op jit(solution)/shard_map/all_to_all | solution.py:101
  101.3 3.6 %reshape.592 = bf16[32,1,8192]{2,1,0:T(2,128)(2,1)S(1)} reshape(bf16[32,2,4096]{2,1,0:T(2,128)(2,1)} %all-to-all-done.1) | data formatting | bytes 1048576
  106.6 2.0 %fusion.5 = f32[2,128,16,64]{1,3,2,0:T(8,128)S(1)} fusion(f32[2,128,16,64]{1,3,2,0:T(8,128)} %convolution_bitcast_fusion.2, bf16[2,128,128,1]{2,1,3,0:T(8,128)(2,1)S(1)} %bitcast.220, f32[1,16,64,128]{3,2,1,0:T(8,128)} %get-tuple-element.68, f32[2,128,16]{1,2,0:T(8,128)S(1)} %exponential_bitcast_fusion, f32[16,64,128]{2,1,0:T(8,128)} %reshape.551, ...), kind=kOutput, calls=%fused_computation.17 | convolution fusion | flops 68419584 | bytes 3227776 | tf_op jit(solution)/shard_map/cqn,chpn->cqhp/dot_general | solution.py:169
  111.1 2.3 %convolution_convert_fusion.3 = bf16[256,1024]{1,0:T(8,128)(2,1)S(1)} fusion(bf16[256,1024]{0,1:T(8,128)(2,1)S(1)} %fusion.16, bf16[1024,1024]{1,0:T(8,128)(2,1)} %all-gather.2.cloned.1.call-done), kind=kOutput, calls=%fused_computation.21 | convolution fusion | flops 537133056 | bytes 3145728 | tf_op jit(solution)/shard_map/dot_general | solution.py:316
  115.0 1.0 reduce.51
  116.4 24.6 %all_to_all.41 = bf16[32,2,4160]{2,1,0:T(2,128)(2,1)S(1)} all-to-all(bf16[32,2,4160]{2,1,0:T(2,128)(2,1)S(1)} %reshape.593), channel_id=1, replica_groups=mesh['dp'=16,'seq'=32] {'seq'}, dimensions={0} | all-to-all | bytes 1064960 | tf_op jit(solution)/shard_map/all_to_all | solution.py:249
  141.0 1.8 %reshape.594 = bf16[32,1,8320]{2,1,0:T(2,128)(2,1)} reshape(bf16[32,2,4160]{2,1,0:T(2,128)(2,1)S(1)} %all_to_all.41) | data formatting | bytes 1064960
  142.8 3.6 %copy.171 = bf16[32,1,8320]{0,2,1:T(8,128)(2,1)S(1)} copy(bf16[32,1,8320]{2,1,0:T(2,128)(2,1)} %reshape.594) | data formatting | bytes 1064960 | tf_op jit(solution)/shard_map/all_to_all | solution.py:249
  146.8 1.2 fusion
  148.1 24.0 %all_to_all.42 = bf16[32,8,1024]{2,1,0:T(8,128)(2,1)S(1)} all-to-all(bf16[32,8,1024]{2,1,0:T(8,128)(2,1)S(1)} %broadcast_in_dim.141), channel_id=1, replica_groups=mesh['dp'=16,'seq'=32] {'seq'}, dimensions={0} | all-to-all | bytes 1048576 | tf_op jit(solution)/shard_map/all_to_all | solution.py:261
  (126 shorter events, 21.6 us)
Async XLA Ops:
  7.2 106.2 %copy-start = (bf16[256,1024]{1,0:T(8,128)(2,1)S(1)}, bf16[256,1024]{1,0:T(8,128)(2,1)}, u32[]{:S(2)}) copy-start(bf16[256,1024]{1,0:T(8,128)(2,1)} %param.26) | copy-start | bytes 1572868
  7.2 9.3 %copy-start.9 = (bf16[1,256,512]{2,1,0:T(8,128)(2,1)S(1)}, bf16[1,256,512]{2,1,0:T(8,128)(2,1)}, u32[]{:S(2)}) copy-start(bf16[1,256,512]{2,1,0:T(8,128)(2,1)} %param.20) | copy-start | bytes 786436
  26.3 4.6 %copy-start.2 = (f32[32,4096]{1,0:T(8,128)S(1)}, f32[32,4096]{1,0:T(8,128)}, u32[]{:S(2)}) copy-start(f32[32,4096]{1,0:T(8,128)} %squeeze.19) | copy-start | bytes 1572868
  29.4 1.5 copy-start.3
  29.4 1.5 copy-start.4
  29.4 1.7 copy-start.5
  33.7 35.5 %all-to-all-start = ((bf16[32,2,4224]{2,1,0:T(2,128)(2,1)}), bf16[32,2,4224]{2,1,0:T(2,128)(2,1)}, u32[]{:S(2)}, u32[]{:S(2)}) async-start(bf16[32,2,4224]{2,1,0:T(2,128)(2,1)} %reshape.589), calls=%async_computation | async-start | bytes 1081344 | tf_op jit(solution)/shard_map/all_to_all | solution.py:65
  49.8 61.3 %all-gather.2.cloned.1.call-start = ((), (), s32[]{:S(2)}) async-start(), calls=%async_computation.4 | async-start | bytes 2228224 | tf_op jit(solution)/shard_map/all_gather | solution.py:318
  74.2 8.3 %copy-start.16 = (f32[16]{0:T(128)S(1)}, f32[16]{0:T(128)}, u32[]{:S(2)}) copy-start(f32[16]{0:T(128)} %get-tuple-element.52) | copy-start | bytes 196
  74.3 8.3 %copy-start.7 = (bf16[1,256,1024]{2,1,0:T(8,128)(2,1)S(1)}, bf16[1,256,1024]{2,1,0:T(8,128)(2,1)}, u32[]{:S(2)}) copy-start(bf16[1,256,1024]{2,1,0:T(8,128)(2,1)} %param.19) | copy-start | bytes 1572868
  76.5 7.8 %copy-start.15 = (f32[16]{0:T(128)S(1)}, f32[16]{0:T(128)}, u32[]{:S(2)}) copy-start(f32[16]{0:T(128)} %param.23) | copy-start | bytes 196
  76.5 8.3 %copy-start.11 = (pred[128,128]{1,0:T(8,128)(4,1)S(1)}, pred[128,128]{1,0:T(8,128)(4,1)}, u32[]{:S(2)}) copy-start(pred[128,128]{1,0:T(8,128)(4,1)} %iota_compare_fusion.1) | copy-start | bytes 49156
  76.5 8.3 %copy-start.13 = (f32[2,16,128]{2,1,0:T(8,128)S(1)}, f32[2,16,128]{2,1,0:T(8,128)}, u32[]{:S(2)}) copy-start(f32[2,16,128]{2,1,0:T(8,128)} %get-tuple-element.92) | copy-start | bytes 49156
  76.5 24.8 %all-to-all-start.1 = ((bf16[32,2,4096]{2,1,0:T(2,128)(2,1)}), bf16[32,2,4096]{2,1,0:T(2,128)(2,1)}, u32[]{:S(2)}, u32[]{:S(2)}) async-start(bf16[32,2,4096]{2,1,0:T(2,128)(2,1)} %reshape.591), calls=%async_computation.1 | async-start | bytes 1048576 | tf_op jit(solution)/shard_map/all_to_all | solution.py:101
  84.7 2.0 %copy-start.10 = (pred[128,128]{1,0:T(8,128)(4,1)S(1)}, pred[128,128]{1,0:T(8,128)(4,1)}, u32[]{:S(2)}) copy-start(pred[128,128]{1,0:T(8,128)(4,1)} %iota_compare_fusion.2) | copy-start | bytes 49156
  84.7 2.0 %copy-start.12 = (f32[2,16,128]{2,1,0:T(8,128)S(1)}, f32[2,16,128]{2,1,0:T(8,128)}, u32[]{:S(2)}) copy-start(f32[2,16,128]{2,1,0:T(8,128)} %get-tuple-element.93) | copy-start | bytes 49156
  106.6 2.1 %copy-start.6 = (f32[2,128,16,64]{1,0,3,2:T(2,128)S(1)}, f32[2,128,16,64]{1,0,3,2:T(2,128)}, u32[]{:S(2)}) copy-start(f32[2,128,16,64]{1,0,3,2:T(2,128)} %reshape.554) | copy-start | bytes 3145732
  106.6 2.1 %copy-start.8 = (f32[1,16,64,128]{3,2,1,0:T(8,128)S(1)}, f32[1,16,64,128]{3,2,1,0:T(8,128)}, u32[]{:S(2)}) copy-start(f32[1,16,64,128]{3,2,1,0:T(8,128)} %get-tuple-element.64) | copy-start | bytes 1572868
  106.6 2.3 %copy-start.17 = (f32[2,128,16,64]{1,3,2,0:T(8,128)S(1)}, f32[2,128,16,64]{1,3,2,0:T(8,128)}, u32[]{:S(2)}) copy-start(f32[2,128,16,64]{1,3,2,0:T(8,128)} %convolution_bitcast_fusion.3) | copy-start | bytes 3145732
  109.7 0.9 copy-start.14
  113.4 1.6 copy-start.1
Sparse Core Ops, SparseCore 0:
  52.8 45.9 all-gather.1

commit v9 on v8

--- a/solution.py
+++ b/solution.py
@@ -52,30 +52,25 @@
     head_count, head_size, state_size = forward_totals[1].shape
     assert count % head_count == 0
     per_head = count // head_count
-    chunk = head_size * state_size // per_head
+    rows = head_size // per_head
     head_of = jnp.arange(count, dtype=jnp.int32) // per_head
-
-    def pack(totals):
-        flat = totals[1].astype(jnp.bfloat16).reshape(count, chunk)
-        high, low = split_wide(totals[0][head_of])
-        tail = jnp.zeros((count, 128), jnp.bfloat16).at[:, 0].set(high).at[:, 1].set(low)
-        return jnp.concatenate([flat, tail], axis=1)
-
-    width = chunk + 128
-    got = lax.all_to_all(
-        jnp.concatenate([pack(forward_totals), pack(backward_totals)], axis=1),
-        axis,
-        0,
-        0,
-        tiled=True,
-    )
-
-    def unpack(block):
-        decay = block[:, chunk].astype(jnp.float32) + block[:, chunk + 1].astype(jnp.float32)
-        return decay, block[:, :chunk].astype(jnp.float32)
-
-    forward_decay, forward_parts = unpack(got[:, :width])
-    backward_decay, backward_parts = unpack(got[:, width:])
+    decay_parts = split_wide(forward_totals[0][head_of]) + split_wide(backward_totals[0][head_of])
+    decay_rows = jnp.zeros((count, 16, state_size), jnp.bfloat16)
+    decay_rows = decay_rows.at[:, 0, :4].set(jnp.stack(decay_parts, axis=1))
+    payload = jnp.concatenate(
+        [
+            forward_totals[1].astype(jnp.bfloat16).reshape(count, rows, state_size),
+            backward_totals[1].astype(jnp.bfloat16).reshape(count, rows, state_size),
+            decay_rows,
+        ],
+        axis=1,
+    )
+    got = lax.all_to_all(payload, axis, 0, 0, tiled=True)
+    forward_parts = got[:, :rows].astype(jnp.float32)
+    backward_parts = got[:, rows : 2 * rows].astype(jnp.float32)
+    decays = got[:, 2 * rows, :4].astype(jnp.float32)
+    forward_decay = decays[:, 0] + decays[:, 1]
+    backward_decay = decays[:, 2] + decays[:, 3]
     place = jnp.arange(count, dtype=jnp.int32)
     dest = place[:, None, None]
     source = place[None, :, None]
@@ -90,12 +85,12 @@
         axis=2,
     )
     backward_weight = jnp.where(place[None, :] > place[:, None], jnp.exp(backward_span), 0.0)
-    forward_in = jnp.dot(
-        forward_weight, forward_parts, precision=lax.Precision.HIGHEST,
+    forward_in = jnp.einsum(
+        "pq,qrn->prn", forward_weight, forward_parts, precision=lax.Precision.HIGHEST,
         preferred_element_type=jnp.float32,
     )
-    backward_in = jnp.dot(
-        backward_weight, backward_parts, precision=lax.Precision.HIGHEST,
+    backward_in = jnp.einsum(
+        "pq,qrn->prn", backward_weight, backward_parts, precision=lax.Precision.HIGHEST,
         preferred_element_type=jnp.float32,
     )
     returned = lax.all_to_all(
@@ -109,8 +104,8 @@
     )
     shape = (head_count, head_size, state_size)
     return (
-        returned[:, :chunk].astype(jnp.float32).reshape(shape),
-        returned[:, chunk:].astype(jnp.float32).reshape(shape),
+        returned[:, :rows].astype(jnp.float32).reshape(shape),
+        returned[:, rows:].astype(jnp.float32).reshape(shape),
     )
 
 

time: 182 us -> 171 us (0.940)
  the two profiles are of different devices: /device:TPU:6 before, /device:TPU:8 now
where the time goes in v9:
time: 171 us
  blocking collectives  57.3 us (34%)
  waiting for transfers between devices  34.4 us (20%)
  starting transfers between devices  21.7 us (13%)
  local copies, waits for them, and re-layouts  18.4 us (11%)
  between operations  15.3 us (9%)
  other arithmetic  13.1 us (8%)
  matrix products  10.4 us (6%)
    all_to_all x1, blocking collectives, all_to_all_pool(): moved = lax.all_to_all(packed, axis, 0, 0, tiled=True)  33.2 us
    all_to_all x1, blocking collectives, all_to_all_pool(): gathered = lax.all_to_all(spread_rows, axis, 0, 0, tiled=True)  24.1 us
    all_to_all x1, waiting for transfers between devices, transposed_scans(): got = lax.all_to_all(payload, axis, 0, 0, tiled=True)  21.4 us
    all_to_all x1, starting transfers between devices, transposed_scans(): got = lax.all_to_all(payload, axis, 0, 0, tiled=True)  16.2 us
    all_to_all x1, waiting for transfers between devices, transposed_scans(): lax.all_to_all(jnp.concatenate([forward_in.astype(jnp.bfloat16), backward...  12.3 us
    unnamed x35, local copies, waits for them, and re-layouts  6.32 us
    all_to_all x1, starting transfers between devices, transposed_scans(): lax.all_to_all(jnp.concatenate([forward_in.astype(jnp.bfloat16), backward...  5.52 us
    dot_general x2, matrix products, block_pass(): jnp.einsum('chqk,ckhp->cqhp', mixing, x_blocks, preferred_element_type=jn...  4.57 us
  transfers between devices with their start and end apart: 3, of which 2 were waited for; matrix products, arithmetic and copies ran while one was open for 7% of the time, Pallas kernels for 0%

profile of v9, /device:TPU:8, one launch (start us, length us, event | category | flops | bytes accessed | tf_op | source)
XLA Modules:
  0.0 170.5 jit_solution(5788422770241011956)
XLA Ops:
  7.9 0.8 fusion.58
  8.7 0.7 exp.109
  10.2 0.8 slice_reduce_fusion.3
  11.1 2.5 %reduce_window_sum.21 = f32[2,16,128]{2,1,0:T(8,128)S(1)} reduce-window(f32[2,16,128]{2,1,0:T(8,128)S(1)} %negate_multiply_fusion, f32[]{:T(128)} %constant.70.clone.1), window={size=1x1x128 pad=0_0x0_0x0_127}, to_apply=%region_1.2 | reduce-window | flops 520192 | bytes 32772 | tf_op jit(solution)/shard_map/block_pass/reduce_window_sum | solution.py:120
  13.8 1.2 copy.128
  15.6 0.9 broadcast_add_fusion.1
  17.2 1.0 fusion.92
  18.6 0.7 gather_fusion
  19.3 0.7 gather_fusion.1
  20.3 1.2 add_convert_fusion.4
  21.5 0.9 fusion.33
  22.4 16.2 %all-to-all-start = ((bf16[32,80,128]{2,1,0:T(8,128)(2,1)}), bf16[32,80,128]{2,1,0:T(8,128)(2,1)S(1)}, u32[]{:S(2)}, u32[]{:S(2)}) async-start(bf16[32,80,128]{2,1,0:T(8,128)(2,1)} %fusion.33), calls=%async_computation | async-start | bytes 1310720 | tf_op jit(solution)/shard_map/all_to_all | solution.py:68
  38.6 0.7 all-gather.2.cloned.1.call-update
  39.4 0.6 bitcast_bitcast_fusion.1
  40.0 21.4 %all-to-all-done = bf16[32,80,128]{2,1,0:T(8,128)(2,1)S(1)} async-done(((bf16[32,80,128]{2,1,0:T(8,128)(2,1)}), bf16[32,80,128]{2,1,0:T(8,128)(2,1)S(1)}, u32[]{:S(2)}, u32[]{:S(2)}) %all-to-all-start) | async-done | bytes 655392 | tf_op jit(solution)/shard_map/all_to_all | solution.py:68
  62.7 1.0 copy.138
  63.7 5.5 %all-to-all-start.1 = ((bf16[32,64,128]{2,1,0:T(8,128)(2,1)}), bf16[32,64,128]{2,1,0:T(8,128)(2,1)S(1)}, u32[]{:S(2)}, u32[]{:S(2)}) async-start(bf16[32,64,128]{2,1,0:T(8,128)(2,1)} %copy.138), calls=%async_computation.1 | async-start | bytes 1048576 | tf_op jit(solution)/shard_map/all_to_all | solution.py:96
  69.5 1.5 reshape.495
  71.5 2.6 %convolution_bitcast_fusion.2 = f32[2,128,16,64]{1,3,2,0:T(8,128)} fusion(f32[2,16,128]{2,1,0:T(8,128)} %get-tuple-element.58, f32[2,16,128]{2,1,0:T(8,128)S(1)} %reduce_window_sum.21, f32[2,128,128]{2,1,0:T(8,128)S(1)} %fusion.97, pred[128,128]{1,0:T(8,128)(4,1)S(1)} %iota_compare_fusion.2, bf16[2,128,16,64]{1,0,3,2:T(2,128)(2,1)S(1)} %reshape_reshape_squeeze.4), kind=kOutput, calls=%fused_computation.16 | convolution fusion | flops 69730304 | bytes 1753088 | tf_op jit(solution)/shard_map/chqk,ckhp->cqhp/dot_general | solution.py:135
  74.1 1.9 %convolution_bitcast_fusion.3 = f32[2,128,16,64]{1,3,2,0:T(8,128)} fusion(f32[2,16,128]{2,1,0:T(8,128)S(1)} %copy-done.8, f32[2,16,128]{2,1,0:T(8,128)S(1)} %reduce_window_sum.20, f32[2,128,128]{2,1,0:T(8,128)S(1)} %fusion.96, pred[128,128]{1,0:T(8,128)(4,1)S(1)} %iota_compare_fusion.3, bf16[2,128,16,64]{1,0,3,2:T(2,128)(2,1)S(1)} %reshape_reshape_squeeze.4), kind=kOutput, calls=%fused_computation.17 | convolution fusion | flops 69730304 | bytes 1753088 | tf_op jit(solution)/shard_map/chqk,ckhp->cqhp/dot_general | solution.py:135
  76.1 12.3 %all-to-all-done.1 = bf16[32,64,128]{2,1,0:T(8,128)(2,1)S(1)} async-done(((bf16[32,64,128]{2,1,0:T(8,128)(2,1)}), bf16[32,64,128]{2,1,0:T(8,128)(2,1)S(1)}, u32[]{:S(2)}, u32[]{:S(2)}) %all-to-all-start.1) | async-done | bytes 524320 | tf_op jit(solution)/shard_map/all_to_all | solution.py:96
  88.5 1.1 copy-done.4
  90.4 0.8 fusion.13
  91.2 0.8 copy.140
  92.6 2.3 %convolution_convert_fusion.1 = bf16[256,1024]{1,0:T(8,128)(2,1)S(1)} fusion(bf16[256,1024]{0,1:T(8,128)(2,1)S(1)} %fusion.17, bf16[1024,1024]{1,0:T(8,128)(2,1)} %all-gather.2.cloned.1.call-done), kind=kOutput, calls=%fused_computation.21 | convolution fusion | flops 537133056 | bytes 3145728 | tf_op jit(solution)/shard_map/dot_general | solution.py:311
  97.1 1.0 reduce.27
  98.5 33.2 %all_to_all.27 = bf16[32,2,4160]{2,1,0:T(2,128)(2,1)S(1)} all-to-all(bf16[32,2,4160]{2,1,0:T(2,128)(2,1)S(1)} %reshape.530), channel_id=1, replica_groups=mesh['dp'=16,'seq'=32] {'seq'}, dimensions={0} | all-to-all | bytes 1064960 | tf_op jit(solution)/shard_map/all_to_all | solution.py:244
  131.6 1.8 %reshape.531 = bf16[32,1,8320]{2,1,0:T(2,128)(2,1)} reshape(bf16[32,2,4160]{2,1,0:T(2,128)(2,1)S(1)} %all_to_all.27) | data formatting | bytes 1064960
  133.5 3.6 %copy.152 = bf16[32,1,8320]{0,2,1:T(8,128)(2,1)S(1)} copy(bf16[32,1,8320]{2,1,0:T(2,128)(2,1)} %reshape.531) | data formatting | bytes 1064960 | tf_op jit(solution)/shard_map/all_to_all | solution.py:244
  137.5 1.2 fusion
  138.8 24.1 %all_to_all.28 = bf16[32,8,1024]{2,1,0:T(8,128)(2,1)S(1)} all-to-all(bf16[32,8,1024]{2,1,0:T(8,128)(2,1)S(1)} %broadcast_in_dim.142), channel_id=1, replica_groups=mesh['dp'=16,'seq'=32] {'seq'}, dimensions={0} | all-to-all | bytes 1048576 | tf_op jit(solution)/shard_map/all_to_all | solution.py:256
  162.9 0.8 copy.197
  (103 shorter events, 9.4 us)
Async XLA Ops:
  7.2 87.7 %copy-start = (bf16[256,1024]{1,0:T(8,128)(2,1)S(1)}, bf16[256,1024]{1,0:T(8,128)(2,1)}, u32[]{:S(2)}) copy-start(bf16[256,1024]{1,0:T(8,128)(2,1)} %param.20) | copy-start | bytes 1572868
  7.2 8.0 %copy-start.7 = (bf16[1,256,512]{2,1,0:T(8,128)(2,1)S(1)}, bf16[1,256,512]{2,1,0:T(8,128)(2,1)}, u32[]{:S(2)}) copy-start(bf16[1,256,512]{2,1,0:T(8,128)(2,1)} %param.14) | copy-start | bytes 786436
  22.4 39.0 %all-to-all-start = ((bf16[32,80,128]{2,1,0:T(8,128)(2,1)}), bf16[32,80,128]{2,1,0:T(8,128)(2,1)S(1)}, u32[]{:S(2)}, u32[]{:S(2)}) async-start(bf16[32,80,128]{2,1,0:T(8,128)(2,1)} %fusion.33), calls=%async_computation | async-start | bytes 1310720 | tf_op jit(solution)/shard_map/all_to_all | solution.py:68
  38.5 54.0 %all-gather.2.cloned.1.call-start = ((), (), s32[]{:S(2)}) async-start(), calls=%async_computation.4 | async-start | bytes 2228224 | tf_op jit(solution)/shard_map/all_gather | solution.py:313
  61.9 7.4 %copy-start.11 = (f32[16]{0:T(128)S(1)}, f32[16]{0:T(128)}, u32[]{:S(2)}) copy-start(f32[16]{0:T(128)} %get-tuple-element.14) | copy-start | bytes 196
  61.9 7.4 %copy-start.5 = (bf16[1,256,1024]{2,1,0:T(8,128)(2,1)S(1)}, bf16[1,256,1024]{2,1,0:T(8,128)(2,1)}, u32[]{:S(2)}) copy-start(bf16[1,256,1024]{2,1,0:T(8,128)(2,1)} %param.13) | copy-start | bytes 1572868
  63.7 7.3 %copy-start.10 = (f32[16]{0:T(128)S(1)}, f32[16]{0:T(128)}, u32[]{:S(2)}) copy-start(f32[16]{0:T(128)} %param.17) | copy-start | bytes 196
  63.7 24.6 %all-to-all-start.1 = ((bf16[32,64,128]{2,1,0:T(8,128)(2,1)}), bf16[32,64,128]{2,1,0:T(8,128)(2,1)S(1)}, u32[]{:S(2)}, u32[]{:S(2)}) async-start(bf16[32,64,128]{2,1,0:T(8,128)(2,1)} %copy.138), calls=%async_computation.1 | async-start | bytes 1048576 | tf_op jit(solution)/shard_map/all_to_all | solution.py:96
  71.5 2.6 %copy-start.8 = (f32[2,16,128]{2,1,0:T(8,128)S(1)}, f32[2,16,128]{2,1,0:T(8,128)}, u32[]{:S(2)}) copy-start(f32[2,16,128]{2,1,0:T(8,128)} %get-tuple-element.59) | copy-start | bytes 49156
  76.0 12.5 %copy-start.2 = (f32[1,16,64,128]{3,2,1,0:T(8,128)S(1)}, f32[1,16,64,128]{3,2,1,0:T(8,128)}, u32[]{:S(2)}) copy-start(f32[1,16,64,128]{3,2,1,0:T(8,128)} %get-tuple-element.30) | copy-start | bytes 1572868
  88.4 1.2 copy-start.4
  88.4 1.5 copy-start.3
  88.5 1.6 copy-start.6
  88.5 1.9 %copy-start.12 = (f32[2,128,16,64]{1,3,2,0:T(8,128)S(1)}, f32[2,128,16,64]{1,3,2,0:T(8,128)}, u32[]{:S(2)}) copy-start(f32[2,128,16,64]{1,3,2,0:T(8,128)} %convolution_bitcast_fusion.3) | copy-start | bytes 3145732
  91.2 0.9 copy-start.9
  94.9 1.6 copy-start.1
Sparse Core Ops, SparseCore 0:
  41.5 48.4 all-gather.1

commit v10 on v9

--- a/solution.py
+++ b/solution.py
@@ -47,7 +47,7 @@
     return rounded.astype(jnp.bfloat16), low
 
 
-def transposed_scans(forward_totals, backward_totals, axis):
+def transposed_scans(forward_totals, backward_totals, axis, carried):
     count = lax.axis_size(axis)
     head_count, head_size, state_size = forward_totals[1].shape
     assert count % head_count == 0
@@ -65,6 +65,7 @@
         ],
         axis=1,
     )
+    payload, carried = lax.optimization_barrier((payload, carried))
     got = lax.all_to_all(payload, axis, 0, 0, tiled=True)
     forward_parts = got[:, :rows].astype(jnp.float32)
     backward_parts = got[:, rows : 2 * rows].astype(jnp.float32)
@@ -106,6 +107,7 @@
     return (
         returned[:, :rows].astype(jnp.float32).reshape(shape),
         returned[:, rows:].astype(jnp.float32).reshape(shape),
+        carried,
     )
 
 
@@ -298,7 +300,17 @@
         decay_rates[1],
         True,
     )
-    forward_in, backward_in = transposed_scans(forward_totals, backward_totals, "seq")
+    weight_groups = lax.axis_size("dp")
+    full_weight = lax.all_to_all(
+        jnp.broadcast_to(out_weight[None], (weight_groups,) + out_weight.shape),
+        "dp",
+        0,
+        0,
+        tiled=True,
+    ).reshape(weight_groups * out_weight.shape[0], out_weight.shape[1])
+    forward_in, backward_in, full_weight = transposed_scans(
+        forward_totals, backward_totals, "seq", full_weight
+    )
     forward_out = apply_state(forward_records, forward_in)
     backward_out = apply_state(backward_records, backward_in)
     skip_wide = jnp.repeat(skip_gain, head_size)
@@ -308,11 +320,7 @@
     mean_square = jnp.mean(squared, axis=2)
     inverse_scale = jnp.repeat(lax.rsqrt(mean_square + 1e-05), head_size, axis=1)
     normed = (gated_out * inverse_scale * norm_gain[None, :]).astype(jnp.bfloat16)
-    projected = jnp.dot(
-        normed,
-        lax.all_gather(out_weight, "dp", axis=0, tiled=True),
-        preferred_element_type=jnp.float32,
-    )
+    projected = jnp.dot(normed, full_weight, preferred_element_type=jnp.float32)
     encoded = projected.astype(jnp.bfloat16)
     score_scale = 1.0 / math.sqrt(model_width)
     scores = (

time: 171 us -> 170 us (level)
  the two profiles are of different devices: /device:TPU:8 before, /device:TPU:6 now
where the time goes in v10:
time: 170 us; the launch traced here: 167 us
  blocking collectives  47.8 us (28%)
  waiting for transfers between devices  41.5 us (24%)
  local copies, waits for them, and re-layouts  28.1 us (17%)
  starting transfers between devices  28.1 us (17%)
  other arithmetic  11 us (6%)
  matrix products  8.79 us (5%)
  between operations  1.8 us (1%)
    all_to_all x1, blocking collectives, all_to_all_pool(): gathered = lax.all_to_all(spread_rows, axis, 0, 0, tiled=True)  23.9 us
    all_to_all x1, blocking collectives, all_to_all_pool(): moved = lax.all_to_all(packed, axis, 0, 0, tiled=True)  23.9 us
    all_to_all x1, waiting for transfers between devices, transposed_scans(): got = lax.all_to_all(payload, axis, 0, 0, tiled=True)  20.6 us
    all_to_all x1, starting transfers between devices, transposed_scans(): got = lax.all_to_all(payload, axis, 0, 0, tiled=True)  12.3 us
    all_to_all x1, waiting for transfers between devices, body(): lax.all_to_all(jnp.broadcast_to(out_weight[None], (weight_groups,) + out_...  12.1 us
    all_to_all x1, starting transfers between devices, body(): lax.all_to_all(jnp.broadcast_to(out_weight[None], (weight_groups,) + out_...  9.56 us
    all_to_all x1, waiting for transfers between devices, transposed_scans(): lax.all_to_all(jnp.concatenate([forward_in.astype(jnp.bfloat16), backward...  8.82 us
    unnamed x41, local copies, waits for them, and re-layouts  8.09 us
  transfers between devices with their start and end apart: 3, of which 3 were waited for; matrix products, arithmetic and copies ran while one was open for 14% of the time, Pallas kernels for 0%

profile of v10, /device:TPU:6, one launch (start us, length us, event | category | flops | bytes accessed | tf_op | source)
XLA Modules:
  0.0 167.2 jit_solution(18140227693140390223)
XLA Ops:
  0.6 2.6 %broadcast_in_dim.82 = bf16[16,64,1024]{2,1,0:T(8,128)(2,1)} broadcast(bf16[64,1024]{1,0:T(8,128)(2,1)} %param.19), dimensions={1,2} | broadcast | bytes 2228224 | tf_op jit(solution)/shard_map/broadcast_in_dim | solution.py:305
  3.2 9.6 %all-to-all-start = ((bf16[16,64,1024]{2,1,0:T(8,128)(2,1)}), bf16[16,64,1024]{2,1,0:T(8,128)(2,1)S(1)}, u32[]{:S(2)}, u32[]{:S(2)}) async-start(bf16[16,64,1024]{2,1,0:T(8,128)(2,1)} %broadcast_in_dim.82), calls=%async_computation | async-start | bytes 4194304 | tf_op jit(solution)/shard_map/all_to_all | solution.py:304
  13.6 2.5 %reduce_window_sum.21 = f32[2,16,128]{2,1,0:T(8,128)S(1)} reduce-window(f32[2,16,128]{2,1,0:T(8,128)S(1)} %negate_multiply_fusion, f32[]{:T(128)} %constant.70.clone.1), window={size=1x1x128 pad=0_0x0_0x0_127}, to_apply=%region_1.2 | reduce-window | flops 520192 | bytes 32772 | tf_op jit(solution)/shard_map/block_pass/reduce_window_sum | solution.py:122
  16.8 1.0 copy.128
  17.8 1.2 reshape_reshape_squeeze.4
  22.3 1.0 fusion.95
  23.6 0.9 broadcast_add_fusion.1
  25.0 0.9 fusion.92
  26.1 0.9 fusion.33
  27.0 12.1 %all-to-all-done = bf16[16,64,1024]{2,1,0:T(8,128)(2,1)S(1)} async-done(((bf16[16,64,1024]{2,1,0:T(8,128)(2,1)}), bf16[16,64,1024]{2,1,0:T(8,128)(2,1)S(1)}, u32[]{:S(2)}, u32[]{:S(2)}) %all-to-all-start) | async-done | bytes 2097184 | tf_op jit(solution)/shard_map/all_to_all | solution.py:304
  39.1 12.3 %all-to-all-start.1 = ((bf16[32,80,128]{2,1,0:T(8,128)(2,1)}), bf16[32,80,128]{2,1,0:T(8,128)(2,1)}, u32[]{:S(2)}, u32[]{:S(2)}) async-start(bf16[32,80,128]{2,1,0:T(8,128)(2,1)} %fusion.33), calls=%async_computation.1 | async-start | bytes 1310720 | tf_op jit(solution)/shard_map/all_to_all | solution.py:69
  52.1 20.6 %all-to-all-done.1 = bf16[32,80,128]{2,1,0:T(8,128)(2,1)} async-done(((bf16[32,80,128]{2,1,0:T(8,128)(2,1)}), bf16[32,80,128]{2,1,0:T(8,128)(2,1)}, u32[]{:S(2)}, u32[]{:S(2)}) %all-to-all-start.1) | async-done | bytes 655392 | tf_op jit(solution)/shard_map/all_to_all | solution.py:69
  72.7 0.9 slice.192
  74.0 1.1 fusion.93
  75.9 1.0 copy.138
  77.0 6.2 %all-to-all-start.2 = ((bf16[32,64,128]{2,1,0:T(8,128)(2,1)}), bf16[32,64,128]{2,1,0:T(8,128)(2,1)}, u32[]{:S(2)}, u32[]{:S(2)}) async-start(bf16[32,64,128]{2,1,0:T(8,128)(2,1)} %copy.138), calls=%async_computation.2 | async-start | bytes 1048576 | tf_op jit(solution)/shard_map/all_to_all | solution.py:97
  83.2 2.0 %copy.142 = bf16[1,256,1024]{1,2,0:T(8,128)(2,1)} copy(bf16[1,256,1024]{2,1,0:T(8,128)(2,1)} %param.13) | data formatting | bytes 1048576 | tf_op args[1]
  85.2 2.5 %reshape.500 = f32[2,128,16,64]{1,0,3,2:T(2,128)} reshape(bf16[1,256,1024]{1,2,0:T(8,128)(2,1)} %copy.142) | data formatting | bytes 1572864 | tf_op jit(solution)/shard_map/convert_element_type | solution.py:318
  88.3 2.6 %convolution_bitcast_fusion.2 = f32[2,128,16,64]{1,3,2,0:T(8,128)} fusion(f32[2,16,128]{2,1,0:T(8,128)} %get-tuple-element.62, f32[2,16,128]{2,1,0:T(8,128)S(1)} %reduce_window_sum.21, f32[2,128,128]{2,1,0:T(8,128)S(1)} %fusion.97, pred[128,128]{1,0:T(8,128)(4,1)S(1)} %iota_compare_fusion.2, bf16[2,128,16,64]{1,0,3,2:T(2,128)(2,1)S(1)} %reshape_reshape_squeeze.4), kind=kOutput, calls=%fused_computation.16 | convolution fusion | flops 69730304 | bytes 1753088 | tf_op jit(solution)/shard_map/chqk,ckhp->cqhp/dot_general | solution.py:137
  90.9 1.9 %convolution_bitcast_fusion.3 = f32[2,128,16,64]{1,3,2,0:T(8,128)} fusion(f32[2,16,128]{2,1,0:T(8,128)S(1)} %copy-done.10, f32[2,16,128]{2,1,0:T(8,128)S(1)} %reduce_window_sum.20, f32[2,128,128]{2,1,0:T(8,128)S(1)} %fusion.96, pred[128,128]{1,0:T(8,128)(4,1)S(1)} %iota_compare_fusion.3, bf16[2,128,16,64]{1,0,3,2:T(2,128)(2,1)S(1)} %reshape_reshape_squeeze.4), kind=kOutput, calls=%fused_computation.17 | convolution fusion | flops 69730304 | bytes 1753088 | tf_op jit(solution)/shard_map/chqk,ckhp->cqhp/dot_general | solution.py:137
  92.8 8.8 %all-to-all-done.2 = bf16[32,64,128]{2,1,0:T(8,128)(2,1)} async-done(((bf16[32,64,128]{2,1,0:T(8,128)(2,1)}), bf16[32,64,128]{2,1,0:T(8,128)(2,1)}, u32[]{:S(2)}, u32[]{:S(2)}) %all-to-all-start.2) | async-done | bytes 524320 | tf_op jit(solution)/shard_map/all_to_all | solution.py:97
  101.6 1.2 fusion.94
  104.7 0.7 fusion.13
  105.4 0.8 copy.140
  107.1 0.7 convolution_convert_fusion.1
  110.0 1.0 reduce.27
  111.4 23.9 %all_to_all.32 = bf16[32,2,4160]{2,1,0:T(2,128)(2,1)S(1)} all-to-all(bf16[32,2,4160]{2,1,0:T(2,128)(2,1)S(1)} %reshape.535), channel_id=1, replica_groups=mesh['dp'=16,'seq'=32] {'seq'}, dimensions={0} | all-to-all | bytes 1064960 | tf_op jit(solution)/shard_map/all_to_all | solution.py:246
  135.3 1.8 %reshape.536 = bf16[32,1,8320]{2,1,0:T(2,128)(2,1)} reshape(bf16[32,2,4160]{2,1,0:T(2,128)(2,1)S(1)} %all_to_all.32) | data formatting | bytes 1064960
  137.2 3.6 %copy.152 = bf16[32,1,8320]{0,2,1:T(8,128)(2,1)S(1)} copy(bf16[32,1,8320]{2,1,0:T(2,128)(2,1)} %reshape.536) | data formatting | bytes 1064960 | tf_op jit(solution)/shard_map/all_to_all | solution.py:246
  141.2 1.2 fusion
  142.5 23.9 %all_to_all.33 = bf16[32,8,1024]{2,1,0:T(8,128)(2,1)S(1)} all-to-all(bf16[32,8,1024]{2,1,0:T(8,128)(2,1)S(1)} %broadcast_in_dim.149), channel_id=1, replica_groups=mesh['dp'=16,'seq'=32] {'seq'}, dimensions={0} | all-to-all | bytes 1048576 | tf_op jit(solution)/shard_map/all_to_all | solution.py:258
  166.4 0.8 copy.197
  (109 shorter events, 13.0 us)
Async XLA Ops:
  0.6 107.2 %copy-start = (bf16[256,1024]{1,0:T(8,128)(2,1)S(1)}, bf16[256,1024]{1,0:T(8,128)(2,1)}, u32[]{:S(2)}) copy-start(bf16[256,1024]{1,0:T(8,128)(2,1)} %param.20) | copy-start | bytes 1572868
  3.2 10.2 %copy-start.12 = (f32[2,16]{1,0:T(2,128)S(1)}, f32[2,16]{1,0:T(2,128)}, u32[]{:S(2)}) copy-start(f32[2,16]{1,0:T(2,128)} %param.16) | copy-start | bytes 388
  3.2 10.3 %copy-start.9 = (f32[1,32,256]{2,1,0:T(8,128)S(1)}, f32[1,32,256]{2,1,0:T(8,128)}, u32[]{:S(2)}) copy-start(f32[1,32,256]{2,1,0:T(8,128)} %param.15) | copy-start | bytes 98308
  3.2 13.5 %copy-start.7 = (bf16[1,256,1024]{2,1,0:T(8,128)(2,1)S(1)}, bf16[1,256,1024]{2,1,0:T(8,128)(2,1)}, u32[]{:S(2)}) copy-start(bf16[1,256,1024]{2,1,0:T(8,128)(2,1)} %param.12) | copy-start | bytes 1572868
  3.2 35.8 %all-to-all-start = ((bf16[16,64,1024]{2,1,0:T(8,128)(2,1)}), bf16[16,64,1024]{2,1,0:T(8,128)(2,1)S(1)}, u32[]{:S(2)}, u32[]{:S(2)}) async-start(bf16[16,64,1024]{2,1,0:T(8,128)(2,1)} %broadcast_in_dim.82), calls=%async_computation | async-start | bytes 4194304 | tf_op jit(solution)/shard_map/all_to_all | solution.py:304
  39.1 33.6 %all-to-all-start.1 = ((bf16[32,80,128]{2,1,0:T(8,128)(2,1)}), bf16[32,80,128]{2,1,0:T(8,128)(2,1)}, u32[]{:S(2)}, u32[]{:S(2)}) async-start(bf16[32,80,128]{2,1,0:T(8,128)(2,1)} %fusion.33), calls=%async_computation.1 | async-start | bytes 1310720 | tf_op jit(solution)/shard_map/all_to_all | solution.py:69
  75.1 8.0 %copy-start.14 = (f32[16]{0:T(128)S(1)}, f32[16]{0:T(128)}, u32[]{:S(2)}) copy-start(f32[16]{0:T(128)} %get-tuple-element.18) | copy-start | bytes 196
  77.0 10.8 %copy-start.13 = (f32[16]{0:T(128)S(1)}, f32[16]{0:T(128)}, u32[]{:S(2)}) copy-start(f32[16]{0:T(128)} %param.17) | copy-start | bytes 196
  77.0 24.7 %all-to-all-start.2 = ((bf16[32,64,128]{2,1,0:T(8,128)(2,1)}), bf16[32,64,128]{2,1,0:T(8,128)(2,1)}, u32[]{:S(2)}, u32[]{:S(2)}) async-start(bf16[32,64,128]{2,1,0:T(8,128)(2,1)} %copy.138), calls=%async_computation.2 | async-start | bytes 1048576 | tf_op jit(solution)/shard_map/all_to_all | solution.py:97
  88.2 2.7 %copy-start.10 = (f32[2,16,128]{2,1,0:T(8,128)S(1)}, f32[2,16,128]{2,1,0:T(8,128)}, u32[]{:S(2)}) copy-start(f32[2,16,128]{2,1,0:T(8,128)} %get-tuple-element.63) | copy-start | bytes 49156
  101.6 1.3 copy-start.4
  101.6 1.5 copy-start.6
  102.9 1.3 copy-start.5
  102.9 1.4 copy-start.8
  102.9 1.8 %copy-start.15 = (f32[2,128,16,64]{1,3,2,0:T(8,128)S(1)}, f32[2,128,16,64]{1,3,2,0:T(8,128)}, u32[]{:S(2)}) copy-start(f32[2,128,16,64]{1,3,2,0:T(8,128)} %convolution_bitcast_fusion.3) | copy-start | bytes 3145732
  105.4 1.0 copy-start.1
  105.4 1.2 copy-start.2
  105.4 1.2 copy-start.11
  107.9 1.6 copy-start.3

commit v11 on v10

--- a/solution.py
+++ b/solution.py
@@ -234,21 +234,19 @@
     row_total, width = weighted_sum.shape
     rows = row_total // count
     stats = jnp.stack(split_wide(local_top) + split_wide(weight_sum), axis=0)
-    stats = stats.reshape(4, count, rows).transpose(1, 0, 2).reshape(count, 4 * rows)
-    pad = (-4 * rows) % 128
+    stats = stats.reshape(4, count, rows).transpose(1, 2, 0)
     packed = jnp.concatenate(
         [
-            weighted_sum.astype(jnp.bfloat16).reshape(count, rows * width),
-            jnp.pad(stats, ((0, 0), (0, pad))),
+            weighted_sum.astype(jnp.bfloat16).reshape(count, rows, width),
+            jnp.pad(stats, ((0, 0), (0, 0), (0, 124))),
         ],
-        axis=1,
+        axis=2,
     )
     moved = lax.all_to_all(packed, axis, 0, 0, tiled=True)
-    parts = moved[:, : rows * width].reshape(count, rows, width).astype(jnp.float32)
-    got = moved[:, rows * width : rows * width + 4 * rows].astype(jnp.float32)
-    got = got.reshape(count, 4, rows)
-    tops = got[:, 0] + got[:, 1]
-    totals = got[:, 2] + got[:, 3]
+    parts = moved[:, :, :width].astype(jnp.float32)
+    got = moved[:, :, width : width + 4].astype(jnp.float32)
+    tops = got[:, :, 0] + got[:, :, 1]
+    totals = got[:, :, 2] + got[:, :, 3]
     top = jnp.max(tops, axis=0)
     scale = jnp.exp(tops - top[None, :])
     total = jnp.sum(totals * scale, axis=0)

time: 170 us -> 163 us (0.959)
  local copies, waits for them, and re-layouts: 28.1 us -> 21.8 us
  other arithmetic: 11 us -> 9.12 us
    all_to_all x2 -> x0, local copies, waits for them, and re-layouts: 4.16 us -> none  [all_to_all_pool(): moved = lax.all_to_all(packed, axis, 0, 0, tiled=True)]
    unnamed x41 -> x40, local copies, waits for them, and re-layouts: 8.09 us -> 6.07 us
  transfers between devices with their start and end apart: 3 -> 3, of which waited for: 3 -> 3; matrix products, arithmetic and copies ran while one was open for 14% -> 15% of each run, Pallas kernels for 0% -> 0%
where the time goes in v11:
time: 163 us; the launch traced here: 160 us
  blocking collectives  48.8 us (30%)
  waiting for transfers between devices  41.5 us (25%)
  starting transfers between devices  28.1 us (17%)
  local copies, waits for them, and re-layouts  21.8 us (13%)
  other arithmetic  9.12 us (6%)
  matrix products  8.79 us (5%)
  between operations  1.77 us (1%)
    all_to_all x1, blocking collectives, all_to_all_pool(): moved = lax.all_to_all(packed, axis, 0, 0, tiled=True)  24.7 us
    all_to_all x1, blocking collectives, all_to_all_pool(): gathered = lax.all_to_all(spread_rows, axis, 0, 0, tiled=True)  24.2 us
    all_to_all x1, waiting for transfers between devices, transposed_scans(): got = lax.all_to_all(payload, axis, 0, 0, tiled=True)  20.6 us
    all_to_all x1, starting transfers between devices, transposed_scans(): got = lax.all_to_all(payload, axis, 0, 0, tiled=True)  12.3 us
    all_to_all x1, waiting for transfers between devices, body(): lax.all_to_all(jnp.broadcast_to(out_weight[None], (weight_groups,) + out_...  12.1 us
    all_to_all x1, starting transfers between devices, body(): lax.all_to_all(jnp.broadcast_to(out_weight[None], (weight_groups,) + out_...  9.56 us
    all_to_all x1, waiting for transfers between devices, transposed_scans(): lax.all_to_all(jnp.concatenate([forward_in.astype(jnp.bfloat16), backward...  8.82 us
    all_to_all x1, starting transfers between devices, transposed_scans(): lax.all_to_all(jnp.concatenate([forward_in.astype(jnp.bfloat16), backward...  6.19 us
  transfers between devices with their start and end apart: 3, of which 3 were waited for; matrix products, arithmetic and copies ran while one was open for 15% of the time, Pallas kernels for 0%

profile of v11, /device:TPU:6, one launch (start us, length us, event | category | flops | bytes accessed | tf_op | source)
XLA Modules:
  0.0 159.9 jit_solution(4310989615330340545)
XLA Ops:
  0.6 2.6 %broadcast_in_dim.82 = bf16[16,64,1024]{2,1,0:T(8,128)(2,1)} broadcast(bf16[64,1024]{1,0:T(8,128)(2,1)} %param.19), dimensions={1,2} | broadcast | bytes 2228224 | tf_op jit(solution)/shard_map/broadcast_in_dim | solution.py:303
  3.2 9.6 %all-to-all-start = ((bf16[16,64,1024]{2,1,0:T(8,128)(2,1)}), bf16[16,64,1024]{2,1,0:T(8,128)(2,1)S(1)}, u32[]{:S(2)}, u32[]{:S(2)}) async-start(bf16[16,64,1024]{2,1,0:T(8,128)(2,1)} %broadcast_in_dim.82), calls=%async_computation | async-start | bytes 4194304 | tf_op jit(solution)/shard_map/all_to_all | solution.py:302
  13.6 2.5 %reduce_window_sum.21 = f32[2,16,128]{2,1,0:T(8,128)S(1)} reduce-window(f32[2,16,128]{2,1,0:T(8,128)S(1)} %negate_multiply_fusion, f32[]{:T(128)} %constant.70.clone.1), window={size=1x1x128 pad=0_0x0_0x0_127}, to_apply=%region_1.2 | reduce-window | flops 520192 | bytes 32772 | tf_op jit(solution)/shard_map/block_pass/reduce_window_sum | solution.py:122
  16.8 1.0 copy.135
  17.8 1.2 reshape_reshape_squeeze.4
  18.9 0.7 slice_reduce_fusion.3
  20.5 0.7 gather_fusion
  21.2 0.7 gather_fusion.1
  22.3 1.0 fusion.92
  23.6 0.9 broadcast_add_fusion.1
  25.0 0.9 fusion.89
  26.1 0.9 fusion.33
  27.0 12.1 %all-to-all-done = bf16[16,64,1024]{2,1,0:T(8,128)(2,1)S(1)} async-done(((bf16[16,64,1024]{2,1,0:T(8,128)(2,1)}), bf16[16,64,1024]{2,1,0:T(8,128)(2,1)S(1)}, u32[]{:S(2)}, u32[]{:S(2)}) %all-to-all-start) | async-done | bytes 2097184 | tf_op jit(solution)/shard_map/all_to_all | solution.py:302
  39.1 12.3 %all-to-all-start.1 = ((bf16[32,80,128]{2,1,0:T(8,128)(2,1)}), bf16[32,80,128]{2,1,0:T(8,128)(2,1)}, u32[]{:S(2)}, u32[]{:S(2)}) async-start(bf16[32,80,128]{2,1,0:T(8,128)(2,1)} %fusion.33), calls=%async_computation.1 | async-start | bytes 1310720 | tf_op jit(solution)/shard_map/all_to_all | solution.py:69
  52.1 20.6 %all-to-all-done.1 = bf16[32,80,128]{2,1,0:T(8,128)(2,1)} async-done(((bf16[32,80,128]{2,1,0:T(8,128)(2,1)}), bf16[32,80,128]{2,1,0:T(8,128)(2,1)}, u32[]{:S(2)}, u32[]{:S(2)}) %all-to-all-start.1) | async-done | bytes 655392 | tf_op jit(solution)/shard_map/all_to_all | solution.py:69
  72.7 0.9 slice.192
  74.0 1.1 fusion.90
  75.9 1.0 copy.145
  77.0 6.2 %all-to-all-start.2 = ((bf16[32,64,128]{2,1,0:T(8,128)(2,1)}), bf16[32,64,128]{2,1,0:T(8,128)(2,1)}, u32[]{:S(2)}, u32[]{:S(2)}) async-start(bf16[32,64,128]{2,1,0:T(8,128)(2,1)} %copy.145), calls=%async_computation.2 | async-start | bytes 1048576 | tf_op jit(solution)/shard_map/all_to_all | solution.py:97
  83.2 2.0 %copy.149 = bf16[1,256,1024]{1,2,0:T(8,128)(2,1)} copy(bf16[1,256,1024]{2,1,0:T(8,128)(2,1)} %param.13) | data formatting | bytes 1048576 | tf_op args[1]
  85.2 2.5 %reshape.464 = f32[2,128,16,64]{1,0,3,2:T(2,128)} reshape(bf16[1,256,1024]{1,2,0:T(8,128)(2,1)} %copy.149) | data formatting | bytes 1572864 | tf_op jit(solution)/shard_map/convert_element_type | solution.py:316
  88.3 2.6 %convolution_bitcast_fusion.2 = f32[2,128,16,64]{1,3,2,0:T(8,128)} fusion(f32[2,16,128]{2,1,0:T(8,128)} %get-tuple-element.60, f32[2,16,128]{2,1,0:T(8,128)S(1)} %reduce_window_sum.21, f32[2,128,128]{2,1,0:T(8,128)S(1)} %fusion.94, pred[128,128]{1,0:T(8,128)(4,1)S(1)} %iota_compare_fusion.2, bf16[2,128,16,64]{1,0,3,2:T(2,128)(2,1)S(1)} %reshape_reshape_squeeze.4), kind=kOutput, calls=%fused_computation.14 | convolution fusion | flops 69730304 | bytes 1753088 | tf_op jit(solution)/shard_map/chqk,ckhp->cqhp/dot_general | solution.py:137
  90.9 1.9 %convolution_bitcast_fusion.3 = f32[2,128,16,64]{1,3,2,0:T(8,128)} fusion(f32[2,16,128]{2,1,0:T(8,128)S(1)} %copy-done.10, f32[2,16,128]{2,1,0:T(8,128)S(1)} %reduce_window_sum.20, f32[2,128,128]{2,1,0:T(8,128)S(1)} %fusion.93, pred[128,128]{1,0:T(8,128)(4,1)S(1)} %iota_compare_fusion.3, bf16[2,128,16,64]{1,0,3,2:T(2,128)(2,1)S(1)} %reshape_reshape_squeeze.4), kind=kOutput, calls=%fused_computation.15 | convolution fusion | flops 69730304 | bytes 1753088 | tf_op jit(solution)/shard_map/chqk,ckhp->cqhp/dot_general | solution.py:137
  92.8 8.8 %all-to-all-done.2 = bf16[32,64,128]{2,1,0:T(8,128)(2,1)} async-done(((bf16[32,64,128]{2,1,0:T(8,128)(2,1)}), bf16[32,64,128]{2,1,0:T(8,128)(2,1)}, u32[]{:S(2)}, u32[]{:S(2)}) %all-to-all-start.2) | async-done | bytes 524320 | tf_op jit(solution)/shard_map/all_to_all | solution.py:97
  101.6 1.2 fusion.91
  103.5 0.6 copy-done.5
  104.7 0.7 fusion.13
  105.4 0.8 copy.147
  107.1 0.7 convolution_convert_fusion.1
  109.3 24.7 %all_to_all.25 = bf16[32,8,1152]{2,1,0:T(8,128)(2,1)S(1)} all-to-all(bf16[32,8,1152]{2,1,0:T(8,128)(2,1)S(1)} %fusion.34), channel_id=1, replica_groups=mesh['dp'=16,'seq'=32] {'seq'}, dimensions={0} | all-to-all | bytes 1179648 | tf_op jit(solution)/shard_map/all_to_all | solution.py:245
  134.9 24.2 %all_to_all.26 = bf16[32,8,1024]{2,1,0:T(8,128)(2,1)S(1)} all-to-all(bf16[32,8,1024]{2,1,0:T(8,128)(2,1)S(1)} %broadcast_in_dim.149), channel_id=1, replica_groups=mesh['dp'=16,'seq'=32] {'seq'}, dimensions={0} | all-to-all | bytes 1048576 | tf_op jit(solution)/shard_map/all_to_all | solution.py:256
  159.1 0.8 copy.207
  (106 shorter events, 9.7 us)
Async XLA Ops:
  0.6 107.2 %copy-start = (bf16[256,1024]{1,0:T(8,128)(2,1)S(1)}, bf16[256,1024]{1,0:T(8,128)(2,1)}, u32[]{:S(2)}) copy-start(bf16[256,1024]{1,0:T(8,128)(2,1)} %param.20) | copy-start | bytes 1572868
  3.2 10.2 %copy-start.12 = (f32[2,16]{1,0:T(2,128)S(1)}, f32[2,16]{1,0:T(2,128)}, u32[]{:S(2)}) copy-start(f32[2,16]{1,0:T(2,128)} %param.16) | copy-start | bytes 388
  3.2 10.3 %copy-start.9 = (f32[1,32,256]{2,1,0:T(8,128)S(1)}, f32[1,32,256]{2,1,0:T(8,128)}, u32[]{:S(2)}) copy-start(f32[1,32,256]{2,1,0:T(8,128)} %param.15) | copy-start | bytes 98308
  3.2 13.5 %copy-start.7 = (bf16[1,256,1024]{2,1,0:T(8,128)(2,1)S(1)}, bf16[1,256,1024]{2,1,0:T(8,128)(2,1)}, u32[]{:S(2)}) copy-start(bf16[1,256,1024]{2,1,0:T(8,128)(2,1)} %param.12) | copy-start | bytes 1572868
  3.2 35.8 %all-to-all-start = ((bf16[16,64,1024]{2,1,0:T(8,128)(2,1)}), bf16[16,64,1024]{2,1,0:T(8,128)(2,1)S(1)}, u32[]{:S(2)}, u32[]{:S(2)}) async-start(bf16[16,64,1024]{2,1,0:T(8,128)(2,1)} %broadcast_in_dim.82), calls=%async_computation | async-start | bytes 4194304 | tf_op jit(solution)/shard_map/all_to_all | solution.py:302
  39.1 33.6 %all-to-all-start.1 = ((bf16[32,80,128]{2,1,0:T(8,128)(2,1)}), bf16[32,80,128]{2,1,0:T(8,128)(2,1)}, u32[]{:S(2)}, u32[]{:S(2)}) async-start(bf16[32,80,128]{2,1,0:T(8,128)(2,1)} %fusion.33), calls=%async_computation.1 | async-start | bytes 1310720 | tf_op jit(solution)/shard_map/all_to_all | solution.py:69
  75.1 8.0 %copy-start.14 = (f32[16]{0:T(128)S(1)}, f32[16]{0:T(128)}, u32[]{:S(2)}) copy-start(f32[16]{0:T(128)} %get-tuple-element.18) | copy-start | bytes 196
  77.0 10.8 %copy-start.13 = (f32[16]{0:T(128)S(1)}, f32[16]{0:T(128)}, u32[]{:S(2)}) copy-start(f32[16]{0:T(128)} %param.17) | copy-start | bytes 196
  77.0 24.7 %all-to-all-start.2 = ((bf16[32,64,128]{2,1,0:T(8,128)(2,1)}), bf16[32,64,128]{2,1,0:T(8,128)(2,1)}, u32[]{:S(2)}, u32[]{:S(2)}) async-start(bf16[32,64,128]{2,1,0:T(8,128)(2,1)} %copy.145), calls=%async_computation.2 | async-start | bytes 1048576 | tf_op jit(solution)/shard_map/all_to_all | solution.py:97
  88.2 2.7 %copy-start.10 = (f32[2,16,128]{2,1,0:T(8,128)S(1)}, f32[2,16,128]{2,1,0:T(8,128)}, u32[]{:S(2)}) copy-start(f32[2,16,128]{2,1,0:T(8,128)} %get-tuple-element.61) | copy-start | bytes 49156
  101.6 1.3 copy-start.4
  101.6 1.5 copy-start.6
  102.9 1.3 copy-start.5
  102.9 1.4 copy-start.8
  102.9 1.8 %copy-start.15 = (f32[2,128,16,64]{1,3,2,0:T(8,128)S(1)}, f32[2,128,16,64]{1,3,2,0:T(8,128)}, u32[]{:S(2)}) copy-start(f32[2,128,16,64]{1,3,2,0:T(8,128)} %convolution_bitcast_fusion.3) | copy-start | bytes 3145732
  105.4 1.0 copy-start.1
  105.4 1.2 copy-start.2
  105.4 1.2 copy-start.11
  107.9 1.5 copy-start.3

commit v12 on v11

--- a/solution.py
+++ b/solution.py
@@ -87,11 +87,11 @@
     )
     backward_weight = jnp.where(place[None, :] > place[:, None], jnp.exp(backward_span), 0.0)
     forward_in = jnp.einsum(
-        "pq,qrn->prn", forward_weight, forward_parts, precision=lax.Precision.HIGHEST,
+        "pq,qrn->prn", forward_weight, forward_parts, precision=lax.Precision.HIGH,
         preferred_element_type=jnp.float32,
     )
     backward_in = jnp.einsum(
-        "pq,qrn->prn", backward_weight, backward_parts, precision=lax.Precision.HIGHEST,
+        "pq,qrn->prn", backward_weight, backward_parts, precision=lax.Precision.HIGH,
         preferred_element_type=jnp.float32,
     )
     returned = lax.all_to_all(

time: 163 us -> 163 us (level)
  the two profiles are of different devices: /device:TPU:6 before, /device:TPU:10 now
where the time goes in v12:
time: 163 us; the launch traced here: 162 us
  blocking collectives  49.7 us (30%)
  waiting for transfers between devices  43.8 us (27%)
  starting transfers between devices  27.4 us (17%)
  local copies, waits for them, and re-layouts  21.8 us (13%)
  other arithmetic  9.12 us (6%)
  matrix products  8.64 us (5%)
  between operations  1.77 us (1%)
    all_to_all x1, blocking collectives, all_to_all_pool(): moved = lax.all_to_all(packed, axis, 0, 0, tiled=True)  25.6 us
    all_to_all x1, blocking collectives, all_to_all_pool(): gathered = lax.all_to_all(spread_rows, axis, 0, 0, tiled=True)  24.1 us
    all_to_all x1, waiting for transfers between devices, transposed_scans(): got = lax.all_to_all(payload, axis, 0, 0, tiled=True)  22 us
    all_to_all x1, starting transfers between devices, transposed_scans(): got = lax.all_to_all(payload, axis, 0, 0, tiled=True)  15.3 us
    all_to_all x1, waiting for transfers between devices, body(): lax.all_to_all(jnp.broadcast_to(out_weight[None], (weight_groups,) + out_...  12.1 us
    all_to_all x1, waiting for transfers between devices, transposed_scans(): lax.all_to_all(jnp.concatenate([forward_in.astype(jnp.bfloat16), backward...  9.73 us
    all_to_all x1, starting transfers between devices, body(): lax.all_to_all(jnp.broadcast_to(out_weight[None], (weight_groups,) + out_...  6.79 us
    unnamed x40, local copies, waits for them, and re-layouts  6.07 us
  transfers between devices with their start and end apart: 3, of which 3 were waited for; matrix products, arithmetic and copies ran while one was open for 15% of the time, Pallas kernels for 0%

profile of v12, /device:TPU:10, one launch (start us, length us, event | category | flops | bytes accessed | tf_op | source)
XLA Modules:
  0.0 162.3 jit_solution(10404187346479393115)
XLA Ops:
  0.6 2.6 %broadcast_in_dim.82 = bf16[16,64,1024]{2,1,0:T(8,128)(2,1)} broadcast(bf16[64,1024]{1,0:T(8,128)(2,1)} %param.19), dimensions={1,2} | broadcast | bytes 2228224 | tf_op jit(solution)/shard_map/broadcast_in_dim | solution.py:303
  3.2 6.8 %all-to-all-start = ((bf16[16,64,1024]{2,1,0:T(8,128)(2,1)}), bf16[16,64,1024]{2,1,0:T(8,128)(2,1)S(1)}, u32[]{:S(2)}, u32[]{:S(2)}) async-start(bf16[16,64,1024]{2,1,0:T(8,128)(2,1)} %broadcast_in_dim.82), calls=%async_computation | async-start | bytes 4194304 | tf_op jit(solution)/shard_map/all_to_all | solution.py:302
  10.8 2.5 %reduce_window_sum.21 = f32[2,16,128]{2,1,0:T(8,128)S(1)} reduce-window(f32[2,16,128]{2,1,0:T(8,128)S(1)} %negate_multiply_fusion, f32[]{:T(128)} %constant.70.clone.1), window={size=1x1x128 pad=0_0x0_0x0_127}, to_apply=%region_1.2 | reduce-window | flops 520192 | bytes 32772 | tf_op jit(solution)/shard_map/block_pass/reduce_window_sum | solution.py:122
  14.0 1.0 copy.135
  15.0 1.2 reshape_reshape_squeeze.4
  16.2 0.7 slice_reduce_fusion.3
  17.7 0.7 gather_fusion
  18.4 0.7 gather_fusion.1
  19.6 1.0 fusion.92
  20.8 0.9 broadcast_add_fusion.1
  22.2 0.9 fusion.89
  23.3 0.9 fusion.33
  24.2 12.1 %all-to-all-done = bf16[16,64,1024]{2,1,0:T(8,128)(2,1)S(1)} async-done(((bf16[16,64,1024]{2,1,0:T(8,128)(2,1)}), bf16[16,64,1024]{2,1,0:T(8,128)(2,1)S(1)}, u32[]{:S(2)}, u32[]{:S(2)}) %all-to-all-start) | async-done | bytes 2097184 | tf_op jit(solution)/shard_map/all_to_all | solution.py:302
  36.3 15.3 %all-to-all-start.1 = ((bf16[32,80,128]{2,1,0:T(8,128)(2,1)}), bf16[32,80,128]{2,1,0:T(8,128)(2,1)}, u32[]{:S(2)}, u32[]{:S(2)}) async-start(bf16[32,80,128]{2,1,0:T(8,128)(2,1)} %fusion.33), calls=%async_computation.1 | async-start | bytes 1310720 | tf_op jit(solution)/shard_map/all_to_all | solution.py:69
  52.4 22.0 %all-to-all-done.1 = bf16[32,80,128]{2,1,0:T(8,128)(2,1)} async-done(((bf16[32,80,128]{2,1,0:T(8,128)(2,1)}), bf16[32,80,128]{2,1,0:T(8,128)(2,1)}, u32[]{:S(2)}, u32[]{:S(2)}) %all-to-all-start.1) | async-done | bytes 655392 | tf_op jit(solution)/shard_map/all_to_all | solution.py:69
  74.3 0.9 slice.192
  75.6 1.1 fusion.90
  77.4 1.0 copy.145
  78.4 5.3 %all-to-all-start.2 = ((bf16[32,64,128]{2,1,0:T(8,128)(2,1)}), bf16[32,64,128]{2,1,0:T(8,128)(2,1)}, u32[]{:S(2)}, u32[]{:S(2)}) async-start(bf16[32,64,128]{2,1,0:T(8,128)(2,1)} %copy.145), calls=%async_computation.2 | async-start | bytes 1048576 | tf_op jit(solution)/shard_map/all_to_all | solution.py:97
  83.8 2.0 %copy.149 = bf16[1,256,1024]{1,2,0:T(8,128)(2,1)} copy(bf16[1,256,1024]{2,1,0:T(8,128)(2,1)} %param.13) | data formatting | bytes 1048576 | tf_op args[1]
  85.8 2.5 %reshape.464 = f32[2,128,16,64]{1,0,3,2:T(2,128)} reshape(bf16[1,256,1024]{1,2,0:T(8,128)(2,1)} %copy.149) | data formatting | bytes 1572864 | tf_op jit(solution)/shard_map/convert_element_type | solution.py:316
  88.9 2.6 %convolution_bitcast_fusion.2 = f32[2,128,16,64]{1,3,2,0:T(8,128)} fusion(f32[2,16,128]{2,1,0:T(8,128)} %get-tuple-element.60, f32[2,16,128]{2,1,0:T(8,128)S(1)} %reduce_window_sum.21, f32[2,128,128]{2,1,0:T(8,128)S(1)} %fusion.94, pred[128,128]{1,0:T(8,128)(4,1)S(1)} %iota_compare_fusion.2, bf16[2,128,16,64]{1,0,3,2:T(2,128)(2,1)S(1)} %reshape_reshape_squeeze.4), kind=kOutput, calls=%fused_computation.14 | convolution fusion | flops 69730304 | bytes 1753088 | tf_op jit(solution)/shard_map/chqk,ckhp->cqhp/dot_general | solution.py:137
  91.5 1.9 %convolution_bitcast_fusion.3 = f32[2,128,16,64]{1,3,2,0:T(8,128)} fusion(f32[2,16,128]{2,1,0:T(8,128)S(1)} %copy-done.10, f32[2,16,128]{2,1,0:T(8,128)S(1)} %reduce_window_sum.20, f32[2,128,128]{2,1,0:T(8,128)S(1)} %fusion.93, pred[128,128]{1,0:T(8,128)(4,1)S(1)} %iota_compare_fusion.3, bf16[2,128,16,64]{1,0,3,2:T(2,128)(2,1)S(1)} %reshape_reshape_squeeze.4), kind=kOutput, calls=%fused_computation.15 | convolution fusion | flops 69730304 | bytes 1753088 | tf_op jit(solution)/shard_map/chqk,ckhp->cqhp/dot_general | solution.py:137
  93.4 9.7 %all-to-all-done.2 = bf16[32,64,128]{2,1,0:T(8,128)(2,1)} async-done(((bf16[32,64,128]{2,1,0:T(8,128)(2,1)}), bf16[32,64,128]{2,1,0:T(8,128)(2,1)}, u32[]{:S(2)}, u32[]{:S(2)}) %all-to-all-start.2) | async-done | bytes 524320 | tf_op jit(solution)/shard_map/all_to_all | solution.py:97
  103.2 1.2 fusion.91
  105.1 0.6 copy-done.5
  106.2 0.7 fusion.13
  107.0 0.8 copy.147
  108.6 0.7 convolution_convert_fusion.1
  110.9 25.6 %all_to_all.25 = bf16[32,8,1152]{2,1,0:T(8,128)(2,1)S(1)} all-to-all(bf16[32,8,1152]{2,1,0:T(8,128)(2,1)S(1)} %fusion.34), channel_id=1, replica_groups=mesh['dp'=16,'seq'=32] {'seq'}, dimensions={0} | all-to-all | bytes 1179648 | tf_op jit(solution)/shard_map/all_to_all | solution.py:245
  137.4 24.1 %all_to_all.26 = bf16[32,8,1024]{2,1,0:T(8,128)(2,1)S(1)} all-to-all(bf16[32,8,1024]{2,1,0:T(8,128)(2,1)S(1)} %broadcast_in_dim.149), channel_id=1, replica_groups=mesh['dp'=16,'seq'=32] {'seq'}, dimensions={0} | all-to-all | bytes 1048576 | tf_op jit(solution)/shard_map/all_to_all | solution.py:256
  161.5 0.8 copy.207
  (106 shorter events, 9.5 us)
Async XLA Ops:
  0.6 108.7 %copy-start = (bf16[256,1024]{1,0:T(8,128)(2,1)S(1)}, bf16[256,1024]{1,0:T(8,128)(2,1)}, u32[]{:S(2)}) copy-start(bf16[256,1024]{1,0:T(8,128)(2,1)} %param.20) | copy-start | bytes 1572868
  3.2 7.4 %copy-start.12 = (f32[2,16]{1,0:T(2,128)S(1)}, f32[2,16]{1,0:T(2,128)}, u32[]{:S(2)}) copy-start(f32[2,16]{1,0:T(2,128)} %param.16) | copy-start | bytes 388
  3.2 7.5 %copy-start.9 = (f32[1,32,256]{2,1,0:T(8,128)S(1)}, f32[1,32,256]{2,1,0:T(8,128)}, u32[]{:S(2)}) copy-start(f32[1,32,256]{2,1,0:T(8,128)} %param.15) | copy-start | bytes 98308
  3.2 10.8 %copy-start.7 = (bf16[1,256,1024]{2,1,0:T(8,128)(2,1)S(1)}, bf16[1,256,1024]{2,1,0:T(8,128)(2,1)}, u32[]{:S(2)}) copy-start(bf16[1,256,1024]{2,1,0:T(8,128)(2,1)} %param.12) | copy-start | bytes 1572868
  3.2 33.1 %all-to-all-start = ((bf16[16,64,1024]{2,1,0:T(8,128)(2,1)}), bf16[16,64,1024]{2,1,0:T(8,128)(2,1)S(1)}, u32[]{:S(2)}, u32[]{:S(2)}) async-start(bf16[16,64,1024]{2,1,0:T(8,128)(2,1)} %broadcast_in_dim.82), calls=%async_computation | async-start | bytes 4194304 | tf_op jit(solution)/shard_map/all_to_all | solution.py:302
  36.3 38.0 %all-to-all-start.1 = ((bf16[32,80,128]{2,1,0:T(8,128)(2,1)}), bf16[32,80,128]{2,1,0:T(8,128)(2,1)}, u32[]{:S(2)}, u32[]{:S(2)}) async-start(bf16[32,80,128]{2,1,0:T(8,128)(2,1)} %fusion.33), calls=%async_computation.1 | async-start | bytes 1310720 | tf_op jit(solution)/shard_map/all_to_all | solution.py:69
  76.7 7.0 %copy-start.14 = (f32[16]{0:T(128)S(1)}, f32[16]{0:T(128)}, u32[]{:S(2)}) copy-start(f32[16]{0:T(128)} %get-tuple-element.18) | copy-start | bytes 196
  78.4 10.0 %copy-start.13 = (f32[16]{0:T(128)S(1)}, f32[16]{0:T(128)}, u32[]{:S(2)}) copy-start(f32[16]{0:T(128)} %param.17) | copy-start | bytes 196
  78.4 24.8 %all-to-all-start.2 = ((bf16[32,64,128]{2,1,0:T(8,128)(2,1)}), bf16[32,64,128]{2,1,0:T(8,128)(2,1)}, u32[]{:S(2)}, u32[]{:S(2)}) async-start(bf16[32,64,128]{2,1,0:T(8,128)(2,1)} %copy.145), calls=%async_computation.2 | async-start | bytes 1048576 | tf_op jit(solution)/shard_map/all_to_all | solution.py:97
  88.9 2.7 %copy-start.10 = (f32[2,16,128]{2,1,0:T(8,128)S(1)}, f32[2,16,128]{2,1,0:T(8,128)}, u32[]{:S(2)}) copy-start(f32[2,16,128]{2,1,0:T(8,128)} %get-tuple-element.61) | copy-start | bytes 49156
  103.2 1.3 copy-start.4
  103.2 1.5 copy-start.6
  104.4 1.3 copy-start.5
  104.4 1.4 copy-start.8
  104.4 1.8 %copy-start.15 = (f32[2,128,16,64]{1,3,2,0:T(8,128)S(1)}, f32[2,128,16,64]{1,3,2,0:T(8,128)}, u32[]{:S(2)}) copy-start(f32[2,128,16,64]{1,3,2,0:T(8,128)} %convolution_bitcast_fusion.3) | copy-start | bytes 3145732
  106.9 1.0 copy-start.1
  106.9 1.2 copy-start.2
  106.9 1.2 copy-start.11
  109.4 1.5 copy-start.3
